TPU v7x, 32 devices: a whole 2x2x4 slice. The times are simulated.
32 devices in a mesh: sea: 8 (over z, y), tm: 4 (over x, core).
Axes of the slice: x: 2, y: 2, z: 4, core: 2. Of those that a mesh axis runs over, the one named last changes fastest.
Arguments:
- motion: bfloat16 [4096, 64, 256], P('sea', 'tm'), may hold values from -6 to 6
- kappa: float32 [4096], P('sea'), may hold values from 0.2 to 5
- react: float32 [4096], P('sea'), may hold values from 0.02 to 0.5
- green: bfloat16 [64, 2, 512, 4096], P('tm', None, None, 'sea'), may hold values from -0.09375 to 0.09375
Outputs:
- prior_part: bfloat16 [4096, 64, 256], P('sea', 'tm')
- sensor_data: float32 [512, 64, 2, 256], P('sea', 'tm')
All inputs are finite; a program needn't handle non-finite values.
Results may differ from a plain program's by a relative error of at most 0.01295.
Values may be sent and summed in bfloat16 or wider, within the bound.
No kernel may reach another device: no remote copies, remote signals or barrier semaphores. Data moves between devices by JAX's collectives and lax.ppermute only.
A program may use at most 192 MiB of HBM per device.

v0:
```python
import math

import jax
import jax.numpy as jnp
from jax import lax
from jax.sharding import PartitionSpec as P

SWEEPS = 6


def passed_along(block, axis, distance):
    devices = range(lax.axis_size(axis))
    route = [(i - distance, i) for i in devices if i - distance in devices]
    return lax.ppermute(block, axis, route)


def with_halo(cells, sides, width):
    for axis, dim in sides:
        count = lax.axis_size(axis)
        ends = count - 1
        head = lax.slice_in_dim(cells, 0, width, axis=dim)
        tail = lax.slice_in_dim(cells, cells.shape[dim] - width, cells.shape[dim], axis=dim)
        cells = jnp.concatenate(
            [
                lax.ppermute(tail, axis, [(i, (i + 1) % count) for i in range(ends)]),
                cells,
                lax.ppermute(head, axis, [((i + 1) % count, i) for i in range(ends)]),
            ],
            axis=dim,
        )
    return cells


def omega_table(count):
    return [
        1.0 / (1.05 + 0.95 * math.cos((2 * k + 1) * math.pi / (2 * count))) for k in range(count)
    ]


def operator_apply(state, padded, left_k, right_k, diag):
    return diag * state - left_k * padded[:-2] - right_k * padded[2:]


def on_device(motion, kappa, react, green):
    points = motion.shape[0]
    groups = lax.axis_size("sea")
    total_points = points * groups
    where_sea = lax.axis_index("sea")
    weights = omega_table(SWEEPS)
    source = motion.astype(jnp.float32)
    own_index = where_sea * points + jnp.arange(points, dtype=jnp.int32)
    own_kappa = jnp.where(own_index == total_points - 1, 0.0, kappa)
    before = passed_along(kappa[points - 1 : points], "sea", 1)
    left_flat = jnp.concatenate([before, kappa[: points - 1]])
    left_k = left_flat[:, None, None]
    right_k = own_kappa[:, None, None]
    diag = left_k + right_k + react[:, None, None]
    state = weights[0] * source / diag
    for k in range(1, SWEEPS):
        padded = with_halo(state, (("sea", 0),), 1)
        applied = operator_apply(state, padded, left_k, right_k, diag)
        state = state + weights[k] * (source - applied) / diag
    prior_part = state.astype(jnp.bfloat16)
    piece = lax.all_to_all(prior_part, "tm", split_axis=0, concat_axis=1, tiled=True)
    steps_all = piece.shape[1]
    freq_ids = jnp.arange(steps_all, dtype=jnp.int32)
    phase_ids = freq_ids[:, None] * freq_ids[None, :] % steps_all
    angles = phase_ids.astype(jnp.float32) * (2.0 * math.pi / steps_all)
    scale = 1.0 / math.sqrt(steps_all)
    table = jnp.stack([jnp.cos(angles) * scale, -jnp.sin(angles) * scale], axis=1)
    table_high = lax.optimization_barrier(table.astype(jnp.bfloat16))
    table_low = (table - table_high.astype(jnp.float32)).astype(jnp.bfloat16)
    spectrum = jnp.einsum("fkt,ptc->fkpc", table_high, piece, preferred_element_type=jnp.float32)
    spectrum = spectrum + jnp.einsum(
        "fkt,ptc->fkpc", table_low, piece, preferred_element_type=jnp.float32
    )
    spectrum = spectrum.astype(jnp.bfloat16)
    spectra = lax.all_to_all(spectrum, "tm", split_axis=0, concat_axis=2, tiled=True)
    prods = jnp.einsum("fksp,fjpc->sfkjc", green, spectra, preferred_element_type=jnp.float32)
    real_part = prods[:, :, 0, 0] - prods[:, :, 1, 1]
    imag_part = prods[:, :, 0, 1] + prods[:, :, 1, 0]
    sensor_data = lax.psum_scatter(
        jnp.stack([real_part, imag_part], axis=2).astype(jnp.bfloat16),
        "sea",
        scatter_dimension=0,
        tiled=True,
    ).astype(jnp.float32)
    return (prior_part, sensor_data)


def solution(mesh):
    in_specs = (P("sea", "tm", None), P("sea"), P("sea"), P("tm", None, None, "sea"))
    out_specs = (P("sea", "tm", None), P("sea", "tm", None, None))
    return jax.shard_map(
        on_device, mesh=mesh, in_specs=in_specs, out_specs=out_specs, check_vma=False
    )
```

profile of v0, /device:TPU:0, one launch (start us, length us, event | category | flops | bytes accessed | tf_op | source)
XLA Modules:
  0.0 534.0 jit_solution(16638603072280033900)
XLA Ops:
  8.4 5.4 %collective-permute-start = (f32[1]{0:T(128)}, f32[1]{0:T(128)}, u32[]{:S(2)}, u32[]{:S(2)}) collective-permute-start(f32[1]{0:T(128)} %slice.88), channel_id=1, source_target_pairs={{0,4},{4,8},{8,12},{12,16},{16,20},{20,24},{24,28},{1,5},{5,9},{9,... | collective-permute-start | bytes 20 | tf_op jit(solution)/shard_map/ppermute | solution.py:14
  16.6 3.1 fusion.5
  19.7 3.7 collective-permute-start.1
  24.9 4.6 collective-permute-done.2
  29.5 5.9 %fusion.8 = f32[512,16,256]{2,1,0:T(8,128)S(1)} fusion(f32[512,16,256]{2,1,0:T(8,128)S(1)} %fusion.5, bf16[512,16,256]{2,1,0:T(8,128)(2,1)S(1)} %copy-done, f32[1,16,256]{2,1,0:T(8,128)S(1)} %collective-permute-done.2, f32[1,16,256]{2,1,0:T(8,128)S(1)} %collective-permute-done.1, f32[512]{0:T(512)S(1)} %get-tuple-element.7, f32[512]{0:T(512)S(1)} %get-tuple-element.8, ...), kind=kLoop, calls=%fused_computation.13 | loop fusion | flops 25165824 | bytes 21010432 | tf_op jit(solution)/shard_map/add | solution.py:62
  35.4 4.8 collective-permute-start.3
  41.7 4.2 collective-permute-done.4
  45.9 5.9 %fusion.11 = f32[512,16,256]{2,1,0:T(8,128)S(1)} fusion(f32[512,16,256]{2,1,0:T(8,128)S(1)} %fusion.8, bf16[512,16,256]{2,1,0:T(8,128)(2,1)S(1)} %copy-done, f32[1,16,256]{2,1,0:T(8,128)S(1)} %collective-permute-done.4, f32[1,16,256]{2,1,0:T(8,128)S(1)} %collective-permute-done.3, f32[512]{0:T(512)S(1)} %get-tuple-element.7, f32[512]{0:T(512)S(1)} %get-tuple-element.8, ...), kind=kLoop, calls=%fused_computation.16 | loop fusion | flops 25165824 | bytes 21010432 | tf_op jit(solution)/shard_map/add | solution.py:62
  51.9 2.9 collective-permute-start.5
  56.2 4.2 collective-permute-done.6
  60.4 5.9 %fusion.14 = f32[512,16,256]{2,1,0:T(8,128)S(1)} fusion(f32[512,16,256]{2,1,0:T(8,128)S(1)} %fusion.11, bf16[512,16,256]{2,1,0:T(8,128)(2,1)S(1)} %copy-done, f32[1,16,256]{2,1,0:T(8,128)S(1)} %collective-permute-done.6, f32[1,16,256]{2,1,0:T(8,128)S(1)} %collective-permute-done.5, f32[512]{0:T(512)S(1)} %get-tuple-element.7, f32[512]{0:T(512)S(1)} %get-tuple-element.8, ...), kind=kLoop, calls=%fused_computation.19 | loop fusion | flops 25165824 | bytes 21010432 | tf_op jit(solution)/shard_map/add | solution.py:62
  66.4 4.8 collective-permute-start.7
  72.7 4.2 collective-permute-done.8
  76.9 11.6 %fusion.17 = f32[512,16,256]{2,1,0:T(8,128)S(1)} fusion(f32[512,16,256]{2,1,0:T(8,128)} %copy-done.1, bf16[512,16,256]{2,1,0:T(8,128)(2,1)S(1)} %copy-done, f32[1,16,256]{2,1,0:T(8,128)S(1)} %collective-permute-done.8, f32[1,16,256]{2,1,0:T(8,128)S(1)} %collective-permute-done.7, f32[512]{0:T(512)S(1)} %get-tuple-element.7, f32[512]{0:T(512)S(1)} %get-tuple-element.8, ...), kind=kLoop, calls=%fused_computation.22 | loop fusion | flops 25165824 | bytes 21010432 | tf_op jit(solution)/shard_map/add | solution.py:62
  88.5 2.9 collective-permute-start.9
  92.8 4.2 collective-permute-done.10
  97.1 6.2 %fusion.45 = bf16[512,16,256]{2,1,0:T(8,128)(2,1)} fusion(f32[512,16,256]{2,1,0:T(8,128)S(1)} %fusion.17, f32[1,16,256]{2,1,0:T(8,128)S(1)} %collective-permute-done.10, f32[1,16,256]{2,1,0:T(8,128)S(1)} %collective-permute-done.9, bf16[512,16,256]{2,1,0:T(8,128)(2,1)S(1)} %copy-done, f32[512]{0:T(512)S(1)} %get-tuple-element.7, ...), kind=kLoop, calls=%fused_computation.64 | loop fusion | flops 27262976 | bytes 16816128 | tf_op jit(solution)/shard_map/convert_element_type | solution.py:63
  103.2 4.9 all-to-all-start
  108.5 47.8 %all-to-all-done = bf16[512,16,256]{2,1,0:T(8,128)(2,1)} async-done(((bf16[512,16,256]{2,1,0:T(8,128)(2,1)}), bf16[512,16,256]{2,1,0:T(8,128)(2,1)}, u32[]{:S(2)}, u32[]{:S(2)}) %all-to-all-start) | async-done | bytes 4194336 | tf_op jit(solution)/shard_map/all_to_all | solution.py:64
  159.1 8.1 %fusion.54 = f32[64,2,128,256]{3,0,2,1:T(8,128)} fusion(bf16[128,64,256,1]{2,1,0,3:T(8,128)(2,1)S(1)} %bitcast.53, bf16[64,2,64]{2,0,1:T(8,128)(2,1)S(1)} %fusion.48), kind=kOutput, calls=%fused_computation.77 | convolution fusion | flops 536870912 | bytes 20987904 | tf_op jit(solution)/shard_map/fkt,ptc->fkpc/dot_general | solution.py:73
  167.1 11.5 %add_convert_fusion = bf16[64,2,128,256]{3,0,2,1:T(8,128)(2,1)} fusion(f32[64,2,128,256]{3,0,2,1:T(8,128)} %fusion.54, bf16[128,64,256,1]{2,1,0,3:T(8,128)(2,1)S(1)} %bitcast.54, bf16[64,2,64]{2,0,1:T(8,128)(2,1)S(1)} %fusion.48, f32[64,1,64]{2,0,1:T(8,128)S(1)} %get-tuple-element.19, f32[64,1,64]{2,0,1:T(8,128)S(1)} %get-tuple-element.20), kind=kOutput, calls=%fused_computation.8 | convolution fusion | flops 545292288 | bytes 29409280 | tf_op jit(solution)/shard_map/fkt,ptc->fkpc/dot_general | solution.py:74
  178.6 11.4 %copy.12 = bf16[64,2,128,256]{3,2,1,0:T(8,128)(2,1)} copy(bf16[64,2,128,256]{3,0,2,1:T(8,128)(2,1)} %add_convert_fusion) | data formatting | bytes 16777216 | tf_op jit(solution)/shard_map/convert_element_type | solution.py:77
  190.0 100.6 %all_to_all.36 = bf16[64,2,128,256]{3,2,1,0:T(8,128)(2,1)} all-to-all(bf16[64,2,128,256]{3,2,1,0:T(8,128)(2,1)} %copy.12), channel_id=1, replica_groups=mesh['sea'=8,'tm'=4] {'tm'}, dimensions={0} | all-to-all | bytes 16777216 | tf_op jit(solution)/shard_map/all_to_all | solution.py:78
  290.6 13.6 %copy.13 = bf16[4,16,2,128,256]{3,0,4,2,1:T(4,128)(2,1)} copy(bf16[4,16,2,128,256]{4,3,2,1,0:T(8,128)(2,1)} %bitcast.55) | data formatting | bytes 16777216 | tf_op jit(solution)/shard_map/all_to_all | solution.py:78
  304.1 13.1 %reshape.125 = bf16[16,2,512,256,1]{2,3,1,0,4:T(8,128)(2,1)} reshape(bf16[16,2,4,128,256]{3,2,4,1,0:T(4,128)(2,1)} %bitcast.56) | data formatting | bytes 16777216 | tf_op jit(solution)/shard_map/all_to_all | solution.py:78
  317.2 22.4 %fusion.2 = f32[512,16,2,2,256]{0,4,2,3,1:T(8,128)} fusion(bf16[16,2,512,512]{3,2,1,0:T(8,128)(2,1)} %param.7, bf16[16,2,512,256,1]{2,3,1,0,4:T(8,128)(2,1)} %reshape.125), kind=kOutput, calls=%fused_computation.9 | convolution fusion | flops 8589934592 | bytes 58720256 | tf_op jit(solution)/shard_map/fksp,fjpc->sfkjc/dot_general | solution.py:79
  339.7 6.6 %fusion.47 = bf16[512,16,1,256]{0,3,1,2:T(8,128)(2,1)S(1)} fusion(f32[512,16,2,2,256]{0,4,2,3,1:T(8,128)} %fusion.2), kind=kLoop, calls=%fused_computation.66 | loop fusion | flops 4194304 | bytes 20971520 | tf_op jit(solution)/shard_map/add | solution.py:81
  346.3 8.8 %fusion.46 = bf16[512,16,1,256]{0,3,1,2:T(8,128)(2,1)} fusion(f32[512,16,2,2,256]{0,4,2,3,1:T(8,128)} %fusion.2), kind=kLoop, calls=%fused_computation.65 | loop fusion | flops 4194304 | bytes 20971520 | tf_op jit(solution)/shard_map/sub | solution.py:80
  355.1 6.2 %pad_maximum_fusion.10 = bf16[512,16,2,256]{0,3,1,2:T(8,128)(2,1)} fusion(bf16[512,16,1,256]{0,3,1,2:T(8,128)(2,1)S(1)} %fusion.47, bf16[512,16,1,256]{0,3,1,2:T(8,128)(2,1)} %fusion.46), kind=kLoop, calls=%fused_computation.62 | loop fusion | flops 4194304 | bytes 16777216 | tf_op jit(solution)/shard_map/stack | solution.py:83
  361.3 14.6 %copy.16 = bf16[512,16,2,256]{3,1,2,0:T(8,128)(2,1)} copy(bf16[512,16,2,256]{0,3,1,2:T(8,128)(2,1)} %pad_maximum_fusion.10) | data formatting | bytes 16777216 | tf_op jit(solution)/shard_map/stack | solution.py:83
  375.9 147.9 %reduce-scatter.2.cloned.1.call-done = bf16[64,16,2,256]{3,1,2,0:T(8,128)(2,1)} async-done(((bf16[512,16,2,256]{3,1,2,0:T(8,128)(2,1)}), bf16[64,16,2,256]{3,1,2,0:T(8,128)(2,1)}) %reduce-scatter.2.cloned.1.call-update) | async-done | bytes 1048592 | tf_op jit(solution)/shard_map/reduce_scatter | solution.py:82
  523.8 3.4 copy.17
  (27 shorter events, 14.2 us)
Async XLA Ops:
  8.4 6.3 %collective-permute-start = (f32[1]{0:T(128)}, f32[1]{0:T(128)}, u32[]{:S(2)}, u32[]{:S(2)}) collective-permute-start(f32[1]{0:T(128)} %slice.88), channel_id=1, source_target_pairs={{0,4},{4,8},{8,12},{12,16},{16,20},{20,24},{24,28},{1,5},{5,9},{9,... | collective-permute-start | bytes 20 | tf_op jit(solution)/shard_map/ppermute | solution.py:14
  13.8 15.6 %copy-start = (bf16[512,16,256]{2,1,0:T(8,128)(2,1)S(1)}, bf16[512,16,256]{2,1,0:T(8,128)(2,1)}, u32[]{:S(2)}) copy-start(bf16[512,16,256]{2,1,0:T(8,128)(2,1)} %param.4) | copy-start | bytes 12582916
  19.7 5.2 collective-permute-start.1
  23.4 6.0 %collective-permute-start.2 = (f32[1,16,256]{2,1,0:T(8,128)S(1)}, f32[1,16,256]{2,1,0:T(8,128)S(1)}, u32[]{:S(2)}, u32[]{:S(2)}) collective-permute-start(f32[1,16,256]{2,1,0:T(8,128)S(1)} %get-tuple-element.18), channel_id=1, source_target_pairs={{4,0},{8,4},{12,8},{16,12},{20,16},{24,20},{28,24},{5,1},{9,5},{13... | collective-permute-start | bytes 49160 | tf_op jit(solution)/shard_map/ppermute | solution.py:27
  35.4 6.3 %collective-permute-start.3 = (f32[1,16,256]{2,1,0:T(8,128)S(1)}, f32[1,16,256]{2,1,0:T(8,128)S(1)}, u32[]{:S(2)}, u32[]{:S(2)}) collective-permute-start(f32[1,16,256]{2,1,0:T(8,128)S(1)} %get-tuple-element.15), channel_id=1, source_target_pairs={{0,4},{4,8},{8,12},{12,16},{16,20},{20,24},{24,28},{1,5},{5,9},{9,... | collective-permute-start | bytes 49160 | tf_op jit(solution)/shard_map/ppermute | solution.py:25
  40.3 5.6 %collective-permute-start.4 = (f32[1,16,256]{2,1,0:T(8,128)S(1)}, f32[1,16,256]{2,1,0:T(8,128)S(1)}, u32[]{:S(2)}, u32[]{:S(2)}) collective-permute-start(f32[1,16,256]{2,1,0:T(8,128)S(1)} %get-tuple-element.16), channel_id=1, source_target_pairs={{4,0},{8,4},{12,8},{16,12},{20,16},{24,20},{28,24},{5,1},{9,5},{13... | collective-permute-start | bytes 49160 | tf_op jit(solution)/shard_map/ppermute | solution.py:27
  51.9 4.4 collective-permute-start.5
  54.8 5.6 %collective-permute-start.6 = (f32[1,16,256]{2,1,0:T(8,128)S(1)}, f32[1,16,256]{2,1,0:T(8,128)S(1)}, u32[]{:S(2)}, u32[]{:S(2)}) collective-permute-start(f32[1,16,256]{2,1,0:T(8,128)S(1)} %get-tuple-element.14), channel_id=1, source_target_pairs={{4,0},{8,4},{12,8},{16,12},{20,16},{24,20},{28,24},{5,1},{9,5},{13... | collective-permute-start | bytes 49160 | tf_op jit(solution)/shard_map/ppermute | solution.py:27
  66.4 6.3 %copy-start.1 = (f32[512,16,256]{2,1,0:T(8,128)}, f32[512,16,256]{2,1,0:T(8,128)S(1)}, u32[]{:S(2)}) copy-start(f32[512,16,256]{2,1,0:T(8,128)S(1)} %fusion.14) | copy-start | bytes 25165828
  66.4 6.3 %collective-permute-start.7 = (f32[1,16,256]{2,1,0:T(8,128)S(1)}, f32[1,16,256]{2,1,0:T(8,128)S(1)}, u32[]{:S(2)}, u32[]{:S(2)}) collective-permute-start(f32[1,16,256]{2,1,0:T(8,128)S(1)} %get-tuple-element.11), channel_id=1, source_target_pairs={{0,4},{4,8},{8,12},{12,16},{16,20},{20,24},{24,28},{1,5},{5,9},{9,... | collective-permute-start | bytes 49160 | tf_op jit(solution)/shard_map/ppermute | solution.py:25
  71.2 5.6 %collective-permute-start.8 = (f32[1,16,256]{2,1,0:T(8,128)S(1)}, f32[1,16,256]{2,1,0:T(8,128)S(1)}, u32[]{:S(2)}, u32[]{:S(2)}) collective-permute-start(f32[1,16,256]{2,1,0:T(8,128)S(1)} %get-tuple-element.12), channel_id=1, source_target_pairs={{4,0},{8,4},{12,8},{16,12},{20,16},{24,20},{28,24},{5,1},{9,5},{13... | collective-permute-start | bytes 49160 | tf_op jit(solution)/shard_map/ppermute | solution.py:27
  88.5 4.4 collective-permute-start.9
  91.4 5.6 %collective-permute-start.10 = (f32[1,16,256]{2,1,0:T(8,128)S(1)}, f32[1,16,256]{2,1,0:T(8,128)S(1)}, u32[]{:S(2)}, u32[]{:S(2)}) collective-permute-start(f32[1,16,256]{2,1,0:T(8,128)S(1)} %get-tuple-element.10), channel_id=1, source_target_pairs={{4,0},{8,4},{12,8},{16,12},{20,16},{24,20},{28,24},{5,1},{9,5},{13... | collective-permute-start | bytes 49160 | tf_op jit(solution)/shard_map/ppermute | solution.py:27
  103.2 53.1 %all-to-all-start = ((bf16[512,16,256]{2,1,0:T(8,128)(2,1)}), bf16[512,16,256]{2,1,0:T(8,128)(2,1)}, u32[]{:S(2)}, u32[]{:S(2)}) async-start(bf16[512,16,256]{2,1,0:T(8,128)(2,1)} %fusion.45), calls=%async_computation | async-start | bytes 8388608 | tf_op jit(solution)/shard_map/all_to_all | solution.py:64
  108.1 415.7 %reduce-scatter.2.cloned.1.call-start = ((), (), s32[]{:S(2)}) async-start(), calls=%async_computation.3 | async-start | bytes 9437184 | tf_op jit(solution)/shard_map/reduce_scatter | solution.py:82
Sparse Core Ops, SparseCore 0:
  376.0 147.6 reduce-scatter.1
where the time goes:
time: 536 us; the launch traced here: 534 us
  waiting for transfers between devices  219 us (41%)
  blocking collectives  101 us (19%)
  other arithmetic  62.4 us (12%)
  local copies, waits for them, and re-layouts  60 us (11%)
  matrix products  41.9 us (8%)
  starting transfers between devices  36.2 us (7%)
  between operations  14.2 us (3%)
    reduce_scatter x1, waiting for transfers between devices, on_device(): lax.psum_scatter(jnp.stack([real_part, imag_part], axis=2).astype(jnp.bfl...  148 us
    all_to_all x1, blocking collectives, on_device(): lax.all_to_all(spectrum, 'tm', split_axis=0, concat_axis=2, tiled=True)  101 us
    all_to_all x1, waiting for transfers between devices, on_device(): lax.all_to_all(prior_part, 'tm', split_axis=0, concat_axis=1, tiled=True)  47.8 us
    add x4, other arithmetic, on_device(): state = state + weights[k] * (source - applied) / diag  29.4 us
    all_to_all x2, local copies, waits for them, and re-layouts, on_device(): lax.all_to_all(spectrum, 'tm', split_axis=0, concat_axis=2, tiled=True)  26.7 us
    dot_general x1, matrix products, on_device(): jnp.einsum('fksp,fjpc->sfkjc', green, spectra, preferred_element_type=jnp...  22.4 us
    ppermute x5, waiting for transfers between devices, with_halo(): lax.ppermute(head, axis, [((i + 1) % count, i) for i in range(ends)])  21.4 us
    ppermute x5, starting transfers between devices, with_halo(): lax.ppermute(tail, axis, [(i, (i + 1) % count) for i in range(ends)])  19.2 us
  transfers between devices with their start and end apart: 13, of which 13 were waited for; matrix products, arithmetic and copies ran while one was open for 0% of the time, Pallas kernels for 0%

commit v1 on v0

v1 whole, which is shorter than its diff:
```python
import math

import jax
import jax.numpy as jnp
from jax import lax
from jax.sharding import PartitionSpec as P

SWEEPS = 6
CHUNKS = 2


def from_left(block, axis):
    count = lax.axis_size(axis)
    return lax.ppermute(block, axis, [(i, i + 1) for i in range(count - 1)])


def from_right(block, axis):
    count = lax.axis_size(axis)
    return lax.ppermute(block, axis, [(i + 1, i) for i in range(count - 1)])


def omega_table(count):
    return [
        1.0 / (1.05 + 0.95 * math.cos((2 * k + 1) * math.pi / (2 * count))) for k in range(count)
    ]


def extended_coefficients(kappa, react, halo):
    points = kappa.shape[0]
    groups = lax.axis_size("sea")
    total_points = points * groups
    where_sea = lax.axis_index("sea")
    kappa_ext = jnp.concatenate(
        [from_left(kappa[points - halo - 1 :], "sea"), kappa, from_right(kappa[:halo], "sea")]
    )
    react_ext = jnp.concatenate(
        [from_left(react[points - halo :], "sea"), react, from_right(react[:halo], "sea")]
    )
    index = where_sea * points - halo + jnp.arange(points + 2 * halo, dtype=jnp.int32)
    valid = (index >= 0) & (index < total_points)
    left_k = jnp.where(valid & (index >= 1), kappa_ext[:-1], 0.0)
    right_k = jnp.where(valid & (index < total_points - 1), kappa_ext[1:], 0.0)
    react_v = jnp.where(valid, react_ext, 1.0)
    diag = left_k + right_k + react_v
    return left_k[:, None, None], right_k[:, None, None], diag[:, None, None]


def smooth(source, left_k, right_k, diag, halo):
    weights = omega_table(SWEEPS)
    state = weights[0] * source / diag
    for k in range(1, SWEEPS):
        padded = jnp.pad(state, ((1, 1), (0, 0), (0, 0)))
        applied = diag * state - left_k * padded[:-2] - right_k * padded[2:]
        state = state + weights[k] * (source - applied) / diag
    return state[halo : state.shape[0] - halo]


def dft_tables(steps_all):
    freq_ids = jnp.arange(steps_all, dtype=jnp.int32)
    phase_ids = freq_ids[:, None] * freq_ids[None, :] % steps_all
    angles = phase_ids.astype(jnp.float32) * (2.0 * math.pi / steps_all)
    scale = 1.0 / math.sqrt(steps_all)
    table = jnp.stack([jnp.cos(angles) * scale, -jnp.sin(angles) * scale], axis=1)
    table_high = lax.optimization_barrier(table.astype(jnp.bfloat16))
    table_low = (table - table_high.astype(jnp.float32)).astype(jnp.bfloat16)
    return table_high, table_low


def forward_chunk(prior_part, green, table_high, table_low):
    piece = lax.all_to_all(prior_part, "tm", split_axis=0, concat_axis=1, tiled=True)
    spectrum = jnp.einsum("fkt,ptc->fkpc", table_high, piece, preferred_element_type=jnp.float32)
    spectrum = spectrum + jnp.einsum(
        "fkt,ptc->fkpc", table_low, piece, preferred_element_type=jnp.float32
    )
    spectrum = spectrum.astype(jnp.bfloat16)
    spectra = lax.all_to_all(spectrum, "tm", split_axis=0, concat_axis=2, tiled=True)
    real_s = spectra[:, 0]
    imag_s = spectra[:, 1]
    mixed = jnp.stack(
        [jnp.stack([real_s, imag_s], axis=2), jnp.stack([-imag_s, real_s], axis=2)], axis=1
    )
    partial = jnp.einsum("fksp,fkprc->sfrc", green, mixed, preferred_element_type=jnp.float32)
    return lax.psum_scatter(
        partial.astype(jnp.bfloat16), "sea", scatter_dimension=0, tiled=True
    ).astype(jnp.float32)


def on_device(motion, kappa, react, green):
    halo = SWEEPS - 1
    cols = motion.shape[2]
    width = cols // CHUNKS
    left_k, right_k, diag = extended_coefficients(kappa, react, halo)
    motion_ext = jnp.concatenate(
        [from_left(motion[motion.shape[0] - halo :], "sea"), motion, from_right(motion[:halo], "sea")]
    )
    table_high, table_low = dft_tables(motion.shape[1] * lax.axis_size("tm"))
    priors = []
    sensors = []
    for c in range(CHUNKS):
        source = motion_ext[:, :, c * width : (c + 1) * width].astype(jnp.float32)
        prior_part = smooth(source, left_k, right_k, diag, halo).astype(jnp.bfloat16)
        priors.append(prior_part)
        sensors.append(forward_chunk(prior_part, green, table_high, table_low))
    return (jnp.concatenate(priors, axis=2), jnp.concatenate(sensors, axis=3))


def solution(mesh):
    in_specs = (P("sea", "tm", None), P("sea"), P("sea"), P("tm", None, None, "sea"))
    out_specs = (P("sea", "tm", None), P("sea", "tm", None, None))
    return jax.shard_map(
        on_device, mesh=mesh, in_specs=in_specs, out_specs=out_specs, check_vma=False
    )
```

time: 536 us -> 413 us (0.77)
  waiting for transfers between devices: 219 us -> 109 us
  matrix products: 41.9 us -> 30.2 us
  starting transfers between devices: 36.2 us -> 27.3 us
  local copies, waits for them, and re-layouts: 60 us -> 65.9 us
    reduce_scatter x1 -> x2, waiting for transfers between devices: 148 us -> 83.3 us  [forward_chunk(): lax.psum_scatter(partial.astype(jnp.bfloat16), 'sea', scatter_dimension=0...]
    all_to_all x1 -> x2, waiting for transfers between devices: 47.8 us -> 25.3 us  [forward_chunk(): lax.all_to_all(prior_part, 'tm', split_axis=0, concat_axis=1, tiled=True)]
    ppermute x11 -> x6, waiting for transfers between devices: 22.9 us -> 0.52 us  [the longest x3 0.52 us: from_right(): return lax.ppermute(block, axis, [(i + 1, i) for i in range(count - 1)])]
    add x6 -> x7, other arithmetic: 37.9 us -> 25.6 us  [smooth(): state = state + weights[k] * (source - applied) / diag]
    dot_general x3 -> x6, matrix products: 41.9 us -> 30.2 us  [the longest x2 25.3 us: forward_chunk(): jnp.einsum('fksp,fkprc->sfrc', green, mixed, preferred_element_type=jnp.f...]
    another operation x1 -> x2, local copies, waits for them, and re-layouts: 14.6 us -> 3.08 us  [forward_chunk(): jnp.stack([real_s, imag_s], axis=2)]
    ppermute x11 -> x6, starting transfers between devices: 31.1 us -> 19.6 us  [the longest x3 15.7 us: from_left(): return lax.ppermute(block, axis, [(i, i + 1) for i in range(count - 1)])]
    convert_element_type x1 -> x4, local copies, waits for them, and re-layouts: 11.4 us -> 21.5 us  [the longest x2 16.1 us: forward_chunk(): partial.astype(jnp.bfloat16)]
  transfers between devices with their start and end apart: 13 -> 10, of which waited for: 13 -> 3; matrix products, arithmetic and copies ran while one was open for 0% -> 21% of each run, Pallas kernels for 0% -> 0%
where the time goes in v1:
time: 413 us; the launch traced here: 411 us
  waiting for transfers between devices  109 us (26%)
  blocking collectives  103 us (25%)
  local copies, waits for them, and re-layouts  65.9 us (16%)
  other arithmetic  61.3 us (15%)
  matrix products  30.2 us (7%)
  starting transfers between devices  27.3 us (7%)
  between operations  14.3 us (3%)
    all_to_all x2, blocking collectives, forward_chunk(): lax.all_to_all(spectrum, 'tm', split_axis=0, concat_axis=2, tiled=True)  103 us
    reduce_scatter x2, waiting for transfers between devices, forward_chunk(): lax.psum_scatter(partial.astype(jnp.bfloat16), 'sea', scatter_dimension=0...  83.3 us
    all_to_all x4, local copies, waits for them, and re-layouts, forward_chunk(): lax.all_to_all(spectrum, 'tm', split_axis=0, concat_axis=2, tiled=True)  29.5 us
    add x7, other arithmetic, smooth(): state = state + weights[k] * (source - applied) / diag  25.6 us
    all_to_all x2, waiting for transfers between devices, forward_chunk(): lax.all_to_all(prior_part, 'tm', split_axis=0, concat_axis=1, tiled=True)  25.3 us
    dot_general x2, matrix products, forward_chunk(): jnp.einsum('fksp,fkprc->sfrc', green, mixed, preferred_element_type=jnp.f...  25.3 us
    convert_element_type x2, local copies, waits for them, and re-layouts, forward_chunk(): partial.astype(jnp.bfloat16)  16.1 us
    ppermute x3, starting transfers between devices, from_left(): return lax.ppermute(block, axis, [(i, i + 1) for i in range(count - 1)])  15.7 us
  transfers between devices with their start and end apart: 10, of which 3 were waited for; matrix products, arithmetic and copies ran while one was open for 21% of the time, Pallas kernels for 0%

profile of v1, /device:TPU:0, one launch (start us, length us, event | category | flops | bytes accessed | tf_op | source)
XLA Modules:
  0.0 411.4 jit_solution(4524062667093932309)
XLA Ops:
  9.9 5.5 %collective-permute-start.2 = (f32[6]{0:T(128)S(1)}, f32[6]{0:T(128)S(1)}, u32[]{:S(2)}, u32[]{:S(2)}) collective-permute-start(f32[6]{0:T(128)S(1)} %slice.113), channel_id=1, source_target_pairs={{0,4},{4,8},{8,12},{12,16},{16,20},{20,24},{24,28},{1,5},{5,9},{9,... | collective-permute-start | bytes 80 | tf_op jit(solution)/shard_map/ppermute | solution.py:14
  17.5 5.4 %collective-permute-start.4 = (f32[5]{0:T(128)S(1)}, f32[5]{0:T(128)S(1)}, u32[]{:S(2)}, u32[]{:S(2)}) collective-permute-start(f32[5]{0:T(128)S(1)} %get-tuple-element.33), channel_id=1, source_target_pairs={{0,4},{4,8},{8,12},{12,16},{16,20},{20,24},{24,28},{1,5},{5,9},{9,... | collective-permute-start | bytes 68 | tf_op jit(solution)/shard_map/ppermute | solution.py:14
  23.8 4.8 %collective-permute-start = (bf16[5,16,256]{2,1,0:T(8,128)(2,1)S(1)}, bf16[5,16,256]{2,1,0:T(8,128)(2,1)S(1)}, u32[]{:S(2)}, u32[]{:S(2)}) collective-permute-start(bf16[5,16,256]{2,1,0:T(8,128)(2,1)S(1)} %get-tuple-element.21), channel_id=1, source_target_pairs={{0,4},{4,8},{8,12},{12,16},{16,20},{20,24},{24,28},{1,5},{5,9},{9,... | collective-permute-start | bytes 122888 | tf_op jit(solution)/shard_map/ppermute | solution.py:14
  36.1 4.0 slice_convert_fusion.1
  40.0 3.5 fusion.13
  43.6 3.5 fusion.16
  47.1 3.6 fusion.19
  50.7 4.6 %fusion.22 = (f32[522,16,128]{2,1,0:T(8,128)S(1)}, f32[522,16,128]{2,1,0:T(8,128)S(1)}) fusion(f32[522,16,128]{2,1,0:T(8,128)S(1)} %get-tuple-element.8, f32[522]{0:T(1024)S(1)} %get-tuple-element.30, f32[522]{0:T(1024)S(1)} %get-tuple-element.28, f32[522]{0:T(1024)S(1)} %get-tuple-element.29, ...), kind=kLoop, calls=%fused_computation.36 | loop fusion | flops 21381120 | bytes 21387384 | tf_op jit(solution)/shard_map/add | solution.py:54
  55.3 3.5 fusion.29
  58.8 3.5 fusion.32
  62.3 3.5 fusion.35
  65.7 4.6 %multiply_subtract_fusion = (f32[522,16,128]{2,1,0:T(8,128)S(1)}, f32[522,16,128]{2,1,0:T(8,128)S(1)}, f32[522,16,128]{2,1,0:T(8,128)S(1)}, f32[522,16,128]{2,1,0:T(8,128)}) fusion(f32[522,16,128]{2,1,0:T(8,128)S(1)} %fusion.35, f32[522]{0:T(1024)S(1)} %get-tuple-element.28, f32[522]{0:T(1024)S(1)} %get-tuple-element.29, f32[522]{0:T(1024)S(1)} %get-tuple-element.30, ...), kind=kLoop, calls=%fused_computation.51 | loop fusion | flops 8552448 | bytes 25663608 | tf_op jit(solution)/shard_map/sub | solution.py:53
  70.3 8.5 %fusion.41 = (bf16[512,16,128]{2,1,0:T(8,128)(2,1)}, bf16[512,16,128]{2,1,0:T(8,128)(2,1)}) fusion(f32[522,16,128]{2,1,0:T(8,128)S(1)} %get-tuple-element.6, f32[522,16,128]{2,1,0:T(8,128)} %get-tuple-element.12, f32[522,16,128]{2,1,0:T(8,128)S(1)} %get-tuple-element.26, f32[522,16,128]{2,1,0:T(8,128)} %get-tuple-element.27, f32[512]{0:T(512)S(1)} %slice.150, ...), kind=kLoop, calls=%fused_computation.63 | loop fusion | flops 12582912 | bytes 37750784 | tf_op jit(solution)/shard_map/convert.2
  78.8 3.8 all-to-all-start.2
  82.8 25.3 %all-to-all-done.2 = bf16[512,16,128]{2,1,0:T(8,128)(2,1)S(1)} async-done(((bf16[512,16,128]{2,1,0:T(8,128)(2,1)}), bf16[512,16,128]{2,1,0:T(8,128)(2,1)S(1)}, u32[]{:S(2)}, u32[]{:S(2)}) %all-to-all-start.2) | async-done | bytes 2097184 | tf_op jit(solution)/shard_map/all_to_all | solution.py:70
  111.2 2.7 copy.19
  114.0 51.6 %all_to_all.72 = bf16[64,2,128,128]{3,2,1,0:T(8,128)(2,1)} all-to-all(bf16[64,2,128,128]{3,2,1,0:T(8,128)(2,1)S(1)} %copy.19), channel_id=1, replica_groups=mesh['sea'=8,'tm'=4] {'tm'}, dimensions={0} | all-to-all | bytes 8388608 | tf_op jit(solution)/shard_map/all_to_all | solution.py:76
  165.6 3.6 all-to-all-start
  169.2 7.5 %copy.20 = bf16[4,16,2,128,128]{3,0,4,1,2:T(4,128)(2,1)} copy(bf16[4,16,2,128,128]{4,3,2,1,0:T(8,128)(2,1)} %bitcast.90) | data formatting | bytes 8388608 | tf_op jit(solution)/shard_map/all_to_all | solution.py:76
  176.7 7.2 %all_to_all.67 = bf16[16,2,512,128]{2,3,0,1:T(8,128)(2,1)} reshape(bf16[16,2,4,128,128]{3,2,4,0,1:T(4,128)(2,1)} %bitcast.91) | data formatting | bytes 8388608 | tf_op jit(solution)/shard_map/all_to_all | solution.py:76
  187.5 3.7 maximum_bitcast_fusion.2
  191.1 12.5 %fusion.37 = bf16[512,16,2,128]{0,3,2,1:T(8,128)(2,1)} fusion(bf16[16,2,512,512]{3,2,1,0:T(8,128)(2,1)} %param.7, bf16[16,1,512,2,128]{2,4,1,3,0:T(8,128)(2,1)} %get-tuple-element.25, bf16[16,1,512,2,128]{2,4,1,3,0:T(8,128)(2,1)} %get-tuple-element.24), kind=kOutput, calls=%fused_computation.55 | convolution fusion | flops 4301258752 | bytes 29360128 | tf_op jit(solution)/shard_map/fksp,fkprc->sfrc/dot_general | solution.py:82
  203.6 8.0 %copy.22 = bf16[512,16,2,128]{3,1,2,0:T(8,128)(2,1)} copy(bf16[512,16,2,128]{0,3,2,1:T(8,128)(2,1)} %fusion.37) | data formatting | bytes 8388608 | tf_op jit(solution)/shard_map/convert_element_type | solution.py:84
  217.7 51.6 %all_to_all.73 = bf16[64,2,128,128]{3,2,1,0:T(8,128)(2,1)} all-to-all(bf16[64,2,128,128]{3,2,1,0:T(8,128)(2,1)S(1)} %copy.14), channel_id=1, replica_groups=mesh['sea'=8,'tm'=4] {'tm'}, dimensions={0} | all-to-all | bytes 8388608 | tf_op jit(solution)/shard_map/all_to_all | solution.py:76
  269.3 7.5 %copy.15 = bf16[4,16,2,128,128]{3,0,4,1,2:T(4,128)(2,1)} copy(bf16[4,16,2,128,128]{4,3,2,1,0:T(8,128)(2,1)} %bitcast.92) | data formatting | bytes 8388608 | tf_op jit(solution)/shard_map/all_to_all | solution.py:76
  276.8 7.4 %all_to_all.59 = bf16[16,2,512,128]{2,3,0,1:T(8,128)(2,1)} reshape(bf16[16,2,4,128,128]{3,2,4,0,1:T(4,128)(2,1)} %bitcast.93) | data formatting | bytes 8388608 | tf_op jit(solution)/shard_map/all_to_all | solution.py:76
  287.4 3.7 maximum_bitcast_fusion
  291.0 12.8 %fusion.36 = bf16[512,16,2,128]{0,3,2,1:T(8,128)(2,1)} fusion(bf16[16,2,512,512]{3,2,1,0:T(8,128)(2,1)} %param.7, bf16[16,1,512,2,128]{2,4,1,3,0:T(8,128)(2,1)} %get-tuple-element.23, bf16[16,1,512,2,128]{2,4,1,3,0:T(8,128)(2,1)} %get-tuple-element.22), kind=kOutput, calls=%fused_computation.54 | convolution fusion | flops 4301258752 | bytes 29360128 | tf_op jit(solution)/shard_map/fksp,fkprc->sfrc/dot_general | solution.py:82
  303.9 8.1 %copy.17 = bf16[512,16,2,128]{3,1,2,0:T(8,128)(2,1)} copy(bf16[512,16,2,128]{0,3,2,1:T(8,128)(2,1)} %fusion.36) | data formatting | bytes 8388608 | tf_op jit(solution)/shard_map/convert_element_type | solution.py:84
  311.9 4.7 %pad_maximum_fusion = bf16[512,16,256]{2,1,0:T(8,128)(2,1)} fusion(bf16[512,16,128]{2,1,0:T(8,128)(2,1)} %get-tuple-element.32, bf16[512,16,128]{2,1,0:T(8,128)(2,1)} %get-tuple-element.31), kind=kLoop, calls=%fused_computation.68 | loop fusion | flops 8388608 | bytes 8388608 | tf_op jit(solution)/shard_map/concatenate | solution.py:104
  316.6 83.3 %reduce-scatter.3.cloned.1.call-done = bf16[64,16,2,128]{3,1,2,0:T(8,128)(2,1)} async-done(((bf16[512,16,2,128]{3,1,2,0:T(8,128)(2,1)}), bf16[64,16,2,128]{3,1,2,0:T(8,128)(2,1)}) %reduce-scatter.3.cloned.1.call-update) | async-done | bytes 524304 | tf_op jit(solution)/shard_map/reduce_scatter | solution.py:83
  401.3 3.2 copy.23
  (44 shorter events, 30.7 us)
Async XLA Ops:
  7.8 20.8 %collective-permute-start.3 = (f32[5]{0:T(128)S(1)}, f32[5]{0:T(128)S(1)}, u32[]{:S(2)}, u32[]{:S(2)}) collective-permute-start(f32[5]{0:T(128)S(1)} %slice.114), channel_id=1, source_target_pairs={{4,0},{8,4},{12,8},{16,12},{20,16},{24,20},{28,24},{5,1},{9,5},{13... | collective-permute-start | bytes 68 | tf_op jit(solution)/shard_map/ppermute | solution.py:19
  9.9 20.0 %collective-permute-start.2 = (f32[6]{0:T(128)S(1)}, f32[6]{0:T(128)S(1)}, u32[]{:S(2)}, u32[]{:S(2)}) collective-permute-start(f32[6]{0:T(128)S(1)} %slice.113), channel_id=1, source_target_pairs={{0,4},{4,8},{8,12},{12,16},{16,20},{20,24},{24,28},{1,5},{5,9},{9,... | collective-permute-start | bytes 80 | tf_op jit(solution)/shard_map/ppermute | solution.py:14
  16.2 14.5 %collective-permute-start.5 = (f32[5]{0:T(128)S(1)}, f32[5]{0:T(128)S(1)}, u32[]{:S(2)}, u32[]{:S(2)}) collective-permute-start(f32[5]{0:T(128)S(1)} %get-tuple-element.34), channel_id=1, source_target_pairs={{4,0},{8,4},{12,8},{16,12},{20,16},{24,20},{28,24},{5,1},{9,5},{13... | collective-permute-start | bytes 68 | tf_op jit(solution)/shard_map/ppermute | solution.py:19
  17.5 13.2 %collective-permute-start.4 = (f32[5]{0:T(128)S(1)}, f32[5]{0:T(128)S(1)}, u32[]{:S(2)}, u32[]{:S(2)}) collective-permute-start(f32[5]{0:T(128)S(1)} %get-tuple-element.33), channel_id=1, source_target_pairs={{0,4},{4,8},{8,12},{12,16},{16,20},{20,24},{24,28},{1,5},{5,9},{9,... | collective-permute-start | bytes 68 | tf_op jit(solution)/shard_map/ppermute | solution.py:14
  23.8 7.8 %collective-permute-start = (bf16[5,16,256]{2,1,0:T(8,128)(2,1)S(1)}, bf16[5,16,256]{2,1,0:T(8,128)(2,1)S(1)}, u32[]{:S(2)}, u32[]{:S(2)}) collective-permute-start(bf16[5,16,256]{2,1,0:T(8,128)(2,1)S(1)} %get-tuple-element.21), channel_id=1, source_target_pairs={{0,4},{4,8},{8,12},{12,16},{16,20},{20,24},{24,28},{1,5},{5,9},{9,... | collective-permute-start | bytes 122888 | tf_op jit(solution)/shard_map/ppermute | solution.py:14
  28.6 5.9 %collective-permute-start.1 = (bf16[5,16,256]{2,1,0:T(8,128)(2,1)S(1)}, bf16[5,16,256]{2,1,0:T(8,128)(2,1)S(1)}, u32[]{:S(2)}, u32[]{:S(2)}) collective-permute-start(bf16[5,16,256]{2,1,0:T(8,128)(2,1)S(1)} %get-tuple-element.20), channel_id=1, source_target_pairs={{4,0},{8,4},{12,8},{16,12},{20,16},{24,20},{28,24},{5,1},{9,5},{13... | collective-permute-start | bytes 122888 | tf_op jit(solution)/shard_map/ppermute | solution.py:19
  78.8 29.3 %all-to-all-start.2 = ((bf16[512,16,128]{2,1,0:T(8,128)(2,1)}), bf16[512,16,128]{2,1,0:T(8,128)(2,1)S(1)}, u32[]{:S(2)}, u32[]{:S(2)}) async-start(bf16[512,16,128]{2,1,0:T(8,128)(2,1)} %get-tuple-element.32), calls=%async_computation.3 | async-start | bytes 4194304 | tf_op jit(solution)/shard_map/all_to_all | solution.py:70
  165.6 46.3 %all-to-all-start = ((bf16[512,16,128]{2,1,0:T(8,128)(2,1)}), bf16[512,16,128]{2,1,0:T(8,128)(2,1)S(1)}, u32[]{:S(2)}, u32[]{:S(2)}) async-start(bf16[512,16,128]{2,1,0:T(8,128)(2,1)} %get-tuple-element.31), calls=%async_computation | async-start | bytes 4194304 | tf_op jit(solution)/shard_map/all_to_all | solution.py:70
  169.2 147.5 %reduce-scatter.5.cloned.1.call-start = ((), (), s32[]{:S(2)}) async-start(), calls=%async_computation.7 | async-start | bytes 4718592 | tf_op jit(solution)/shard_map/reduce_scatter | solution.py:83
  183.9 3.4 copy-start
  211.6 188.3 %reduce-scatter.3.cloned.1.call-start = ((), (), s32[]{:S(2)}) async-start(), calls=%async_computation.6 | async-start | bytes 4718592 | tf_op jit(solution)/shard_map/reduce_scatter | solution.py:83
  284.1 2.8 copy-start.1
Sparse Core Ops, SparseCore 0:
  211.7 89.3 reduce-scatter.4
  312.1 87.8 reduce-scatter.2

commit v2 on v1

--- a/solution.py
+++ b/solution.py
@@ -25,17 +25,30 @@
     ]
 
 
-def extended_coefficients(kappa, react, halo):
-    points = kappa.shape[0]
+def exchange_halo(motion, kappa, react, halo):
+    points = motion.shape[0]
+    shape = (halo,) + motion.shape[1:]
+    size = math.prod(shape)
+    tail = jnp.concatenate(
+        [motion[points - halo :].astype(jnp.float32).reshape(-1), kappa[points - halo - 1 :], react[points - halo :]]
+    )
+    head = jnp.concatenate(
+        [motion[:halo].astype(jnp.float32).reshape(-1), kappa[:halo], react[:halo]]
+    )
+    before = from_left(tail, "sea")
+    after = from_right(head, "sea")
+    motion_ext = jnp.concatenate(
+        [before[:size].reshape(shape), motion.astype(jnp.float32), after[:size].reshape(shape)]
+    )
+    kappa_ext = jnp.concatenate([before[size : size + halo + 1], kappa, after[size : size + halo]])
+    react_ext = jnp.concatenate([before[size + halo + 1 :], react, after[size + halo :]])
+    return motion_ext, kappa_ext, react_ext
+
+
+def extended_coefficients(kappa_ext, react_ext, points, halo):
     groups = lax.axis_size("sea")
     total_points = points * groups
     where_sea = lax.axis_index("sea")
-    kappa_ext = jnp.concatenate(
-        [from_left(kappa[points - halo - 1 :], "sea"), kappa, from_right(kappa[:halo], "sea")]
-    )
-    react_ext = jnp.concatenate(
-        [from_left(react[points - halo :], "sea"), react, from_right(react[:halo], "sea")]
-    )
     index = where_sea * points - halo + jnp.arange(points + 2 * halo, dtype=jnp.int32)
     valid = (index >= 0) & (index < total_points)
     left_k = jnp.where(valid & (index >= 1), kappa_ext[:-1], 0.0)
@@ -89,15 +102,15 @@
     halo = SWEEPS - 1
     cols = motion.shape[2]
     width = cols // CHUNKS
-    left_k, right_k, diag = extended_coefficients(kappa, react, halo)
-    motion_ext = jnp.concatenate(
-        [from_left(motion[motion.shape[0] - halo :], "sea"), motion, from_right(motion[:halo], "sea")]
-    )
+    motion_ext, kappa_ext, react_ext = exchange_halo(motion, kappa, react, halo)
+    left_k, right_k, diag = extended_coefficients(kappa_ext, react_ext, motion.shape[0], halo)
     table_high, table_low = dft_tables(motion.shape[1] * lax.axis_size("tm"))
     priors = []
     sensors = []
     for c in range(CHUNKS):
-        source = motion_ext[:, :, c * width : (c + 1) * width].astype(jnp.float32)
+        source = motion_ext[:, :, c * width : (c + 1) * width]
+        if priors:
+            source, _ = lax.optimization_barrier((source, priors[-1]))
         prior_part = smooth(source, left_k, right_k, diag, halo).astype(jnp.bfloat16)
         priors.append(prior_part)
         sensors.append(forward_chunk(prior_part, green, table_high, table_low))

time: 413 us -> 390 us (0.944)
  blocking collectives: 103 us -> 51.6 us
  waiting for transfers between devices: 109 us -> 129 us
  other arithmetic: 61.3 us -> 79 us
  starting transfers between devices: 27.3 us -> 19.6 us
    all_to_all x2 -> x1, blocking collectives: 103 us -> 51.6 us  [forward_chunk(): lax.all_to_all(spectrum, 'tm', split_axis=0, concat_axis=2, tiled=True)]
    all_to_all x0 -> x1, waiting for transfers between devices: none -> 30.6 us  [forward_chunk(): lax.all_to_all(spectrum, 'tm', split_axis=0, concat_axis=2, tiled=True)]
    all_to_all x2, waiting for transfers between devices: 25.3 us -> 13.8 us  [forward_chunk(): lax.all_to_all(prior_part, 'tm', split_axis=0, concat_axis=1, tiled=True)]
    ppermute x3 -> x1, starting transfers between devices: 15.7 us -> 5.49 us  [from_left(): return lax.ppermute(block, axis, [(i, i + 1) for i in range(count - 1)])]
    add x7 -> x8, other arithmetic: 25.6 us -> 34.4 us  [smooth(): state = state + weights[k] * (source - applied) / diag]
    all_to_all x0 -> x1, starting transfers between devices: none -> 4.96 us  [forward_chunk(): lax.all_to_all(spectrum, 'tm', split_axis=0, concat_axis=2, tiled=True)]
    another operation x1 -> x2, other arithmetic: 8.5 us -> 5.48 us
  transfers between devices with their start and end apart: 10 -> 7, of which waited for: 3 -> 3; matrix products, arithmetic and copies ran while one was open for 21% -> 30% of each run, Pallas kernels for 0% -> 0%
where the time goes in v2:
time: 390 us; the launch traced here: 389 us
  waiting for transfers between devices  129 us (33%)
  other arithmetic  79 us (20%)
  local copies, waits for them, and re-layouts  65.2 us (17%)
  blocking collectives  51.6 us (13%)
  matrix products  30.3 us (8%)
  starting transfers between devices  19.6 us (5%)
  between operations  14.4 us (4%)
    reduce_scatter x2, waiting for transfers between devices, forward_chunk(): lax.psum_scatter(partial.astype(jnp.bfloat16), 'sea', scatter_dimension=0...  84.2 us
    all_to_all x1, blocking collectives, forward_chunk(): lax.all_to_all(spectrum, 'tm', split_axis=0, concat_axis=2, tiled=True)  51.6 us
    add x8, other arithmetic, smooth(): state = state + weights[k] * (source - applied) / diag  34.4 us
    all_to_all x1, waiting for transfers between devices, forward_chunk(): lax.all_to_all(spectrum, 'tm', split_axis=0, concat_axis=2, tiled=True)  30.6 us
    all_to_all x4, local copies, waits for them, and re-layouts, forward_chunk(): lax.all_to_all(spectrum, 'tm', split_axis=0, concat_axis=2, tiled=True)  29.3 us
    dot_general x2, matrix products, forward_chunk(): jnp.einsum('fksp,fkprc->sfrc', green, mixed, preferred_element_type=jnp.f...  25.4 us
    convert_element_type x2, local copies, waits for them, and re-layouts, forward_chunk(): partial.astype(jnp.bfloat16)  16.1 us
    all_to_all x2, waiting for transfers between devices, forward_chunk(): lax.all_to_all(prior_part, 'tm', split_axis=0, concat_axis=1, tiled=True)  13.8 us
  transfers between devices with their start and end apart: 7, of which 3 were waited for; matrix products, arithmetic and copies ran while one was open for 30% of the time, Pallas kernels for 0%

profile of v2, /device:TPU:0, one launch (start us, length us, event | category | flops | bytes accessed | tf_op | source)
XLA Modules:
  0.0 388.7 jit_solution(687354931740833314)
XLA Ops:
  11.8 5.5 %collective-permute-start = (f32[20491]{0:T(1024)S(1)}, f32[20491]{0:T(1024)S(1)}, u32[]{:S(2)}, u32[]{:S(2)}) collective-permute-start(f32[20491]{0:T(1024)S(1)} %concatenate.24), channel_id=1, source_target_pairs={{0,4},{4,8},{8,12},{12,16},{16,20},{20,24},{24,28},{1,5},{5,9},{9,... | collective-permute-start | bytes 245900 | tf_op jit(solution)/shard_map/ppermute | solution.py:14
  17.3 6.7 %convert_element_type.63 = f32[512,16,256]{2,1,0:T(8,128)} convert(bf16[512,16,256]{2,1,0:T(8,128)(2,1)} %param.4) | non-fusion elementwise | flops 2097152 | bytes 12582912 | tf_op jit(solution)/shard_map/convert_element_type | solution.py:41
  24.7 4.0 %pad_maximum_fusion = f32[522,16,256]{2,1,0:T(8,128)S(1)} fusion(f32[5,16,256]{2,1,0:T(8,128)S(1)} %reshape.125, f32[512,16,256]{2,1,0:T(8,128)} %convert_element_type.63, f32[5,16,256]{2,1,0:T(8,128)S(1)} %reshape.122), kind=kLoop, calls=%fused_computation.4 | loop fusion | flops 4276224 | bytes 17104896 | tf_op jit(solution)/shard_map/concatenate | solution.py:40
  28.7 3.3 fusion.52
  32.0 3.5 divide_add_fusion.7
  35.5 3.5 divide_add_fusion.6
  39.0 3.5 divide_add_fusion.5
  42.5 3.5 divide_add_fusion.4
  51.5 3.9 %all-to-all-start = ((bf16[512,16,128]{2,1,0:T(8,128)(2,1)}), bf16[512,16,128]{2,1,0:T(8,128)(2,1)S(1)}, u32[]{:S(2)}, u32[]{:S(2)}) async-start(bf16[512,16,128]{2,1,0:T(8,128)(2,1)} %fusion.15), calls=%async_computation | async-start | bytes 4194304 | tf_op jit(solution)/shard_map/all_to_all | solution.py:83
  55.4 3.3 multiply_divide_fusion
  58.9 3.3 divide_add_fusion.3
  62.2 4.9 %divide_add_fusion.2 = f32[522,16,128]{2,1,0:T(8,128)} fusion(f32[522,16,128]{2,1,0:T(8,128)S(1)} %divide_add_fusion.3, f32[522,16,128]{2,1,0:T(8,128)S(1)} %bitcast.91, f32[522]{0:T(1024)S(1)} %get-tuple-element.29, f32[522]{0:T(1024)S(1)} %get-tuple-element.27, f32[522]{0:T(1024)S(1)} %get-tuple-element.28), kind=kLoop, calls=%fused_computation.19 | loop fusion | flops 9621504 | bytes 12834936 | tf_op jit(solution)/shard_map/add | solution.py:67
  67.1 13.8 %all-to-all-done = bf16[512,16,128]{2,1,0:T(8,128)(2,1)S(1)} async-done(((bf16[512,16,128]{2,1,0:T(8,128)(2,1)}), bf16[512,16,128]{2,1,0:T(8,128)(2,1)S(1)}, u32[]{:S(2)}, u32[]{:S(2)}) %all-to-all-start) | async-done | bytes 2097184 | tf_op jit(solution)/shard_map/all_to_all | solution.py:83
  84.0 4.7 %copy.14 = bf16[64,2,128,128]{3,2,1,0:T(8,128)(2,1)} copy(bf16[64,2,128,128]{3,0,2,1:T(8,128)(2,1)S(1)} %add_convert_fusion.1) | data formatting | bytes 8388608 | tf_op jit(solution)/shard_map/convert_element_type | solution.py:88
  88.8 5.0 %all-to-all-start.1 = ((bf16[64,2,128,128]{3,2,1,0:T(8,128)(2,1)}), bf16[64,2,128,128]{3,2,1,0:T(8,128)(2,1)}, u32[]{:S(2)}, u32[]{:S(2)}) async-start(bf16[64,2,128,128]{3,2,1,0:T(8,128)(2,1)} %copy.14), calls=%async_computation.1 | async-start | bytes 8388608 | tf_op jit(solution)/shard_map/all_to_all | solution.py:89
  93.7 8.8 %divide_add_fusion.1 = f32[522,16,128]{2,1,0:T(8,128)S(1)} fusion(f32[522,16,128]{2,1,0:T(8,128)} %divide_add_fusion.2, f32[522,16,128]{2,1,0:T(8,128)} %get-tuple-element.3, f32[522]{0:T(1024)S(1)} %get-tuple-element.29, f32[522]{0:T(1024)S(1)} %get-tuple-element.27, f32[522]{0:T(1024)S(1)} %get-tuple-element.28), kind=kLoop, calls=%fused_computation.18 | loop fusion | flops 9621504 | bytes 12834936 | tf_op jit(solution)/shard_map/add | solution.py:67
  102.6 3.4 divide_add_fusion
  111.3 30.6 %all-to-all-done.1 = bf16[64,2,128,128]{3,2,1,0:T(8,128)(2,1)} async-done(((bf16[64,2,128,128]{3,2,1,0:T(8,128)(2,1)}), bf16[64,2,128,128]{3,2,1,0:T(8,128)(2,1)}, u32[]{:S(2)}, u32[]{:S(2)}) %all-to-all-start.1) | async-done | bytes 4194336 | tf_op jit(solution)/shard_map/all_to_all | solution.py:89
  142.0 3.6 all-to-all-start.2
  145.8 7.5 %copy.15 = bf16[4,16,2,128,128]{3,0,4,1,2:T(4,128)(2,1)} copy(bf16[4,16,2,128,128]{4,3,2,1,0:T(8,128)(2,1)} %bitcast.10) | data formatting | bytes 8388608 | tf_op jit(solution)/shard_map/all_to_all | solution.py:89
  153.3 7.2 %all_to_all.59 = bf16[16,2,512,128]{2,3,0,1:T(8,128)(2,1)} reshape(bf16[16,2,4,128,128]{3,2,4,0,1:T(4,128)(2,1)} %bitcast.98) | data formatting | bytes 8388608 | tf_op jit(solution)/shard_map/all_to_all | solution.py:89
  164.1 3.7 maximum_bitcast_fusion
  167.7 12.4 %fusion.10 = bf16[512,16,2,128]{0,3,2,1:T(8,128)(2,1)} fusion(bf16[16,2,512,512]{3,2,1,0:T(8,128)(2,1)} %param.7, bf16[16,1,512,2,128]{2,4,1,3,0:T(8,128)(2,1)} %get-tuple-element.22, bf16[16,1,512,2,128]{2,4,1,3,0:T(8,128)(2,1)} %get-tuple-element.21), kind=kOutput, calls=%fused_computation.29 | convolution fusion | flops 4301258752 | bytes 29360128 | tf_op jit(solution)/shard_map/fksp,fkprc->sfrc/dot_general | solution.py:95
  180.2 8.0 %copy.17 = bf16[512,16,2,128]{3,1,2,0:T(8,128)(2,1)} copy(bf16[512,16,2,128]{0,3,2,1:T(8,128)(2,1)} %fusion.10) | data formatting | bytes 8388608 | tf_op jit(solution)/shard_map/convert_element_type | solution.py:97
  194.1 51.6 %all_to_all.72 = bf16[64,2,128,128]{3,2,1,0:T(8,128)(2,1)} all-to-all(bf16[64,2,128,128]{3,2,1,0:T(8,128)(2,1)S(1)} %copy.19), channel_id=1, replica_groups=mesh['sea'=8,'tm'=4] {'tm'}, dimensions={0} | all-to-all | bytes 8388608 | tf_op jit(solution)/shard_map/all_to_all | solution.py:89
  245.7 7.4 %copy.20 = bf16[4,16,2,128,128]{3,0,4,1,2:T(4,128)(2,1)} copy(bf16[4,16,2,128,128]{4,3,2,1,0:T(8,128)(2,1)} %bitcast.99) | data formatting | bytes 8388608 | tf_op jit(solution)/shard_map/all_to_all | solution.py:89
  253.2 7.3 %all_to_all.67 = bf16[16,2,512,128]{2,3,0,1:T(8,128)(2,1)} reshape(bf16[16,2,4,128,128]{3,2,4,0,1:T(4,128)(2,1)} %bitcast.100) | data formatting | bytes 8388608 | tf_op jit(solution)/shard_map/all_to_all | solution.py:89
  263.7 3.7 maximum_bitcast_fusion.2
  267.3 12.9 %fusion.11 = bf16[512,16,2,128]{0,3,2,1:T(8,128)(2,1)} fusion(bf16[16,2,512,512]{3,2,1,0:T(8,128)(2,1)} %param.7, bf16[16,1,512,2,128]{2,4,1,3,0:T(8,128)(2,1)} %get-tuple-element.24, bf16[16,1,512,2,128]{2,4,1,3,0:T(8,128)(2,1)} %get-tuple-element.23), kind=kOutput, calls=%fused_computation.30 | convolution fusion | flops 4301258752 | bytes 29360128 | tf_op jit(solution)/shard_map/fksp,fkprc->sfrc/dot_general | solution.py:95
  280.2 8.1 %copy.22 = bf16[512,16,2,128]{3,1,2,0:T(8,128)(2,1)} copy(bf16[512,16,2,128]{0,3,2,1:T(8,128)(2,1)} %fusion.11) | data formatting | bytes 8388608 | tf_op jit(solution)/shard_map/convert_element_type | solution.py:97
  288.4 4.7 %pad_maximum_fusion.1 = bf16[512,16,256]{2,1,0:T(8,128)(2,1)} fusion(bf16[512,16,128]{2,1,0:T(8,128)(2,1)} %fusion.12, bf16[512,16,128]{2,1,0:T(8,128)(2,1)} %fusion.15), kind=kLoop, calls=%fused_computation.43 | loop fusion | flops 8388608 | bytes 8388608 | tf_op jit(solution)/shard_map/concatenate | solution.py:117
  293.1 84.2 %reduce-scatter.5.cloned.1.call-done = bf16[64,16,2,128]{3,1,2,0:T(8,128)(2,1)} async-done(((bf16[512,16,2,128]{3,1,2,0:T(8,128)(2,1)}), bf16[64,16,2,128]{3,1,2,0:T(8,128)(2,1)}) %reduce-scatter.5.cloned.1.call-update) | async-done | bytes 524304 | tf_op jit(solution)/shard_map/reduce_scatter | solution.py:96
  (64 shorter events, 36.9 us)
Async XLA Ops:
  9.6 14.6 %collective-permute-start.1 = (f32[20490]{0:T(1024)S(1)}, f32[20490]{0:T(1024)S(1)}, u32[]{:S(2)}, u32[]{:S(2)}) collective-permute-start(f32[20490]{0:T(1024)S(1)} %concatenate.25), channel_id=1, source_target_pairs={{4,0},{8,4},{12,8},{16,12},{20,16},{24,20},{28,24},{5,1},{9,5},{13... | collective-permute-start | bytes 245888 | tf_op jit(solution)/shard_map/ppermute | solution.py:19
  11.8 12.5 %collective-permute-start = (f32[20491]{0:T(1024)S(1)}, f32[20491]{0:T(1024)S(1)}, u32[]{:S(2)}, u32[]{:S(2)}) collective-permute-start(f32[20491]{0:T(1024)S(1)} %concatenate.24), channel_id=1, source_target_pairs={{0,4},{4,8},{8,12},{12,16},{16,20},{20,24},{24,28},{1,5},{5,9},{9,... | collective-permute-start | bytes 245900 | tf_op jit(solution)/shard_map/ppermute | solution.py:14
  17.3 7.1 %copy-start.3 = (f32[512]{0:T(512)S(1)}, f32[512]{0:T(512)}, u32[]{:S(2)}) copy-start(f32[512]{0:T(512)} %param.5) | copy-start | bytes 6148
  17.3 7.2 %copy-start.2 = (f32[512]{0:T(512)S(1)}, f32[512]{0:T(512)}, u32[]{:S(2)}) copy-start(f32[512]{0:T(512)} %param.6) | copy-start | bytes 6148
  51.5 7.2 %slice-start = ((s8[4276224]{0:T(1024)(128)(4,1)}), s8[81920]{0:T(1024)(128)(4,1)S(1)}, s32[]{:S(2)}) async-start(s8[4276224]{0:T(1024)(128)(4,1)} %bitcast.90), calls=%async_computation.8 | async-start | bytes 163840
  51.5 29.4 %all-to-all-start = ((bf16[512,16,128]{2,1,0:T(8,128)(2,1)}), bf16[512,16,128]{2,1,0:T(8,128)(2,1)S(1)}, u32[]{:S(2)}, u32[]{:S(2)}) async-start(bf16[512,16,128]{2,1,0:T(8,128)(2,1)} %fusion.15), calls=%async_computation | async-start | bytes 4194304 | tf_op jit(solution)/shard_map/all_to_all | solution.py:83
  55.4 3.5 slice-start.1
  88.8 13.8 %slice-start.2 = ((s8[4276224]{0:T(1024)(128)(4,1)}), s8[81920]{0:T(1024)(128)(4,1)S(1)}, s32[]{:S(2)}) async-start(s8[4276224]{0:T(1024)(128)(4,1)} %bitcast.92), calls=%async_computation.10 | async-start | bytes 163840
  88.8 53.2 %all-to-all-start.1 = ((bf16[64,2,128,128]{3,2,1,0:T(8,128)(2,1)}), bf16[64,2,128,128]{3,2,1,0:T(8,128)(2,1)}, u32[]{:S(2)}, u32[]{:S(2)}) async-start(bf16[64,2,128,128]{3,2,1,0:T(8,128)(2,1)} %copy.14), calls=%async_computation.1 | async-start | bytes 8388608 | tf_op jit(solution)/shard_map/all_to_all | solution.py:89
  93.7 8.9 %slice-start.3 = ((s8[4276224]{0:T(1024)(128)(4,1)}), s8[4194304]{0:T(1024)(128)(4,1)S(1)}, s32[]{:S(2)}) async-start(s8[4276224]{0:T(1024)(128)(4,1)} %bitcast.92), calls=%async_computation.11 | async-start | bytes 8388608
  142.0 46.3 %all-to-all-start.2 = ((bf16[512,16,128]{2,1,0:T(8,128)(2,1)}), bf16[512,16,128]{2,1,0:T(8,128)(2,1)S(1)}, u32[]{:S(2)}, u32[]{:S(2)}) async-start(bf16[512,16,128]{2,1,0:T(8,128)(2,1)} %fusion.12), calls=%async_computation.3 | async-start | bytes 4194304 | tf_op jit(solution)/shard_map/all_to_all | solution.py:83
  145.6 147.5 %reduce-scatter.3.cloned.1.call-start = ((), (), s32[]{:S(2)}) async-start(), calls=%async_computation.6 | async-start | bytes 4718592 | tf_op jit(solution)/shard_map/reduce_scatter | solution.py:96
  160.5 3.4 copy-start
  188.2 189.1 %reduce-scatter.5.cloned.1.call-start = ((), (), s32[]{:S(2)}) async-start(), calls=%async_computation.7 | async-start | bytes 4718592 | tf_op jit(solution)/shard_map/reduce_scatter | solution.py:96
  260.4 2.8 copy-start.1
Sparse Core Ops, SparseCore 0:
  188.3 89.8 reduce-scatter.2
  288.5 88.7 reduce-scatter.4

commit v3 on v2

--- a/solution.py
+++ b/solution.py
@@ -38,7 +38,11 @@
     before = from_left(tail, "sea")
     after = from_right(head, "sea")
     motion_ext = jnp.concatenate(
-        [before[:size].reshape(shape), motion.astype(jnp.float32), after[:size].reshape(shape)]
+        [
+            before[:size].reshape(shape).astype(motion.dtype),
+            motion,
+            after[:size].reshape(shape).astype(motion.dtype),
+        ]
     )
     kappa_ext = jnp.concatenate([before[size : size + halo + 1], kappa, after[size : size + halo]])
     react_ext = jnp.concatenate([before[size + halo + 1 :], react, after[size + halo :]])
@@ -80,22 +84,26 @@
 
 
 def forward_chunk(prior_part, green, table_high, table_low):
+    ways = lax.axis_size("tm")
     piece = lax.all_to_all(prior_part, "tm", split_axis=0, concat_axis=1, tiled=True)
-    spectrum = jnp.einsum("fkt,ptc->fkpc", table_high, piece, preferred_element_type=jnp.float32)
+    steps_all = piece.shape[1]
+    high = table_high.reshape(ways, steps_all // ways, 2, steps_all)
+    low = table_low.reshape(ways, steps_all // ways, 2, steps_all)
+    spectrum = jnp.einsum("jfkt,qtc->jfkqc", high, piece, preferred_element_type=jnp.float32)
     spectrum = spectrum + jnp.einsum(
-        "fkt,ptc->fkpc", table_low, piece, preferred_element_type=jnp.float32
+        "jfkt,qtc->jfkqc", low, piece, preferred_element_type=jnp.float32
     )
     spectrum = spectrum.astype(jnp.bfloat16)
-    spectra = lax.all_to_all(spectrum, "tm", split_axis=0, concat_axis=2, tiled=True)
-    real_s = spectra[:, 0]
-    imag_s = spectra[:, 1]
+    spectra = lax.all_to_all(spectrum, "tm", split_axis=0, concat_axis=0)
+    real_s = spectra[:, :, 0]
+    imag_s = spectra[:, :, 1]
     mixed = jnp.stack(
-        [jnp.stack([real_s, imag_s], axis=2), jnp.stack([-imag_s, real_s], axis=2)], axis=1
+        [jnp.stack([real_s, imag_s], axis=2), jnp.stack([-imag_s, real_s], axis=2)], axis=0
     )
-    partial = jnp.einsum("fksp,fkprc->sfrc", green, mixed, preferred_element_type=jnp.float32)
-    return lax.psum_scatter(
-        partial.astype(jnp.bfloat16), "sea", scatter_dimension=0, tiled=True
-    ).astype(jnp.float32)
+    blocks = green.reshape(green.shape[:3] + (ways, green.shape[3] // ways))
+    partial = jnp.einsum("fksjq,kjfrqc->fsrc", blocks, mixed, preferred_element_type=jnp.float32)
+    summed = lax.psum_scatter(partial.astype(jnp.bfloat16), "sea", scatter_dimension=1, tiled=True)
+    return jnp.transpose(summed, (1, 0, 2, 3)).astype(jnp.float32)
 
 
 def on_device(motion, kappa, react, green):
@@ -111,7 +119,7 @@
         source = motion_ext[:, :, c * width : (c + 1) * width]
         if priors:
             source, _ = lax.optimization_barrier((source, priors[-1]))
-        prior_part = smooth(source, left_k, right_k, diag, halo).astype(jnp.bfloat16)
+        prior_part = smooth(source.astype(jnp.float32), left_k, right_k, diag, halo).astype(jnp.bfloat16)
         priors.append(prior_part)
         sensors.append(forward_chunk(prior_part, green, table_high, table_low))
     return (jnp.concatenate(priors, axis=2), jnp.concatenate(sensors, axis=3))

time: 390 us -> 388 us (level)
  local copies, waits for them, and re-layouts: 65.2 us -> 51.3 us
  matrix products: 30.3 us -> 39.2 us
  waiting for transfers between devices: 129 us -> 135 us
    all_to_all x4 -> x0, local copies, waits for them, and re-layouts: 29.3 us -> none  [forward_chunk(): lax.all_to_all(spectrum, 'tm', split_axis=0, concat_axis=2, tiled=True)]
    reshape x2 -> x1, local copies, waits for them, and re-layouts: 0.05 us -> 23.7 us  [forward_chunk(): blocks = green.reshape(green.shape[:3] + (ways, green.shape[3] // ways))]
    dot_general x6, matrix products: 30.3 us -> 39.2 us  [the longest x2 32.2 us: forward_chunk(): jnp.einsum('fksjq,kjfrqc->fsrc', blocks, mixed, preferred_element_type=jn...]
    another operation x2 -> x4, other arithmetic: 7.3 us -> 15.2 us  [forward_chunk(): jnp.stack([jnp.stack([real_s, imag_s], axis=2), jnp.stack([-imag_s, real_...]
    convert_element_type x2, local copies, waits for them, and re-layouts: 7.41 us -> 0.04 us  [the longest x1 0.02 us: exchange_halo(): after[:size].reshape(shape).astype(motion.dtype)]
    reduce_scatter x2, waiting for transfers between devices: 84.2 us -> 90.2 us  [forward_chunk(): lax.psum_scatter(partial.astype(jnp.bfloat16), 'sea', scatter_dimension=1...]
    concatenate x1 -> x0, other arithmetic: 4.03 us -> none  [exchange_halo(): jnp.concatenate([before[:size].reshape(shape), motion.astype(jnp.float32)...]
  transfers between devices with their start and end apart: 7 -> 7, of which waited for: 3 -> 3; matrix products, arithmetic and copies ran while one was open for 30% -> 33% of each run, Pallas kernels for 0% -> 0%
where the time goes in v3:
time: 388 us; the launch traced here: 386 us
  waiting for transfers between devices  135 us (35%)
  other arithmetic  75.2 us (19%)
  local copies, waits for them, and re-layouts  51.3 us (13%)
  blocking collectives  51.2 us (13%)
  matrix products  39.2 us (10%)
  starting transfers between devices  20.1 us (5%)
  between operations  14.4 us (4%)
    reduce_scatter x2, waiting for transfers between devices, forward_chunk(): lax.psum_scatter(partial.astype(jnp.bfloat16), 'sea', scatter_dimension=1...  90.2 us
    all_to_all x1, blocking collectives, forward_chunk(): spectra = lax.all_to_all(spectrum, 'tm', split_axis=0, concat_axis=0)  51.2 us
    add x8, other arithmetic, smooth(): state = state + weights[k] * (source - applied) / diag  33.7 us
    dot_general x2, matrix products, forward_chunk(): jnp.einsum('fksjq,kjfrqc->fsrc', blocks, mixed, preferred_element_type=jn...  32.2 us
    all_to_all x1, waiting for transfers between devices, forward_chunk(): spectra = lax.all_to_all(spectrum, 'tm', split_axis=0, concat_axis=0)  31.6 us
    reshape x1, local copies, waits for them, and re-layouts, forward_chunk(): blocks = green.reshape(green.shape[:3] + (ways, green.shape[3] // ways))  23.7 us
    convert_element_type x2, local copies, waits for them, and re-layouts, forward_chunk(): partial.astype(jnp.bfloat16)  16.2 us
    another operation x4, other arithmetic, forward_chunk(): jnp.stack([jnp.stack([real_s, imag_s], axis=2), jnp.stack([-imag_s, real_...  15.2 us
  transfers between devices with their start and end apart: 7, of which 3 were waited for; matrix products, arithmetic and copies ran while one was open for 33% of the time, Pallas kernels for 0%

profile of v3, /device:TPU:0, one launch (start us, length us, event | category | flops | bytes accessed | tf_op | source)
XLA Modules:
  0.0 386.5 jit_solution(12631033525058090273)
XLA Ops:
  11.8 5.5 %collective-permute-start = (f32[20491]{0:T(1024)S(1)}, f32[20491]{0:T(1024)S(1)}, u32[]{:S(2)}, u32[]{:S(2)}) collective-permute-start(f32[20491]{0:T(1024)S(1)} %concatenate.24), channel_id=1, source_target_pairs={{0,4},{4,8},{8,12},{12,16},{16,20},{20,24},{24,28},{1,5},{5,9},{9,... | collective-permute-start | bytes 245900 | tf_op jit(solution)/shard_map/ppermute | solution.py:14
  17.5 23.7 %reshape.116 = bf16[16,2,512,4,128]{4,3,2,1,0:T(4,128)(2,1)} reshape(bf16[16,2,512,512]{3,2,1,0:T(8,128)(2,1)} %param.7) | data formatting | bytes 33554432 | tf_op jit(solution)/shard_map/reshape | solution.py:103
  41.4 2.5 constant_dynamic-update-slice_fusion.1
  46.3 3.5 fusion.9
  49.9 3.5 fusion.12
  53.4 3.5 fusion.15
  56.9 3.5 fusion.18
  60.4 2.7 multiply_subtract_fusion.1
  63.0 2.8 fusion.37
  65.9 4.5 %all-to-all-start = ((bf16[512,16,128]{2,1,0:T(8,128)(2,1)}), bf16[512,16,128]{2,1,0:T(8,128)(2,1)}, u32[]{:S(2)}, u32[]{:S(2)}) async-start(bf16[512,16,128]{2,1,0:T(8,128)(2,1)} %fusion.37), calls=%async_computation | async-start | bytes 4194304 | tf_op jit(solution)/shard_map/all_to_all | solution.py:88
  74.3 3.5 fusion.22
  77.8 5.0 %fusion.25 = f32[522,16,128]{2,1,0:T(8,128)} fusion(f32[522,16,128]{2,1,0:T(8,128)S(1)} %fusion.22, bf16[522,16,128]{2,1,0:T(8,128)(2,1)S(1)} %get-tuple-element.3, f32[522]{0:T(1024)S(1)} %get-tuple-element.26, f32[522]{0:T(1024)S(1)} %get-tuple-element.24, f32[522]{0:T(1024)S(1)} %get-tuple-element.25), kind=kLoop, calls=%fused_computation.41 | loop fusion | flops 10690560 | bytes 10696824 | tf_op jit(solution)/shard_map/add | solution.py:71
  82.8 13.4 %all-to-all-done = bf16[512,16,128]{2,1,0:T(8,128)(2,1)} async-done(((bf16[512,16,128]{2,1,0:T(8,128)(2,1)}), bf16[512,16,128]{2,1,0:T(8,128)(2,1)}, u32[]{:S(2)}, u32[]{:S(2)}) %all-to-all-start) | async-done | bytes 2097184 | tf_op jit(solution)/shard_map/all_to_all | solution.py:88
  99.6 3.2 add_convert_fusion.1
  102.9 5.1 %all-to-all-start.1 = ((bf16[4,16,2,128,128]{4,1,3,2,0:T(8,128)(2,1)}), bf16[4,16,2,128,128]{4,1,3,2,0:T(8,128)(2,1)}, u32[]{:S(2)}, u32[]{:S(2)}) async-start(bf16[4,16,2,128,128]{4,1,3,2,0:T(8,128)(2,1)} %add_convert_fusion.1), calls=%async_computation.1 | async-start | bytes 8388608 | tf_op jit(solution)/shard_map/all_to_all | solution.py:97
  108.0 7.7 %fusion.28 = f32[522,16,128]{2,1,0:T(8,128)S(1)} fusion(f32[522,16,128]{2,1,0:T(8,128)} %fusion.25, bf16[522,16,128]{2,1,0:T(8,128)(2,1)S(1)} %get-tuple-element.3, f32[522]{0:T(1024)S(1)} %get-tuple-element.26, f32[522]{0:T(1024)S(1)} %get-tuple-element.24, f32[522]{0:T(1024)S(1)} %get-tuple-element.25), kind=kLoop, calls=%fused_computation.44 | loop fusion | flops 10690560 | bytes 10696824 | tf_op jit(solution)/shard_map/add | solution.py:71
  115.7 3.5 fusion.31
  119.2 2.7 multiply_subtract_fusion
  121.9 2.6 fusion.34
  124.4 31.6 %all-to-all-done.1 = bf16[4,16,2,128,128]{4,1,3,2,0:T(8,128)(2,1)} async-done(((bf16[4,16,2,128,128]{4,1,3,2,0:T(8,128)(2,1)}), bf16[4,16,2,128,128]{4,1,3,2,0:T(8,128)(2,1)}, u32[]{:S(2)}, u32[]{:S(2)}) %all-to-all-start.1) | async-done | bytes 4194336 | tf_op jit(solution)/shard_map/all_to_all | solution.py:97
  156.0 3.6 all-to-all-start.2
  159.7 2.6 slice_negate_fusion.1
  162.7 6.2 %pad_maximum_fusion = bf16[2,4,16,2,128,128]{5,2,4,3,1,0:T(8,128)(2,1)} fusion(bf16[1,4,16,2,128,128]{5,2,4,3,1,0:T(8,128)(2,1)S(1)} %maximum_bitcast_fusion, bf16[1,4,16,2,128,128]{5,2,4,3,1,0:T(8,128)(2,1)} %bitcast.12), kind=kLoop, calls=%fused_computation.4 | loop fusion | flops 4194304 | bytes 16777216 | tf_op jit(solution)/shard_map/stack | solution.py:100
  168.9 16.1 %fusion.32 = bf16[16,512,2,128]{1,3,2,0:T(8,128)(2,1)} fusion(bf16[16,2,512,4,128,1]{4,3,2,1,0,5:T(4,128)(2,1)} %bitcast.67, bf16[2,4,16,2,128,128]{5,2,4,3,1,0:T(8,128)(2,1)} %pad_maximum_fusion), kind=kOutput, calls=%fused_computation.52 | convolution fusion | flops 4297064448 | bytes 29360128 | tf_op jit(solution)/shard_map/fksjq,kjfrqc->fsrc/dot_general | solution.py:104
  185.0 8.0 %copy.29 = bf16[16,512,2,128]{3,0,2,1:T(8,128)(2,1)} copy(bf16[16,512,2,128]{1,3,2,0:T(8,128)(2,1)} %fusion.32) | data formatting | bytes 8388608 | tf_op jit(solution)/shard_map/convert_element_type | solution.py:105
  196.3 51.2 %all_to_all.46 = bf16[4,16,2,128,128]{4,1,3,2,0:T(8,128)(2,1)S(1)} all-to-all(bf16[4,16,2,128,128]{4,1,3,2,0:T(8,128)(2,1)S(1)} %add_convert_fusion), channel_id=1, replica_groups=mesh['sea'=8,'tm'=4] {'tm'}, dimensions={0} | all-to-all | bytes 8388608 | tf_op jit(solution)/shard_map/all_to_all | solution.py:97
  250.2 6.2 %pad_maximum_fusion.1 = bf16[2,4,16,2,128,128]{5,2,4,3,1,0:T(8,128)(2,1)} fusion(bf16[1,4,16,2,128,128]{5,2,4,3,1,0:T(8,128)(2,1)} %maximum_bitcast_fusion.1, bf16[1,4,16,2,128,128]{5,2,4,3,1,0:T(8,128)(2,1)S(1)} %bitcast.60), kind=kLoop, calls=%fused_computation.5 | loop fusion | flops 4194304 | bytes 16777216 | tf_op jit(solution)/shard_map/stack | solution.py:100
  256.5 16.1 %fusion.33 = bf16[16,512,2,128]{1,3,2,0:T(8,128)(2,1)} fusion(bf16[16,2,512,4,128,1]{4,3,2,1,0,5:T(4,128)(2,1)} %bitcast.68, bf16[2,4,16,2,128,128]{5,2,4,3,1,0:T(8,128)(2,1)} %pad_maximum_fusion.1), kind=kOutput, calls=%fused_computation.53 | convolution fusion | flops 4297064448 | bytes 29360128 | tf_op jit(solution)/shard_map/fksjq,kjfrqc->fsrc/dot_general | solution.py:104
  272.6 8.2 %copy.35 = bf16[16,512,2,128]{3,0,2,1:T(8,128)(2,1)} copy(bf16[16,512,2,128]{1,3,2,0:T(8,128)(2,1)} %fusion.33) | data formatting | bytes 8388608 | tf_op jit(solution)/shard_map/convert_element_type | solution.py:105
  280.8 4.1 %pad_maximum_fusion.2 = bf16[512,16,256]{2,1,0:T(8,128)(2,1)} fusion(bf16[512,16,128]{2,1,0:T(8,128)(2,1)} %fusion.34, bf16[512,16,128]{2,1,0:T(8,128)(2,1)S(1)} %copy-done), kind=kLoop, calls=%fused_computation.66 | loop fusion | flops 8388608 | bytes 8388608 | tf_op jit(solution)/shard_map/concatenate | solution.py:125
  284.9 90.2 %reduce-scatter.5.cloned.1.call-done = bf16[16,64,2,128]{3,0,2,1:T(8,128)(2,1)} async-done(((bf16[16,512,2,128]{3,0,2,1:T(8,128)(2,1)}), bf16[16,64,2,128]{3,0,2,1:T(8,128)(2,1)}) %reduce-scatter.5.cloned.1.call-update) | async-done | bytes 524304 | tf_op jit(solution)/shard_map/reduce_scatter | solution.py:105
  376.4 3.2 copy.36
  (56 shorter events, 22.5 us)
Async XLA Ops:
  9.6 31.6 %collective-permute-start.1 = (f32[20490]{0:T(1024)S(1)}, f32[20490]{0:T(1024)S(1)}, u32[]{:S(2)}, u32[]{:S(2)}) collective-permute-start(f32[20490]{0:T(1024)S(1)} %concatenate.25), channel_id=1, source_target_pairs={{4,0},{8,4},{12,8},{16,12},{20,16},{24,20},{28,24},{5,1},{9,5},{13... | collective-permute-start | bytes 245888 | tf_op jit(solution)/shard_map/ppermute | solution.py:19
  11.8 29.6 %collective-permute-start = (f32[20491]{0:T(1024)S(1)}, f32[20491]{0:T(1024)S(1)}, u32[]{:S(2)}, u32[]{:S(2)}) collective-permute-start(f32[20491]{0:T(1024)S(1)} %concatenate.24), channel_id=1, source_target_pairs={{0,4},{4,8},{8,12},{12,16},{16,20},{20,24},{24,28},{1,5},{5,9},{9,... | collective-permute-start | bytes 245900 | tf_op jit(solution)/shard_map/ppermute | solution.py:14
  41.4 2.5 copy-start.2
  41.4 2.7 copy-start.1
  65.9 30.3 %all-to-all-start = ((bf16[512,16,128]{2,1,0:T(8,128)(2,1)}), bf16[512,16,128]{2,1,0:T(8,128)(2,1)}, u32[]{:S(2)}, u32[]{:S(2)}) async-start(bf16[512,16,128]{2,1,0:T(8,128)(2,1)} %fusion.37), calls=%async_computation | async-start | bytes 4194304 | tf_op jit(solution)/shard_map/all_to_all | solution.py:88
  102.9 53.1 %all-to-all-start.1 = ((bf16[4,16,2,128,128]{4,1,3,2,0:T(8,128)(2,1)}), bf16[4,16,2,128,128]{4,1,3,2,0:T(8,128)(2,1)}, u32[]{:S(2)}, u32[]{:S(2)}) async-start(bf16[4,16,2,128,128]{4,1,3,2,0:T(8,128)(2,1)} %add_convert_fusion.1), calls=%async_computation.1 | async-start | bytes 8388608 | tf_op jit(solution)/shard_map/all_to_all | solution.py:97
  115.7 6.2 %slice-start = ((s8[4276224]{0:T(1024)(128)(4,1)}), s8[4194304]{0:T(1024)(128)(4,1)S(1)}, s32[]{:S(2)}) async-start(s8[4276224]{0:T(1024)(128)(4,1)} %bitcast.65), calls=%async_computation.8 | async-start | bytes 8388608
  119.2 2.7 slice-start.1
  156.0 37.1 %all-to-all-start.2 = ((bf16[512,16,128]{2,1,0:T(8,128)(2,1)}), bf16[512,16,128]{2,1,0:T(8,128)(2,1)S(1)}, u32[]{:S(2)}, u32[]{:S(2)}) async-start(bf16[512,16,128]{2,1,0:T(8,128)(2,1)} %fusion.34), calls=%async_computation.3 | async-start | bytes 4194304 | tf_op jit(solution)/shard_map/all_to_all | solution.py:88
  159.6 125.2 %reduce-scatter.3.cloned.1.call-start = ((), (), s32[]{:S(2)}) async-start(), calls=%async_computation.6 | async-start | bytes 4718592 | tf_op jit(solution)/shard_map/reduce_scatter | solution.py:105
  193.1 182.0 %reduce-scatter.5.cloned.1.call-start = ((), (), s32[]{:S(2)}) async-start(), calls=%async_computation.7 | async-start | bytes 4718592 | tf_op jit(solution)/shard_map/reduce_scatter | solution.py:105
  272.6 8.2 %copy-start = (bf16[512,16,128]{2,1,0:T(8,128)(2,1)S(1)}, bf16[512,16,128]{2,1,0:T(8,128)(2,1)}, u32[]{:S(2)}) copy-start(bf16[512,16,128]{2,1,0:T(8,128)(2,1)} %fusion.37) | copy-start | bytes 6291460
Sparse Core Ops, SparseCore 0:
  193.2 89.9 reduce-scatter.2
  287.3 87.6 reduce-scatter.4

commit v4 on v3

--- a/solution.py
+++ b/solution.py
@@ -106,6 +106,44 @@
     return jnp.transpose(summed, (1, 0, 2, 3)).astype(jnp.float32)
 
 
+def gathered_tables(blocks, steps_all):
+    ways = lax.axis_size("tm")
+    where_tm = lax.axis_index("tm").astype(jnp.int32)
+    local = steps_all // ways
+    freq_ids = where_tm * local + jnp.arange(local, dtype=jnp.int32)
+    step_ids = (jnp.stack(blocks)[:, None] * local + jnp.arange(local, dtype=jnp.int32)).reshape(-1)
+    phase_ids = freq_ids[:, None] * step_ids[None, :] % steps_all
+    angles = phase_ids.astype(jnp.float32) * (2.0 * math.pi / steps_all)
+    scale = 1.0 / math.sqrt(steps_all)
+    real_w = jnp.cos(angles) * scale
+    imag_w = -jnp.sin(angles) * scale
+    table = jnp.stack(
+        [jnp.stack([real_w, imag_w], axis=1), jnp.stack([-imag_w, real_w], axis=1)], axis=1
+    )
+    table_high = lax.optimization_barrier(table.astype(jnp.bfloat16))
+    table_low = (table - table_high.astype(jnp.float32)).astype(jnp.bfloat16)
+    return table_high, table_low
+
+
+def forward_gathered(prior_part, green):
+    where_tm = lax.axis_index("tm").astype(jnp.int32)
+    across = lax.ppermute(prior_part, "tm", [(0, 2), (2, 0), (1, 3), (3, 1)])
+    mine = jnp.concatenate([prior_part, across], axis=1)
+    theirs = lax.ppermute(mine, "tm", [(0, 1), (1, 0), (2, 3), (3, 2)])
+    stacked = jnp.concatenate([mine, theirs], axis=1)
+    blocks = [where_tm, where_tm ^ 2, where_tm ^ 1, where_tm ^ 3]
+    steps_all = prior_part.shape[1] * len(blocks)
+    table_high, table_low = gathered_tables(blocks, steps_all)
+    mixed = jnp.einsum("fkrt,ptc->fkrpc", table_high, stacked, preferred_element_type=jnp.float32)
+    mixed = mixed + jnp.einsum(
+        "fkrt,ptc->fkrpc", table_low, stacked, preferred_element_type=jnp.float32
+    )
+    mixed = mixed.astype(jnp.bfloat16)
+    partial = jnp.einsum("fksp,fkrpc->fsrc", green, mixed, preferred_element_type=jnp.float32)
+    summed = lax.psum_scatter(partial.astype(jnp.bfloat16), "sea", scatter_dimension=1, tiled=True)
+    return jnp.transpose(summed, (1, 0, 2, 3)).astype(jnp.float32)
+
+
 def on_device(motion, kappa, react, green):
     halo = SWEEPS - 1
     cols = motion.shape[2]
@@ -121,7 +159,10 @@
             source, _ = lax.optimization_barrier((source, priors[-1]))
         prior_part = smooth(source.astype(jnp.float32), left_k, right_k, diag, halo).astype(jnp.bfloat16)
         priors.append(prior_part)
-        sensors.append(forward_chunk(prior_part, green, table_high, table_low))
+        if lax.axis_size("tm") == 4:
+            sensors.append(forward_gathered(prior_part, green))
+        else:
+            sensors.append(forward_chunk(prior_part, green, table_high, table_low))
     return (jnp.concatenate(priors, axis=2), jnp.concatenate(sensors, axis=3))
 
 

time: 388 us -> 392 us (1.010)
  waiting for transfers between devices: 135 us -> 216 us
  blocking collectives: 51.2 us -> 0 us
  matrix products: 39.2 us -> 69.7 us
  local copies, waits for them, and re-layouts: 51.3 us -> 24.7 us
  other arithmetic: 75.2 us -> 56 us
  starting transfers between devices: 20.1 us -> 10.6 us
    ppermute x0 -> x4, waiting for transfers between devices: none -> 78.8 us  [the longest x2 78.8 us: forward_gathered(): across = lax.ppermute(prior_part, 'tm', [(0, 2), (2, 0), (1, 3), (3, 1)])]
    all_to_all x1 -> x0, blocking collectives: 51.2 us -> none  [forward_chunk(): spectra = lax.all_to_all(spectrum, 'tm', split_axis=0, concat_axis=0)]
    all_to_all x3 -> x0, waiting for transfers between devices: 44.9 us -> none  [the longest x1 31.6 us: forward_chunk(): spectra = lax.all_to_all(spectrum, 'tm', split_axis=0, concat_axis=0)]
    reduce_scatter x2, waiting for transfers between devices: 90.2 us -> 135 us  [forward_gathered(): lax.psum_scatter(partial.astype(jnp.bfloat16), 'sea', scatter_dimension=1...]
    dot_general x6, matrix products: 39.2 us -> 69.7 us  [the longest x2 25.9 us: forward_gathered(): jnp.einsum('fksp,fkrpc->fsrc', green, mixed, preferred_element_type=jnp.f...]
    reshape x1 -> x0, local copies, waits for them, and re-layouts: 23.7 us -> none  [forward_chunk(): blocks = green.reshape(green.shape[:3] + (ways, green.shape[3] // ways))]
    another operation x6 -> x3, other arithmetic: 20.6 us -> 4.45 us  [the longest x4 15.2 us: forward_chunk(): jnp.stack([jnp.stack([real_s, imag_s], axis=2), jnp.stack([-imag_s, real_...]
    all_to_all x3 -> x0, starting transfers between devices: 13.2 us -> none  [the longest x2 8.11 us: forward_chunk(): lax.all_to_all(prior_part, 'tm', split_axis=0, concat_axis=1, tiled=True)]
  transfers between devices with their start and end apart: 7 -> 8, of which waited for: 3 -> 5; matrix products, arithmetic and copies ran while one was open for 33% -> 30% of each run, Pallas kernels for 0% -> 0%
where the time goes in v4:
time: 392 us; the launch traced here: 391 us
  waiting for transfers between devices  216 us (55%)
  matrix products  69.7 us (18%)
  other arithmetic  56 us (14%)
  local copies, waits for them, and re-layouts  24.7 us (6%)
  between operations  14.3 us (4%)
  starting transfers between devices  10.6 us (3%)
    reduce_scatter x2, waiting for transfers between devices, forward_gathered(): lax.psum_scatter(partial.astype(jnp.bfloat16), 'sea', scatter_dimension=1...  135 us
    ppermute x2, waiting for transfers between devices, forward_gathered(): across = lax.ppermute(prior_part, 'tm', [(0, 2), (2, 0), (1, 3), (3, 1)])  78.8 us
    add x8, other arithmetic, smooth(): state = state + weights[k] * (source - applied) / diag  28 us
    dot_general x2, matrix products, forward_gathered(): jnp.einsum('fksp,fkrpc->fsrc', green, mixed, preferred_element_type=jnp.f...  25.9 us
    dot_general x2, matrix products, forward_gathered(): jnp.einsum('fkrt,ptc->fkrpc', table_high, stacked, preferred_element_type...  25.9 us
    dot_general x2, matrix products, forward_gathered(): jnp.einsum('fkrt,ptc->fkrpc', table_low, stacked, preferred_element_type=...  17.9 us
    convert_element_type x2, local copies, waits for them, and re-layouts, forward_gathered(): partial.astype(jnp.bfloat16)  16.1 us
  transfers between devices with their start and end apart: 8, of which 5 were waited for; matrix products, arithmetic and copies ran while one was open for 30% of the time, Pallas kernels for 0%

profile of v4, /device:TPU:0, one launch (start us, length us, event | category | flops | bytes accessed | tf_op | source)
XLA Modules:
  0.0 390.9 jit_solution(10044823175186444433)
XLA Ops:
  11.8 5.5 %collective-permute-start = (f32[20491]{0:T(1024)S(1)}, f32[20491]{0:T(1024)S(1)}, u32[]{:S(2)}, u32[]{:S(2)}) collective-permute-start(f32[20491]{0:T(1024)S(1)} %concatenate.42), channel_id=1, source_target_pairs={{0,4},{4,8},{8,12},{12,16},{16,20},{20,24},{24,28},{1,5},{5,9},{9,... | collective-permute-start | bytes 245900 | tf_op jit(solution)/shard_map/ppermute | solution.py:14
  17.5 2.0 collective-permute-done
  19.5 2.5 constant_dynamic-update-slice_fusion.1
  24.4 3.5 fusion.11
  27.9 3.5 fusion.14
  31.4 3.5 fusion.17
  34.9 3.5 fusion.20
  38.4 2.7 multiply_subtract_fusion.1
  41.1 1.7 fusion.39
  42.8 2.1 collective-permute-start.2
  46.4 3.5 fusion.24
  49.9 3.5 fusion.27
  53.4 3.5 fusion.30
  56.9 32.5 %collective-permute-done.2 = bf16[512,16,128]{2,1,0:T(8,128)(2,1)S(1)} collective-permute-done((bf16[512,16,128]{2,1,0:T(8,128)(2,1)S(1)}, bf16[512,16,128]{2,1,0:T(8,128)(2,1)S(1)}, u32[]{:S(2)}, u32[]{:S(2)}) %collective-permute-start.2) | collective-permute-done | bytes 2097184 | tf_op jit(solution)/shard_map/ppermute | solution.py:130
  89.5 2.7 pad_maximum_fusion.1
  92.2 3.5 fusion.33
  96.0 2.7 multiply_subtract_fusion
  98.6 2.7 fusion.36
  103.4 46.3 %collective-permute-done.4 = bf16[512,16,128]{2,1,0:T(8,128)(2,1)} collective-permute-done((bf16[512,16,128]{2,1,0:T(8,128)(2,1)}, bf16[512,16,128]{2,1,0:T(8,128)(2,1)}, u32[]{:S(2)}, u32[]{:S(2)}) %collective-permute-start.4) | collective-permute-done | bytes 2097184 | tf_op jit(solution)/shard_map/ppermute | solution.py:130
  149.7 5.0 %pad_maximum_fusion.2 = bf16[512,32,128]{2,1,0:T(8,128)(2,1)} fusion(bf16[512,16,128]{2,1,0:T(8,128)(2,1)} %collective-permute-done.4, bf16[512,16,128]{2,1,0:T(8,128)(2,1)} %fusion.36), kind=kLoop, calls=%fused_computation.70 | loop fusion | flops 8388608 | bytes 8388608 | tf_op jit(solution)/shard_map/concatenate | solution.py:131
  154.7 8.7 %fusion.7 = f32[16,2,2,512,128]{4,0,3,2,1:T(8,128)} fusion(bf16[512,32,128]{2,1,0:T(8,128)(2,1)} %collective-permute-done.3, bf16[512,16,128]{2,1,0:T(8,128)(2,1)S(1)} %copy-done.1, bf16[512,16,128]{2,1,0:T(8,128)(2,1)S(1)} %fusion.39, bf16[16,2,2,64]{3,0,2,1:T(8,128)(2,1)S(1)} %fusion.50, f32[16,1,2,64]{3,0,2,1:T(8,128)S(1)} %get-tuple-element.21, ...), kind=kOutput, calls=%fused_computation.23 | convolution fusion | flops 562053120 | bytes 25190400 | tf_op jit(solution)/shard_map/fkrt,ptc->fkrpc/dot_general | solution.py:138
  163.4 12.4 %add_convert_fusion.1 = bf16[16,2,2,512,128]{4,0,3,2,1:T(8,128)(2,1)} fusion(f32[16,2,2,512,128]{4,0,3,2,1:T(8,128)} %fusion.7, bf16[512,32,128]{2,1,0:T(8,128)(2,1)} %collective-permute-done.3, bf16[512,16,128]{2,1,0:T(8,128)(2,1)} %copy-done, bf16[512,16,128]{2,1,0:T(8,128)(2,1)S(1)} %fusion.39, bf16[16,2,2,64]{3,0,2,1:T(8,128)(2,1)S(1)} %fusion.50), kind=kOutput, calls=%fused_computation.5 | convolution fusion | flops 570425344 | bytes 33562624 | tf_op jit(solution)/shard_map/fkrt,ptc->fkrpc/dot_general | solution.py:137
  175.9 12.7 %fusion.34 = bf16[16,512,2,128]{1,3,2,0:T(8,128)(2,1)} fusion(bf16[16,2,512,512]{3,2,1,0:T(8,128)(2,1)} %param.7, bf16[16,2,2,512,128]{4,0,3,2,1:T(8,128)(2,1)} %add_convert_fusion.1), kind=kOutput, calls=%fused_computation.54 | convolution fusion | flops 4297064448 | bytes 29360128 | tf_op jit(solution)/shard_map/fksp,fkrpc->fsrc/dot_general | solution.py:142
  188.6 8.1 %copy.11 = bf16[16,512,2,128]{3,0,2,1:T(8,128)(2,1)} copy(bf16[16,512,2,128]{1,3,2,0:T(8,128)(2,1)} %fusion.34) | data formatting | bytes 8388608 | tf_op jit(solution)/shard_map/convert_element_type | solution.py:143
  196.8 9.1 %fusion.6 = f32[16,2,2,512,128]{4,0,3,2,1:T(8,128)} fusion(bf16[512,32,128]{2,1,0:T(8,128)(2,1)} %collective-permute-done.5, bf16[512,16,128]{2,1,0:T(8,128)(2,1)} %collective-permute-done.4, bf16[512,16,128]{2,1,0:T(8,128)(2,1)} %fusion.36, bf16[16,2,2,64]{3,0,2,1:T(8,128)(2,1)S(1)} %fusion.50, f32[16,1,2,64]{3,0,2,1:T(8,128)S(1)} %get-tuple-element.21, ...), kind=kOutput, calls=%fused_computation.22 | convolution fusion | flops 562053120 | bytes 25190400 | tf_op jit(solution)/shard_map/fkrt,ptc->fkrpc/dot_general | solution.py:138
  205.9 13.4 %add_convert_fusion = bf16[16,2,2,512,128]{4,0,3,2,1:T(8,128)(2,1)} fusion(f32[16,2,2,512,128]{4,0,3,2,1:T(8,128)} %fusion.6, bf16[512,32,128]{2,1,0:T(8,128)(2,1)} %collective-permute-done.5, bf16[512,16,128]{2,1,0:T(8,128)(2,1)} %collective-permute-done.4, bf16[512,16,128]{2,1,0:T(8,128)(2,1)} %fusion.36, bf16[16,2,2,64]{3,0,2,1:T(8,128)(2,1)S(1)} %fusion.50), kind=kOutput, calls=%fused_computation.4 | convolution fusion | flops 570425344 | bytes 33562624 | tf_op jit(solution)/shard_map/fkrt,ptc->fkrpc/dot_general | solution.py:137
  219.3 13.2 %fusion.35 = bf16[16,512,2,128]{1,3,2,0:T(8,128)(2,1)} fusion(bf16[16,2,512,512]{3,2,1,0:T(8,128)(2,1)} %param.7, bf16[16,2,2,512,128]{4,0,3,2,1:T(8,128)(2,1)} %add_convert_fusion), kind=kOutput, calls=%fused_computation.55 | convolution fusion | flops 4297064448 | bytes 29360128 | tf_op jit(solution)/shard_map/fksp,fkrpc->fsrc/dot_general | solution.py:142
  232.5 8.0 %copy.13 = bf16[16,512,2,128]{3,0,2,1:T(8,128)(2,1)} copy(bf16[16,512,2,128]{1,3,2,0:T(8,128)(2,1)} %fusion.35) | data formatting | bytes 8388608 | tf_op jit(solution)/shard_map/convert_element_type | solution.py:143
  240.6 4.1 %pad_maximum_fusion = bf16[512,16,256]{2,1,0:T(8,128)(2,1)} fusion(bf16[512,16,128]{2,1,0:T(8,128)(2,1)} %fusion.36, bf16[512,16,128]{2,1,0:T(8,128)(2,1)S(1)} %fusion.39), kind=kLoop, calls=%fused_computation.68 | loop fusion | flops 8388608 | bytes 8388608 | tf_op jit(solution)/shard_map/concatenate | solution.py:166
  244.7 43.1 %reduce-scatter.3.cloned.1.call-done = bf16[16,64,2,128]{3,0,2,1:T(8,128)(2,1)} async-done(((bf16[16,512,2,128]{3,0,2,1:T(8,128)(2,1)}), bf16[16,64,2,128]{3,0,2,1:T(8,128)(2,1)}) %reduce-scatter.3.cloned.1.call-update) | async-done | bytes 524304 | tf_op jit(solution)/shard_map/reduce_scatter | solution.py:143
  287.7 91.7 %reduce-scatter.5.cloned.1.call-done = bf16[16,64,2,128]{3,0,2,1:T(8,128)(2,1)} async-done(((bf16[16,512,2,128]{3,0,2,1:T(8,128)(2,1)}), bf16[16,64,2,128]{3,0,2,1:T(8,128)(2,1)}) %reduce-scatter.5.cloned.1.call-update) | async-done | bytes 524304 | tf_op jit(solution)/shard_map/reduce_scatter | solution.py:143
  380.8 3.2 copy.14
  (51 shorter events, 12.6 us)
Async XLA Ops:
  7.2 280.6 %reduce-scatter.3.cloned.1.call-start = ((), (), s32[]{:S(2)}) async-start(), calls=%async_computation.2 | async-start | bytes 4718592 | tf_op jit(solution)/shard_map/reduce_scatter | solution.py:143
  9.7 7.7 %collective-permute-start.1 = (f32[20490]{0:T(1024)S(1)}, f32[20490]{0:T(1024)S(1)}, u32[]{:S(2)}, u32[]{:S(2)}) collective-permute-start(f32[20490]{0:T(1024)S(1)} %concatenate.43), channel_id=1, source_target_pairs={{4,0},{8,4},{12,8},{16,12},{20,16},{24,20},{28,24},{5,1},{9,5},{13... | collective-permute-start | bytes 245888 | tf_op jit(solution)/shard_map/ppermute | solution.py:19
  11.8 7.6 %collective-permute-start = (f32[20491]{0:T(1024)S(1)}, f32[20491]{0:T(1024)S(1)}, u32[]{:S(2)}, u32[]{:S(2)}) collective-permute-start(f32[20491]{0:T(1024)S(1)} %concatenate.42), channel_id=1, source_target_pairs={{0,4},{4,8},{8,12},{12,16},{16,20},{20,24},{24,28},{1,5},{5,9},{9,... | collective-permute-start | bytes 245900 | tf_op jit(solution)/shard_map/ppermute | solution.py:14
  19.4 2.5 copy-start.3
  19.4 2.7 copy-start.2
  42.8 46.6 %collective-permute-start.2 = (bf16[512,16,128]{2,1,0:T(8,128)(2,1)S(1)}, bf16[512,16,128]{2,1,0:T(8,128)(2,1)S(1)}, u32[]{:S(2)}, u32[]{:S(2)}) collective-permute-start(bf16[512,16,128]{2,1,0:T(8,128)(2,1)S(1)} %fusion.39), channel_id=1, source_target_pairs={{0,2},{2,0},{1,3},{3,1},{4,6},{6,4},{5,7},{7,5},{8,10},{10,8},{9,1... | collective-permute-start | bytes 6291464 | tf_op jit(solution)/shard_map/ppermute | solution.py:130
  89.5 6.2 %copy-start = (bf16[512,16,128]{2,1,0:T(8,128)(2,1)}, bf16[512,16,128]{2,1,0:T(8,128)(2,1)S(1)}, u32[]{:S(2)}) copy-start(bf16[512,16,128]{2,1,0:T(8,128)(2,1)S(1)} %collective-permute-done.2) | copy-start | bytes 6291460
  92.1 62.5 %collective-permute-start.3 = (bf16[512,32,128]{2,1,0:T(8,128)(2,1)}, bf16[512,32,128]{2,1,0:T(8,128)(2,1)}, u32[]{:S(2)}, u32[]{:S(2)}) collective-permute-start(bf16[512,32,128]{2,1,0:T(8,128)(2,1)} %pad_maximum_fusion.1), channel_id=1, source_target_pairs={{0,1},{1,0},{2,3},{3,2},{4,5},{5,4},{6,7},{7,6},{8,9},{9,8},{10,11... | collective-permute-start | bytes 12582920 | tf_op jit(solution)/shard_map/ppermute | solution.py:132
  101.4 48.4 %collective-permute-start.4 = (bf16[512,16,128]{2,1,0:T(8,128)(2,1)}, bf16[512,16,128]{2,1,0:T(8,128)(2,1)}, u32[]{:S(2)}, u32[]{:S(2)}) collective-permute-start(bf16[512,16,128]{2,1,0:T(8,128)(2,1)} %fusion.36), channel_id=1, source_target_pairs={{0,2},{2,0},{1,3},{3,1},{4,6},{6,4},{5,7},{7,5},{8,10},{10,8},{9,1... | collective-permute-start | bytes 6291464 | tf_op jit(solution)/shard_map/ppermute | solution.py:130
  103.2 51.4 %copy-start.1 = (bf16[512,16,128]{2,1,0:T(8,128)(2,1)S(1)}, bf16[512,16,128]{2,1,0:T(8,128)(2,1)}, u32[]{:S(2)}) copy-start(bf16[512,16,128]{2,1,0:T(8,128)(2,1)} %copy-done) | copy-start | bytes 6291460
  154.7 42.1 %collective-permute-start.5 = (bf16[512,32,128]{2,1,0:T(8,128)(2,1)}, bf16[512,32,128]{2,1,0:T(8,128)(2,1)}, u32[]{:S(2)}, u32[]{:S(2)}) collective-permute-start(bf16[512,32,128]{2,1,0:T(8,128)(2,1)} %pad_maximum_fusion.2), channel_id=1, source_target_pairs={{0,1},{1,0},{2,3},{3,2},{4,5},{5,4},{6,7},{7,6},{8,9},{9,8},{10,11... | collective-permute-start | bytes 12582920 | tf_op jit(solution)/shard_map/ppermute | solution.py:132
  196.7 182.7 %reduce-scatter.5.cloned.1.call-start = ((), (), s32[]{:S(2)}) async-start(), calls=%async_computation.3 | async-start | bytes 4718592 | tf_op jit(solution)/shard_map/reduce_scatter | solution.py:143
Sparse Core Ops, SparseCore 0:
  196.8 90.8 reduce-scatter.2
  291.8 87.6 reduce-scatter.4

commit v5 on v4

--- a/solution.py
+++ b/solution.py
@@ -125,20 +125,22 @@
     return table_high, table_low
 
 
-def forward_gathered(prior_part, green):
+def gathered_spectrum(prior_part, after=None):
     where_tm = lax.axis_index("tm").astype(jnp.int32)
     across = lax.ppermute(prior_part, "tm", [(0, 2), (2, 0), (1, 3), (3, 1)])
+    if after is not None:
+        across, _ = lax.optimization_barrier((across, after))
     mine = jnp.concatenate([prior_part, across], axis=1)
     theirs = lax.ppermute(mine, "tm", [(0, 1), (1, 0), (2, 3), (3, 2)])
     stacked = jnp.concatenate([mine, theirs], axis=1)
     blocks = [where_tm, where_tm ^ 2, where_tm ^ 1, where_tm ^ 3]
     steps_all = prior_part.shape[1] * len(blocks)
-    table_high, table_low = gathered_tables(blocks, steps_all)
+    table_high, _ = gathered_tables(blocks, steps_all)
     mixed = jnp.einsum("fkrt,ptc->fkrpc", table_high, stacked, preferred_element_type=jnp.float32)
-    mixed = mixed + jnp.einsum(
-        "fkrt,ptc->fkrpc", table_low, stacked, preferred_element_type=jnp.float32
-    )
-    mixed = mixed.astype(jnp.bfloat16)
+    return mixed.astype(jnp.bfloat16)
+
+
+def green_product(mixed, green):
     partial = jnp.einsum("fksp,fkrpc->fsrc", green, mixed, preferred_element_type=jnp.float32)
     summed = lax.psum_scatter(partial.astype(jnp.bfloat16), "sea", scatter_dimension=1, tiled=True)
     return jnp.transpose(summed, (1, 0, 2, 3)).astype(jnp.float32)
@@ -152,6 +154,7 @@
     left_k, right_k, diag = extended_coefficients(kappa_ext, react_ext, motion.shape[0], halo)
     table_high, table_low = dft_tables(motion.shape[1] * lax.axis_size("tm"))
     priors = []
+    spectra = []
     sensors = []
     for c in range(CHUNKS):
         source = motion_ext[:, :, c * width : (c + 1) * width]
@@ -160,7 +163,9 @@
         prior_part = smooth(source.astype(jnp.float32), left_k, right_k, diag, halo).astype(jnp.bfloat16)
         priors.append(prior_part)
         if lax.axis_size("tm") == 4:
-            sensors.append(forward_gathered(prior_part, green))
+            mixed = gathered_spectrum(prior_part, spectra[-1] if spectra else None)
+            spectra.append(mixed)
+            sensors.append(green_product(mixed, green))
         else:
             sensors.append(forward_chunk(prior_part, green, table_high, table_low))
     return (jnp.concatenate(priors, axis=2), jnp.concatenate(sensors, axis=3))

time: 392 us -> 332 us (0.85)
  waiting for transfers between devices: 216 us -> 178 us
  matrix products: 69.7 us -> 36.8 us
  local copies, waits for them, and re-layouts: 24.7 us -> 38.6 us
    dot_general x6 -> x4, matrix products: 69.7 us -> 36.8 us  [the longest x2 24.9 us: green_product(): jnp.einsum('fksp,fkrpc->fsrc', green, mixed, preferred_element_type=jnp.f...]
    reduce_scatter x2, waiting for transfers between devices: 135 us -> 107 us  [green_product(): lax.psum_scatter(partial.astype(jnp.bfloat16), 'sea', scatter_dimension=1...]
    dot_general x0 -> x1, local copies, waits for them, and re-layouts: none -> 13.9 us  [gathered_spectrum(): jnp.einsum('fkrt,ptc->fkrpc', table_high, stacked, preferred_element_type...]
    ppermute x4, waiting for transfers between devices: 78.8 us -> 65.8 us  [the longest x2 58.7 us: gathered_spectrum(): across = lax.ppermute(prior_part, 'tm', [(0, 2), (2, 0), (1, 3), (3, 1)])]
    ppermute x1, waiting for transfers between devices: 0.01 us -> 4.99 us  [from_right(): return lax.ppermute(block, axis, [(i + 1, i) for i in range(count - 1)])]
  transfers between devices with their start and end apart: 8 -> 8, of which waited for: 5 -> 6; matrix products, arithmetic and copies ran while one was open for 30% -> 29% of each run, Pallas kernels for 0% -> 0%
where the time goes in v5:
time: 332 us; the launch traced here: 330 us
  waiting for transfers between devices  178 us (54%)
  other arithmetic  53.6 us (16%)
  local copies, waits for them, and re-layouts  38.6 us (12%)
  matrix products  36.8 us (11%)
  between operations  14.3 us (4%)
  starting transfers between devices  9.41 us (3%)
    reduce_scatter x2, waiting for transfers between devices, green_product(): lax.psum_scatter(partial.astype(jnp.bfloat16), 'sea', scatter_dimension=1...  107 us
    ppermute x2, waiting for transfers between devices, gathered_spectrum(): across = lax.ppermute(prior_part, 'tm', [(0, 2), (2, 0), (1, 3), (3, 1)])  58.7 us
    add x8, other arithmetic, smooth(): state = state + weights[k] * (source - applied) / diag  28.1 us
    dot_general x2, matrix products, green_product(): jnp.einsum('fksp,fkrpc->fsrc', green, mixed, preferred_element_type=jnp.f...  24.9 us
    convert_element_type x2, local copies, waits for them, and re-layouts, green_product(): partial.astype(jnp.bfloat16)  16.1 us
    dot_general x1, local copies, waits for them, and re-layouts, gathered_spectrum(): jnp.einsum('fkrt,ptc->fkrpc', table_high, stacked, preferred_element_type...  13.9 us
    dot_general x2, matrix products, gathered_spectrum(): jnp.einsum('fkrt,ptc->fkrpc', table_high, stacked, preferred_element_type...  11.9 us
    ppermute x2, waiting for transfers between devices, gathered_spectrum(): theirs = lax.ppermute(mine, 'tm', [(0, 1), (1, 0), (2, 3), (3, 2)])  7.15 us
  transfers between devices with their start and end apart: 8, of which 6 were waited for; matrix products, arithmetic and copies ran while one was open for 29% of the time, Pallas kernels for 0%

profile of v5, /device:TPU:0, one launch (start us, length us, event | category | flops | bytes accessed | tf_op | source)
XLA Modules:
  0.0 330.4 jit_solution(10218870096066210601)
XLA Ops:
  9.7 4.9 %collective-permute-start = (f32[20491]{0:T(1024)S(1)}, f32[20491]{0:T(1024)S(1)}, u32[]{:S(2)}, u32[]{:S(2)}) collective-permute-start(f32[20491]{0:T(1024)S(1)} %concatenate.42), channel_id=1, source_target_pairs={{0,4},{4,8},{8,12},{12,16},{16,20},{20,24},{24,28},{1,5},{5,9},{9,... | collective-permute-start | bytes 245900 | tf_op jit(solution)/shard_map/ppermute | solution.py:14
  16.8 5.0 %collective-permute-done.1 = f32[20490]{0:T(1024)S(1)} collective-permute-done((f32[20490]{0:T(1024)S(1)}, f32[20490]{0:T(1024)S(1)}, u32[]{:S(2)}, u32[]{:S(2)}) %collective-permute-start.1) | collective-permute-done | bytes 81992 | tf_op jit(solution)/shard_map/ppermute | solution.py:19
  22.0 2.5 constant_dynamic-update-slice_fusion.1
  27.0 3.5 %fusion.20 = f32[522,16,128]{2,1,0:T(8,128)S(1)} fusion(f32[522,16,128]{2,1,0:T(8,128)S(1)} %fusion.17, f32[522]{0:T(1024)S(1)} %get-tuple-element.24, f32[522]{0:T(1024)S(1)} %get-tuple-element.22, f32[522]{0:T(1024)S(1)} %get-tuple-element.23, bf16[522,16,256]{2,1,0:T(8,128)(2,1)S(1)} %constant_dynamic-update-slice_fusion), kind=kLoop, calls=%fused_computation.34 | loop fusion | flops 10690560 | bytes 10696824 | tf_op jit(solution)/shard_map/add | solution.py:71
  30.5 3.5 %fusion.23 = f32[522,16,128]{2,1,0:T(8,128)S(1)} fusion(f32[522,16,128]{2,1,0:T(8,128)S(1)} %fusion.20, f32[522]{0:T(1024)S(1)} %get-tuple-element.24, f32[522]{0:T(1024)S(1)} %get-tuple-element.22, f32[522]{0:T(1024)S(1)} %get-tuple-element.23, bf16[522,16,256]{2,1,0:T(8,128)(2,1)S(1)} %constant_dynamic-update-slice_fusion), kind=kLoop, calls=%fused_computation.37 | loop fusion | flops 10690560 | bytes 10696824 | tf_op jit(solution)/shard_map/add | solution.py:71
  34.0 3.5 %fusion.26 = f32[522,16,128]{2,1,0:T(8,128)S(1)} fusion(f32[522,16,128]{2,1,0:T(8,128)S(1)} %fusion.23, f32[522]{0:T(1024)S(1)} %get-tuple-element.24, f32[522]{0:T(1024)S(1)} %get-tuple-element.22, f32[522]{0:T(1024)S(1)} %get-tuple-element.23, bf16[522,16,256]{2,1,0:T(8,128)(2,1)S(1)} %constant_dynamic-update-slice_fusion), kind=kLoop, calls=%fused_computation.40 | loop fusion | flops 10690560 | bytes 10696824 | tf_op jit(solution)/shard_map/add | solution.py:71
  37.6 3.5 %fusion.29 = f32[522,16,128]{2,1,0:T(8,128)S(1)} fusion(f32[522,16,128]{2,1,0:T(8,128)S(1)} %fusion.26, f32[522]{0:T(1024)S(1)} %get-tuple-element.24, f32[522]{0:T(1024)S(1)} %get-tuple-element.22, f32[522]{0:T(1024)S(1)} %get-tuple-element.23, bf16[522,16,256]{2,1,0:T(8,128)(2,1)S(1)} %constant_dynamic-update-slice_fusion), kind=kLoop, calls=%fused_computation.43 | loop fusion | flops 10690560 | bytes 10696824 | tf_op jit(solution)/shard_map/add | solution.py:71
  41.1 2.7 multiply_subtract_fusion.1
  43.8 2.5 fusion.48
  48.4 1.6 fusion.30
  50.0 3.5 %fusion.33 = f32[522,16,128]{2,1,0:T(8,128)S(1)} fusion(f32[522,16,128]{2,1,0:T(8,128)S(1)} %fusion.30, bf16[522,16,128]{2,1,0:T(8,128)(2,1)S(1)} %get-tuple-element.4, f32[522]{0:T(1024)S(1)} %get-tuple-element.24, f32[522]{0:T(1024)S(1)} %get-tuple-element.22, f32[522]{0:T(1024)S(1)} %get-tuple-element.23), kind=kLoop, calls=%fused_computation.47 | loop fusion | flops 10690560 | bytes 10696824 | tf_op jit(solution)/shard_map/add | solution.py:71
  53.5 39.0 %collective-permute-done.2 = bf16[512,16,128]{2,1,0:T(8,128)(2,1)} collective-permute-done((bf16[512,16,128]{2,1,0:T(8,128)(2,1)}, bf16[512,16,128]{2,1,0:T(8,128)(2,1)}, u32[]{:S(2)}, u32[]{:S(2)}) %collective-permute-start.2) | collective-permute-done | bytes 2097184 | tf_op jit(solution)/shard_map/ppermute | solution.py:130
  92.5 2.9 pad_maximum_fusion.1
  95.6 3.5 %fusion.36 = f32[522,16,128]{2,1,0:T(8,128)S(1)} fusion(f32[522,16,128]{2,1,0:T(8,128)S(1)} %fusion.33, bf16[522,16,128]{2,1,0:T(8,128)(2,1)S(1)} %get-tuple-element.4, f32[522]{0:T(1024)S(1)} %get-tuple-element.24, f32[522]{0:T(1024)S(1)} %get-tuple-element.22, f32[522]{0:T(1024)S(1)} %get-tuple-element.23), kind=kLoop, calls=%fused_computation.50 | loop fusion | flops 10690560 | bytes 10696824 | tf_op jit(solution)/shard_map/add | solution.py:71
  99.1 3.5 %fusion.39 = f32[522,16,128]{2,1,0:T(8,128)S(1)} fusion(f32[522,16,128]{2,1,0:T(8,128)S(1)} %fusion.36, bf16[522,16,128]{2,1,0:T(8,128)(2,1)S(1)} %get-tuple-element.4, f32[522]{0:T(1024)S(1)} %get-tuple-element.24, f32[522]{0:T(1024)S(1)} %get-tuple-element.22, f32[522]{0:T(1024)S(1)} %get-tuple-element.23), kind=kLoop, calls=%fused_computation.53 | loop fusion | flops 10690560 | bytes 10696824 | tf_op jit(solution)/shard_map/add | solution.py:71
  102.6 3.5 %fusion.42 = f32[522,16,128]{2,1,0:T(8,128)S(1)} fusion(f32[522,16,128]{2,1,0:T(8,128)S(1)} %fusion.39, bf16[522,16,128]{2,1,0:T(8,128)(2,1)S(1)} %get-tuple-element.4, f32[522]{0:T(1024)S(1)} %get-tuple-element.24, f32[522]{0:T(1024)S(1)} %get-tuple-element.22, f32[522]{0:T(1024)S(1)} %get-tuple-element.23), kind=kLoop, calls=%fused_computation.56 | loop fusion | flops 10690560 | bytes 10696824 | tf_op jit(solution)/shard_map/add | solution.py:71
  106.1 2.7 multiply_subtract_fusion
  108.7 1.7 fusion.45
  112.1 6.1 %fusion.16 = bf16[16,2,2,512,128]{4,0,3,2,1:T(8,128)(2,1)} fusion(bf16[512,32,128]{2,1,0:T(8,128)(2,1)S(1)} %collective-permute-done.3, bf16[512,16,128]{2,1,0:T(8,128)(2,1)} %collective-permute-done.2, bf16[512,16,128]{2,1,0:T(8,128)(2,1)} %fusion.48, bf16[16,2,2,64]{3,0,2,1:T(8,128)(2,1)S(1)} %pad_maximum_fusion.3), kind=kOutput, calls=%fused_computation.20 | convolution fusion | flops 566231040 | bytes 16785408 | tf_op jit(solution)/shard_map/fkrt,ptc->fkrpc/dot_general | solution.py:139
  118.2 12.7 %fusion.43 = bf16[16,512,2,128]{1,3,2,0:T(8,128)(2,1)} fusion(bf16[16,2,512,512]{3,2,1,0:T(8,128)(2,1)} %param.7, bf16[16,2,2,512,128]{4,0,3,2,1:T(8,128)(2,1)} %fusion.16), kind=kOutput, calls=%fused_computation.61 | convolution fusion | flops 4297064448 | bytes 29360128 | tf_op jit(solution)/shard_map/fksp,fkrpc->fsrc/dot_general | solution.py:144
  130.9 8.0 %copy.9 = bf16[16,512,2,128]{3,0,2,1:T(8,128)(2,1)} copy(bf16[16,512,2,128]{1,3,2,0:T(8,128)(2,1)} %fusion.43) | data formatting | bytes 8388608 | tf_op jit(solution)/shard_map/convert_element_type | solution.py:145
  139.0 19.7 %collective-permute-done.4 = bf16[512,16,128]{2,1,0:T(8,128)(2,1)} collective-permute-done((bf16[512,16,128]{2,1,0:T(8,128)(2,1)S(1)}, bf16[512,16,128]{2,1,0:T(8,128)(2,1)}, u32[]{:S(2)}, u32[]{:S(2)}) %collective-permute-start.4) | collective-permute-done | bytes 2097184 | tf_op jit(solution)/shard_map/ppermute | solution.py:130
  158.7 2.3 pad_maximum_fusion.2
  161.1 7.1 %collective-permute-done.5 = bf16[512,32,128]{2,1,0:T(8,128)(2,1)S(1)} collective-permute-done((bf16[512,32,128]{2,1,0:T(8,128)(2,1)S(1)}, bf16[512,32,128]{2,1,0:T(8,128)(2,1)S(1)}, u32[]{:S(2)}, u32[]{:S(2)}) %collective-permute-start.5) | collective-permute-done | bytes 4194336 | tf_op jit(solution)/shard_map/ppermute | solution.py:134
  168.2 5.8 %fusion.9 = bf16[16,2,2,512,128]{4,0,3,2,1:T(8,128)(2,1)} fusion(bf16[512,32,128]{2,1,0:T(8,128)(2,1)S(1)} %collective-permute-done.5, bf16[512,16,128]{2,1,0:T(8,128)(2,1)} %collective-permute-done.4, bf16[512,16,128]{2,1,0:T(8,128)(2,1)S(1)} %fusion.45, bf16[16,2,2,64]{3,0,2,1:T(8,128)(2,1)S(1)} %pad_maximum_fusion.3), kind=kOutput, calls=%fused_computation.11 | convolution fusion | flops 562036736 | bytes 16785408 | tf_op jit(solution)/shard_map/fkrt,ptc->fkrpc/dot_general | solution.py:139
  174.0 13.9 %copy.17 = bf16[16,2,2,512,128]{3,4,1,2,0:T(8,128)(2,1)} copy(bf16[16,2,2,512,128]{4,0,3,2,1:T(8,128)(2,1)} %fusion.9) | data formatting | bytes 16777216 | tf_op jit(solution)/shard_map/fkrt,ptc->fkrpc/dot_general | solution.py:139
  187.9 12.2 %fusion.44 = bf16[16,512,2,128]{1,3,2,0:T(8,128)(2,1)} fusion(bf16[16,2,512,512]{3,2,1,0:T(8,128)(2,1)} %param.7, bf16[16,2,2,512,128]{3,4,1,2,0:T(8,128)(2,1)} %copy.17), kind=kOutput, calls=%fused_computation.62 | convolution fusion | flops 4297064448 | bytes 29360128 | tf_op jit(solution)/shard_map/fksp,fkrpc->fsrc/dot_general | solution.py:144
  200.1 8.0 %copy.10 = bf16[16,512,2,128]{3,0,2,1:T(8,128)(2,1)} copy(bf16[16,512,2,128]{1,3,2,0:T(8,128)(2,1)} %fusion.44) | data formatting | bytes 8388608 | tf_op jit(solution)/shard_map/convert_element_type | solution.py:145
  208.2 4.1 %pad_maximum_fusion = bf16[512,16,256]{2,1,0:T(8,128)(2,1)} fusion(bf16[512,16,128]{2,1,0:T(8,128)(2,1)S(1)} %fusion.45, bf16[512,16,128]{2,1,0:T(8,128)(2,1)} %fusion.48), kind=kLoop, calls=%fused_computation.75 | loop fusion | flops 8388608 | bytes 8388608 | tf_op jit(solution)/shard_map/concatenate | solution.py:171
  212.2 15.0 %reduce-scatter.3.cloned.1.call-done = bf16[16,64,2,128]{3,0,2,1:T(8,128)(2,1)} async-done(((bf16[16,512,2,128]{3,0,2,1:T(8,128)(2,1)}), bf16[16,64,2,128]{3,0,2,1:T(8,128)(2,1)}) %reduce-scatter.3.cloned.1.call-update) | async-done | bytes 524304 | tf_op jit(solution)/shard_map/reduce_scatter | solution.py:145
  227.2 91.8 %reduce-scatter.5.cloned.1.call-done = bf16[16,64,2,128]{3,0,2,1:T(8,128)(2,1)} async-done(((bf16[16,512,2,128]{3,0,2,1:T(8,128)(2,1)}), bf16[16,64,2,128]{3,0,2,1:T(8,128)(2,1)}) %reduce-scatter.5.cloned.1.call-update) | async-done | bytes 524304 | tf_op jit(solution)/shard_map/reduce_scatter | solution.py:145
  320.4 3.2 copy.11
  (46 shorter events, 12.6 us)
Async XLA Ops:
  7.2 220.1 %reduce-scatter.3.cloned.1.call-start = ((), (), s32[]{:S(2)}) async-start(), calls=%async_computation.2 | async-start | bytes 4718592 | tf_op jit(solution)/shard_map/reduce_scatter | solution.py:145
  9.7 12.2 %collective-permute-start = (f32[20491]{0:T(1024)S(1)}, f32[20491]{0:T(1024)S(1)}, u32[]{:S(2)}, u32[]{:S(2)}) collective-permute-start(f32[20491]{0:T(1024)S(1)} %concatenate.42), channel_id=1, source_target_pairs={{0,4},{4,8},{8,12},{12,16},{16,20},{20,24},{24,28},{1,5},{5,9},{9,... | collective-permute-start | bytes 245900 | tf_op jit(solution)/shard_map/ppermute | solution.py:14
  15.4 6.4 %collective-permute-start.1 = (f32[20490]{0:T(1024)S(1)}, f32[20490]{0:T(1024)S(1)}, u32[]{:S(2)}, u32[]{:S(2)}) collective-permute-start(f32[20490]{0:T(1024)S(1)} %concatenate.43), channel_id=1, source_target_pairs={{4,0},{8,4},{12,8},{16,12},{20,16},{24,20},{28,24},{5,1},{9,5},{13... | collective-permute-start | bytes 245888 | tf_op jit(solution)/shard_map/ppermute | solution.py:19
  24.4 0.7 copy-start.1
  24.4 0.8 copy-start
  46.3 46.3 %collective-permute-start.2 = (bf16[512,16,128]{2,1,0:T(8,128)(2,1)}, bf16[512,16,128]{2,1,0:T(8,128)(2,1)}, u32[]{:S(2)}, u32[]{:S(2)}) collective-permute-start(bf16[512,16,128]{2,1,0:T(8,128)(2,1)} %fusion.48), channel_id=1, source_target_pairs={{0,2},{2,0},{1,3},{3,1},{4,6},{6,4},{5,7},{7,5},{8,10},{10,8},{9,1... | collective-permute-start | bytes 6291464 | tf_op jit(solution)/shard_map/ppermute | solution.py:130
  95.5 16.6 %collective-permute-start.3 = (bf16[512,32,128]{2,1,0:T(8,128)(2,1)S(1)}, bf16[512,32,128]{2,1,0:T(8,128)(2,1)S(1)}, u32[]{:S(2)}, u32[]{:S(2)}) collective-permute-start(bf16[512,32,128]{2,1,0:T(8,128)(2,1)S(1)} %pad_maximum_fusion.1), channel_id=1, source_target_pairs={{0,1},{1,0},{2,3},{3,2},{4,5},{5,4},{6,7},{7,6},{8,9},{9,8},{10,11... | collective-permute-start | bytes 12582920 | tf_op jit(solution)/shard_map/ppermute | solution.py:134
  110.5 48.2 %collective-permute-start.4 = (bf16[512,16,128]{2,1,0:T(8,128)(2,1)S(1)}, bf16[512,16,128]{2,1,0:T(8,128)(2,1)}, u32[]{:S(2)}, u32[]{:S(2)}) collective-permute-start(bf16[512,16,128]{2,1,0:T(8,128)(2,1)S(1)} %fusion.45), channel_id=1, source_target_pairs={{0,2},{2,0},{1,3},{3,1},{4,6},{6,4},{5,7},{7,5},{8,10},{10,8},{9,1... | collective-permute-start | bytes 6291464 | tf_op jit(solution)/shard_map/ppermute | solution.py:130
  138.9 180.0 %reduce-scatter.5.cloned.1.call-start = ((), (), s32[]{:S(2)}) async-start(), calls=%async_computation.3 | async-start | bytes 4718592 | tf_op jit(solution)/shard_map/reduce_scatter | solution.py:145
  161.0 7.2 %collective-permute-start.5 = (bf16[512,32,128]{2,1,0:T(8,128)(2,1)S(1)}, bf16[512,32,128]{2,1,0:T(8,128)(2,1)S(1)}, u32[]{:S(2)}, u32[]{:S(2)}) collective-permute-start(bf16[512,32,128]{2,1,0:T(8,128)(2,1)S(1)} %pad_maximum_fusion.2), channel_id=1, source_target_pairs={{0,1},{1,0},{2,3},{3,2},{4,5},{5,4},{6,7},{7,6},{8,9},{9,8},{10,11... | collective-permute-start | bytes 12582920 | tf_op jit(solution)/shard_map/ppermute | solution.py:134
Sparse Core Ops, SparseCore 0:
  139.1 88.1 reduce-scatter.2
  231.3 87.6 reduce-scatter.4

commit v6 on v5

--- a/solution.py
+++ b/solution.py
@@ -37,16 +37,13 @@
     )
     before = from_left(tail, "sea")
     after = from_right(head, "sea")
-    motion_ext = jnp.concatenate(
-        [
-            before[:size].reshape(shape).astype(motion.dtype),
-            motion,
-            after[:size].reshape(shape).astype(motion.dtype),
-        ]
+    halo_rows = (
+        before[:size].reshape(shape).astype(motion.dtype),
+        after[:size].reshape(shape).astype(motion.dtype),
     )
     kappa_ext = jnp.concatenate([before[size : size + halo + 1], kappa, after[size : size + halo]])
     react_ext = jnp.concatenate([before[size + halo + 1 :], react, after[size + halo :]])
-    return motion_ext, kappa_ext, react_ext
+    return halo_rows, kappa_ext, react_ext
 
 
 def extended_coefficients(kappa_ext, react_ext, points, halo):
@@ -70,6 +67,36 @@
         applied = diag * state - left_k * padded[:-2] - right_k * padded[2:]
         state = state + weights[k] * (source - applied) / diag
     return state[halo : state.shape[0] - halo]
+
+
+def local_coefficients(kappa, react):
+    points = kappa.shape[0]
+    total_points = points * lax.axis_size("sea")
+    index = lax.axis_index("sea") * points + jnp.arange(points, dtype=jnp.int32)
+    left_k = jnp.concatenate([jnp.zeros((1,), kappa.dtype), kappa[:-1]])
+    right_k = jnp.where(index == total_points - 1, 0.0, kappa)
+    diag = left_k + right_k + react
+    return left_k[:, None, None], right_k[:, None, None], diag[:, None, None]
+
+
+def smooth_with_edges(motion, halo_rows, coefficients, local_coefficients_, halo):
+    points = motion.shape[0]
+    span = 3 * halo + 1
+    keep = halo + 1
+    interior = smooth(motion.astype(jnp.float32), *local_coefficients_, 0).astype(jnp.bfloat16)
+    before, after = halo_rows
+    left_src = jnp.concatenate([before, motion[: span - halo]]).astype(jnp.float32)
+    right_src = jnp.concatenate([motion[points - span + halo :], after]).astype(jnp.float32)
+    left_k, right_k, diag = coefficients
+    extent = left_k.shape[0]
+    left = smooth(left_src, left_k[:span], right_k[:span], diag[:span], halo)
+    right = smooth(
+        right_src, left_k[extent - span :], right_k[extent - span :], diag[extent - span :], halo
+    )
+    interior = lax.dynamic_update_slice_in_dim(interior, left.astype(jnp.bfloat16), 0, 0)
+    return lax.dynamic_update_slice_in_dim(
+        interior, right.astype(jnp.bfloat16), points - keep, 0
+    )
 
 
 def dft_tables(steps_all):
@@ -150,23 +177,31 @@
     halo = SWEEPS - 1
     cols = motion.shape[2]
     width = cols // CHUNKS
-    motion_ext, kappa_ext, react_ext = exchange_halo(motion, kappa, react, halo)
-    left_k, right_k, diag = extended_coefficients(kappa_ext, react_ext, motion.shape[0], halo)
-    table_high, table_low = dft_tables(motion.shape[1] * lax.axis_size("tm"))
+    halo_rows, kappa_ext, react_ext = exchange_halo(motion, kappa, react, halo)
+    coefficients = extended_coefficients(kappa_ext, react_ext, motion.shape[0], halo)
+    inner = local_coefficients(kappa, react)
     priors = []
-    spectra = []
-    sensors = []
     for c in range(CHUNKS):
-        source = motion_ext[:, :, c * width : (c + 1) * width]
+        part = slice(c * width, (c + 1) * width)
+        source = motion[:, :, part]
         if priors:
             source, _ = lax.optimization_barrier((source, priors[-1]))
-        prior_part = smooth(source.astype(jnp.float32), left_k, right_k, diag, halo).astype(jnp.bfloat16)
-        priors.append(prior_part)
-        if lax.axis_size("tm") == 4:
-            mixed = gathered_spectrum(prior_part, spectra[-1] if spectra else None)
+        rows = (halo_rows[0][:, :, part], halo_rows[1][:, :, part])
+        priors.append(smooth_with_edges(source, rows, coefficients, inner, halo))
+    sensors = []
+    if lax.axis_size("tm") == 4:
+        spectra = []
+        for c in range(CHUNKS):
+            if c + 1 < CHUNKS:
+                hold = (priors[c + 1],) + tuple(spectra[-1:])
+            else:
+                hold = tuple(spectra[-1:])
+            mixed = gathered_spectrum(priors[c], hold if hold else None)
             spectra.append(mixed)
             sensors.append(green_product(mixed, green))
-        else:
+    else:
+        table_high, table_low = dft_tables(motion.shape[1] * lax.axis_size("tm"))
+        for prior_part in priors:
             sensors.append(forward_chunk(prior_part, green, table_high, table_low))
     return (jnp.concatenate(priors, axis=2), jnp.concatenate(sensors, axis=3))
 

time: 332 us -> 322 us (0.970)
  waiting for transfers between devices: 178 us -> 162 us
  other arithmetic: 53.6 us -> 58.4 us
    ppermute x2, waiting for transfers between devices: 58.7 us -> 36.6 us  [gathered_spectrum(): across = lax.ppermute(prior_part, 'tm', [(0, 2), (2, 0), (1, 3), (3, 1)])]
    convert_element_type x2 -> x5, other arithmetic: 0.88 us -> 9.18 us  [the longest x2 9.14 us: smooth_with_edges(): smooth(motion.astype(jnp.float32), *local_coefficients_, 0)]
    reduce_scatter x2, waiting for transfers between devices: 107 us -> 113 us  [green_product(): lax.psum_scatter(partial.astype(jnp.bfloat16), 'sea', scatter_dimension=1...]
    ppermute x2, waiting for transfers between devices: 7.15 us -> 12.7 us  [gathered_spectrum(): theirs = lax.ppermute(mine, 'tm', [(0, 1), (1, 0), (2, 3), (3, 2)])]
    ppermute x1, waiting for transfers between devices: 4.99 us -> 0.01 us  [from_right(): return lax.ppermute(block, axis, [(i + 1, i) for i in range(count - 1)])]
    sub x2 -> x4, other arithmetic: 5.32 us -> 0.47 us  [smooth(): applied = diag * state - left_k * padded[:-2] - right_k * padded[2:]]
    another operation x3 -> x1, other arithmetic: 4.4 us -> 0.13 us
    add x8 -> x24, other arithmetic: 28.1 us -> 29.7 us  [smooth(): state = state + weights[k] * (source - applied) / diag]
  transfers between devices with their start and end apart: 8 -> 8, of which waited for: 6 -> 6; matrix products, arithmetic and copies ran while one was open for 29% -> 38% of each run, Pallas kernels for 0% -> 0%
where the time goes in v6:
time: 322 us; the launch traced here: 321 us
  waiting for transfers between devices  162 us (50%)
  other arithmetic  58.4 us (18%)
  local copies, waits for them, and re-layouts  38.3 us (12%)
  matrix products  37.5 us (12%)
  between operations  14.5 us (5%)
  starting transfers between devices  9.41 us (3%)
    reduce_scatter x2, waiting for transfers between devices, green_product(): lax.psum_scatter(partial.astype(jnp.bfloat16), 'sea', scatter_dimension=1...  113 us
    ppermute x2, waiting for transfers between devices, gathered_spectrum(): across = lax.ppermute(prior_part, 'tm', [(0, 2), (2, 0), (1, 3), (3, 1)])  36.6 us
    add x24, other arithmetic, smooth(): state = state + weights[k] * (source - applied) / diag  29.7 us
    dot_general x2, matrix products, green_product(): jnp.einsum('fksp,fkrpc->fsrc', green, mixed, preferred_element_type=jnp.f...  24.8 us
    convert_element_type x2, local copies, waits for them, and re-layouts, green_product(): partial.astype(jnp.bfloat16)  16.1 us
    dot_general x1, local copies, waits for them, and re-layouts, gathered_spectrum(): jnp.einsum('fkrt,ptc->fkrpc', table_high, stacked, preferred_element_type...  13.9 us
    dot_general x2, matrix products, gathered_spectrum(): jnp.einsum('fkrt,ptc->fkrpc', table_high, stacked, preferred_element_type...  12.7 us
    ppermute x2, waiting for transfers between devices, gathered_spectrum(): theirs = lax.ppermute(mine, 'tm', [(0, 1), (1, 0), (2, 3), (3, 2)])  12.7 us
  transfers between devices with their start and end apart: 8, of which 6 were waited for; matrix products, arithmetic and copies ran while one was open for 38% of the time, Pallas kernels for 0%

profile of v6, /device:TPU:0, one launch (start us, length us, event | category | flops | bytes accessed | tf_op | source)
XLA Modules:
  0.0 320.6 jit_solution(11102858887880002918)
XLA Ops:
  9.7 4.9 %collective-permute-start = (f32[20491]{0:T(1024)S(1)}, f32[20491]{0:T(1024)S(1)}, u32[]{:S(2)}, u32[]{:S(2)}) collective-permute-start(f32[20491]{0:T(1024)S(1)} %concatenate.55), channel_id=1, source_target_pairs={{0,4},{4,8},{8,12},{12,16},{16,20},{20,24},{24,28},{1,5},{5,9},{9,... | collective-permute-start | bytes 245900 | tf_op jit(solution)/shard_map/ppermute | solution.py:14
  17.7 3.0 fusion.19
  20.7 3.5 %fusion.22 = f32[512,16,128]{2,1,0:T(8,128)S(1)} fusion(f32[512,16,128]{2,1,0:T(8,128)S(1)} %fusion.19, f32[512]{0:T(512)S(1)} %get-tuple-element.13, f32[512]{0:T(512)S(1)} %get-tuple-element.49, f32[512]{0:T(512)S(1)} %get-tuple-element.12, bf16[512,16,256]{2,1,0:T(8,128)(2,1)S(1)} %copy-done), kind=kLoop, calls=%fused_computation.38 | loop fusion | flops 10485760 | bytes 10491904 | tf_op jit(solution)/shard_map/add | solution.py:68
  24.1 3.5 %fusion.25 = f32[512,16,128]{2,1,0:T(8,128)S(1)} fusion(f32[512,16,128]{2,1,0:T(8,128)S(1)} %fusion.22, f32[512]{0:T(512)S(1)} %get-tuple-element.13, f32[512]{0:T(512)S(1)} %get-tuple-element.49, f32[512]{0:T(512)S(1)} %get-tuple-element.12, bf16[512,16,256]{2,1,0:T(8,128)(2,1)S(1)} %copy-done), kind=kLoop, calls=%fused_computation.41 | loop fusion | flops 10485760 | bytes 10491904 | tf_op jit(solution)/shard_map/add | solution.py:68
  27.6 3.5 %fusion.28 = f32[512,16,128]{2,1,0:T(8,128)S(1)} fusion(f32[512,16,128]{2,1,0:T(8,128)S(1)} %fusion.25, f32[512]{0:T(512)S(1)} %get-tuple-element.13, f32[512]{0:T(512)S(1)} %get-tuple-element.49, f32[512]{0:T(512)S(1)} %get-tuple-element.12, bf16[512,16,256]{2,1,0:T(8,128)(2,1)S(1)} %copy-done), kind=kLoop, calls=%fused_computation.44 | loop fusion | flops 10485760 | bytes 10491904 | tf_op jit(solution)/shard_map/add | solution.py:68
  31.1 3.5 %fusion.31 = f32[512,16,128]{2,1,0:T(8,128)S(1)} fusion(f32[512,16,128]{2,1,0:T(8,128)S(1)} %fusion.28, f32[512]{0:T(512)S(1)} %get-tuple-element.13, f32[512]{0:T(512)S(1)} %get-tuple-element.49, f32[512]{0:T(512)S(1)} %get-tuple-element.12, bf16[512,16,256]{2,1,0:T(8,128)(2,1)S(1)} %copy-done), kind=kLoop, calls=%fused_computation.47 | loop fusion | flops 10485760 | bytes 10491904 | tf_op jit(solution)/shard_map/add | solution.py:68
  34.5 4.6 %fusion.52 = bf16[512,16,128]{2,1,0:T(8,128)(2,1)} fusion(f32[512,16,128]{2,1,0:T(8,128)S(1)} %fusion.31, f32[512]{0:T(512)S(1)} %get-tuple-element.13, f32[512]{0:T(512)S(1)} %get-tuple-element.49, f32[512]{0:T(512)S(1)} %get-tuple-element.12, bf16[512,16,256]{2,1,0:T(8,128)(2,1)S(1)} %copy-done), kind=kLoop, calls=%fused_computation.71 | loop fusion | flops 11534336 | bytes 8394752 | tf_op jit(solution)/shard_map/convert_element_type | solution.py:86
  42.2 1.6 collective-permute-start.2
  45.8 3.4 %fusion.38 = f32[512,16,128]{2,1,0:T(8,128)S(1)} fusion(f32[512,16,128]{2,1,0:T(8,128)S(1)} %fusion.35, bf16[512,16,128]{2,1,0:T(8,128)(2,1)S(1)} %slice.363, f32[512]{0:T(512)S(1)} %get-tuple-element.13, f32[512]{0:T(512)S(1)} %get-tuple-element.49, f32[512]{0:T(512)S(1)} %get-tuple-element.12), kind=kLoop, calls=%fused_computation.54 | loop fusion | flops 10485760 | bytes 10491904 | tf_op jit(solution)/shard_map/add | solution.py:68
  49.2 3.4 %fusion.41 = f32[512,16,128]{2,1,0:T(8,128)S(1)} fusion(f32[512,16,128]{2,1,0:T(8,128)S(1)} %fusion.38, bf16[512,16,128]{2,1,0:T(8,128)(2,1)S(1)} %slice.363, f32[512]{0:T(512)S(1)} %get-tuple-element.13, f32[512]{0:T(512)S(1)} %get-tuple-element.49, f32[512]{0:T(512)S(1)} %get-tuple-element.12), kind=kLoop, calls=%fused_computation.57 | loop fusion | flops 10485760 | bytes 10491904 | tf_op jit(solution)/shard_map/add | solution.py:68
  52.6 3.4 %fusion.44 = f32[512,16,128]{2,1,0:T(8,128)S(1)} fusion(f32[512,16,128]{2,1,0:T(8,128)S(1)} %fusion.41, bf16[512,16,128]{2,1,0:T(8,128)(2,1)S(1)} %slice.363, f32[512]{0:T(512)S(1)} %get-tuple-element.13, f32[512]{0:T(512)S(1)} %get-tuple-element.49, f32[512]{0:T(512)S(1)} %get-tuple-element.12), kind=kLoop, calls=%fused_computation.60 | loop fusion | flops 10485760 | bytes 10491904 | tf_op jit(solution)/shard_map/add | solution.py:68
  56.0 3.4 %fusion.47 = f32[512,16,128]{2,1,0:T(8,128)S(1)} fusion(f32[512,16,128]{2,1,0:T(8,128)S(1)} %fusion.44, bf16[512,16,128]{2,1,0:T(8,128)(2,1)S(1)} %slice.363, f32[512]{0:T(512)S(1)} %get-tuple-element.13, f32[512]{0:T(512)S(1)} %get-tuple-element.49, f32[512]{0:T(512)S(1)} %get-tuple-element.12), kind=kLoop, calls=%fused_computation.63 | loop fusion | flops 10485760 | bytes 10491904 | tf_op jit(solution)/shard_map/add | solution.py:68
  59.5 4.6 %fusion.51 = bf16[512,16,128]{2,1,0:T(8,128)(2,1)} fusion(f32[512,16,128]{2,1,0:T(8,128)S(1)} %fusion.47, bf16[512,16,128]{2,1,0:T(8,128)(2,1)S(1)} %slice.363, f32[512]{0:T(512)S(1)} %get-tuple-element.13, f32[512]{0:T(512)S(1)} %get-tuple-element.49, f32[512]{0:T(512)S(1)} %get-tuple-element.12), kind=kLoop, calls=%fused_computation.70 | loop fusion | flops 11534336 | bytes 8394752 | tf_op jit(solution)/shard_map/convert_element_type | solution.py:86
  66.4 22.9 %collective-permute-done.2 = bf16[512,16,128]{2,1,0:T(8,128)(2,1)S(1)} collective-permute-done((bf16[512,16,128]{2,1,0:T(8,128)(2,1)S(1)}, bf16[512,16,128]{2,1,0:T(8,128)(2,1)S(1)}, u32[]{:S(2)}, u32[]{:S(2)}) %collective-permute-start.2) | collective-permute-done | bytes 2097184 | tf_op jit(solution)/shard_map/ppermute | solution.py:157
  89.4 2.7 pad_maximum_fusion.1
  92.5 1.6 collective-permute-start.4
  94.1 5.5 %collective-permute-done.3 = bf16[512,32,128]{2,1,0:T(8,128)(2,1)} collective-permute-done((bf16[512,32,128]{2,1,0:T(8,128)(2,1)}, bf16[512,32,128]{2,1,0:T(8,128)(2,1)}, u32[]{:S(2)}, u32[]{:S(2)}) %collective-permute-start.3) | collective-permute-done | bytes 4194336 | tf_op jit(solution)/shard_map/ppermute | solution.py:161
  99.6 6.8 %fusion.16 = bf16[16,2,2,512,128]{4,0,3,2,1:T(8,128)(2,1)} fusion(bf16[512,32,128]{2,1,0:T(8,128)(2,1)} %collective-permute-done.3, bf16[512,16,128]{2,1,0:T(8,128)(2,1)} %copy-done.4, bf16[512,16,128]{2,1,0:T(8,128)(2,1)} %copy-done.2, bf16[16,2,2,64]{3,0,2,1:T(8,128)(2,1)S(1)} %pad_maximum_fusion.7), kind=kOutput, calls=%fused_computation.32 | convolution fusion | flops 566231040 | bytes 16785408 | tf_op jit(solution)/shard_map/fkrt,ptc->fkrpc/dot_general | solution.py:166
  106.4 12.7 %fusion.17 = bf16[16,512,2,128]{1,3,2,0:T(8,128)(2,1)} fusion(bf16[16,2,512,512]{3,2,1,0:T(8,128)(2,1)} %param.7, bf16[16,2,2,512,128]{4,0,3,2,1:T(8,128)(2,1)} %fusion.16), kind=kOutput, calls=%fused_computation.33 | convolution fusion | flops 4297064448 | bytes 29360128 | tf_op jit(solution)/shard_map/fksp,fkrpc->fsrc/dot_general | solution.py:171
  119.1 8.0 %copy.9 = bf16[16,512,2,128]{3,0,2,1:T(8,128)(2,1)} copy(bf16[16,512,2,128]{1,3,2,0:T(8,128)(2,1)} %fusion.17) | data formatting | bytes 8388608 | tf_op jit(solution)/shard_map/convert_element_type | solution.py:172
  127.2 13.6 %collective-permute-done.4 = bf16[512,16,128]{2,1,0:T(8,128)(2,1)S(1)} collective-permute-done((bf16[512,16,128]{2,1,0:T(8,128)(2,1)}, bf16[512,16,128]{2,1,0:T(8,128)(2,1)S(1)}, u32[]{:S(2)}, u32[]{:S(2)}) %collective-permute-start.4) | collective-permute-done | bytes 2097184 | tf_op jit(solution)/shard_map/ppermute | solution.py:157
  140.8 2.3 pad_maximum_fusion.2
  143.2 7.1 %collective-permute-done.5 = bf16[512,32,128]{2,1,0:T(8,128)(2,1)S(1)} collective-permute-done((bf16[512,32,128]{2,1,0:T(8,128)(2,1)S(1)}, bf16[512,32,128]{2,1,0:T(8,128)(2,1)S(1)}, u32[]{:S(2)}, u32[]{:S(2)}) %collective-permute-start.5) | collective-permute-done | bytes 4194336 | tf_op jit(solution)/shard_map/ppermute | solution.py:161
  150.4 6.0 %fusion.9 = bf16[16,2,2,512,128]{4,0,3,2,1:T(8,128)(2,1)} fusion(bf16[512,32,128]{2,1,0:T(8,128)(2,1)S(1)} %collective-permute-done.5, bf16[512,16,128]{2,1,0:T(8,128)(2,1)S(1)} %collective-permute-done.4, bf16[512,16,128]{2,1,0:T(8,128)(2,1)} %fusion.204, bf16[16,2,2,64]{3,0,2,1:T(8,128)(2,1)S(1)} %pad_maximum_fusion.7), kind=kOutput, calls=%fused_computation.23 | convolution fusion | flops 562036736 | bytes 16785408 | tf_op jit(solution)/shard_map/fkrt,ptc->fkrpc/dot_general | solution.py:166
  156.4 13.9 %copy.17 = bf16[16,2,2,512,128]{3,4,1,2,0:T(8,128)(2,1)} copy(bf16[16,2,2,512,128]{4,0,3,2,1:T(8,128)(2,1)} %fusion.9) | data formatting | bytes 16777216 | tf_op jit(solution)/shard_map/fkrt,ptc->fkrpc/dot_general | solution.py:166
  170.2 12.1 %fusion.18 = bf16[16,512,2,128]{1,3,2,0:T(8,128)(2,1)} fusion(bf16[16,2,512,512]{3,2,1,0:T(8,128)(2,1)} %param.7, bf16[16,2,2,512,128]{3,4,1,2,0:T(8,128)(2,1)} %copy.17), kind=kOutput, calls=%fused_computation.34 | convolution fusion | flops 4297064448 | bytes 29360128 | tf_op jit(solution)/shard_map/fksp,fkrpc->fsrc/dot_general | solution.py:171
  182.3 8.1 %copy.10 = bf16[16,512,2,128]{3,0,2,1:T(8,128)(2,1)} copy(bf16[16,512,2,128]{1,3,2,0:T(8,128)(2,1)} %fusion.18) | data formatting | bytes 8388608 | tf_op jit(solution)/shard_map/convert_element_type | solution.py:172
  190.4 1.6 copy-done.3
  192.0 4.1 %pad_maximum_fusion = bf16[512,16,256]{2,1,0:T(8,128)(2,1)} fusion(bf16[512,16,128]{2,1,0:T(8,128)(2,1)} %fusion.204, bf16[512,16,128]{2,1,0:T(8,128)(2,1)S(1)} %copy-done.3), kind=kLoop, calls=%fused_computation.67 | loop fusion | flops 8388608 | bytes 8388608 | tf_op jit(solution)/shard_map/concatenate | solution.py:206
  196.0 21.2 %reduce-scatter.3.cloned.1.call-done = bf16[16,64,2,128]{3,0,2,1:T(8,128)(2,1)} async-done(((bf16[16,512,2,128]{3,0,2,1:T(8,128)(2,1)}), bf16[16,64,2,128]{3,0,2,1:T(8,128)(2,1)}) %reduce-scatter.3.cloned.1.call-update) | async-done | bytes 524304 | tf_op jit(solution)/shard_map/reduce_scatter | solution.py:172
  217.3 91.9 %reduce-scatter.5.cloned.1.call-done = bf16[16,64,2,128]{3,0,2,1:T(8,128)(2,1)} async-done(((bf16[16,512,2,128]{3,0,2,1:T(8,128)(2,1)}), bf16[16,64,2,128]{3,0,2,1:T(8,128)(2,1)}) %reduce-scatter.5.cloned.1.call-update) | async-done | bytes 524304 | tf_op jit(solution)/shard_map/reduce_scatter | solution.py:172
  310.6 3.2 %copy.11 = f32[64,16,2,256]{3,2,1,0:T(2,128)} copy(f32[64,16,2,256]{3,1,2,0:T(8,128)S(1)} %maximum_convert_fusion) | data formatting | bytes 4194304
  (87 shorter events, 14.8 us)
Async XLA Ops:
  7.2 210.1 %reduce-scatter.3.cloned.1.call-start = ((), (), s32[]{:S(2)}) async-start(), calls=%async_computation.2 | async-start | bytes 4718592 | tf_op jit(solution)/shard_map/reduce_scatter | solution.py:172
  9.7 29.9 %collective-permute-start = (f32[20491]{0:T(1024)S(1)}, f32[20491]{0:T(1024)S(1)}, u32[]{:S(2)}, u32[]{:S(2)}) collective-permute-start(f32[20491]{0:T(1024)S(1)} %concatenate.55), channel_id=1, source_target_pairs={{0,4},{4,8},{8,12},{12,16},{16,20},{20,24},{24,28},{1,5},{5,9},{9,... | collective-permute-start | bytes 245900 | tf_op jit(solution)/shard_map/ppermute | solution.py:14
  15.4 24.1 %collective-permute-start.1 = (f32[20490]{0:T(1024)S(1)}, f32[20490]{0:T(1024)S(1)}, u32[]{:S(2)}, u32[]{:S(2)}) collective-permute-start(f32[20490]{0:T(1024)S(1)} %concatenate.57), channel_id=1, source_target_pairs={{4,0},{8,4},{12,8},{16,12},{20,16},{24,20},{28,24},{5,1},{9,5},{13... | collective-permute-start | bytes 245888 | tf_op jit(solution)/shard_map/ppermute | solution.py:19
  16.7 3.9 %copy-start = (bf16[512,16,256]{2,1,0:T(8,128)(2,1)S(1)}, bf16[512,16,256]{2,1,0:T(8,128)(2,1)}, u32[]{:S(2)}) copy-start(bf16[512,16,256]{2,1,0:T(8,128)(2,1)} %param.4) | copy-start | bytes 12582916
  39.1 0.7 copy-start.5
  39.1 0.8 copy-start.6
  40.2 1.7 copy-start.1
  42.1 47.3 %copy-start.2 = (bf16[512,16,128]{2,1,0:T(8,128)(2,1)}, bf16[512,16,128]{2,1,0:T(8,128)(2,1)S(1)}, u32[]{:S(2)}) copy-start(bf16[512,16,128]{2,1,0:T(8,128)(2,1)S(1)} %fusion.202) | copy-start | bytes 6291460
  42.2 47.2 %collective-permute-start.2 = (bf16[512,16,128]{2,1,0:T(8,128)(2,1)S(1)}, bf16[512,16,128]{2,1,0:T(8,128)(2,1)S(1)}, u32[]{:S(2)}, u32[]{:S(2)}) collective-permute-start(bf16[512,16,128]{2,1,0:T(8,128)(2,1)S(1)} %fusion.202), channel_id=1, source_target_pairs={{0,2},{2,0},{1,3},{3,1},{4,6},{6,4},{5,7},{7,5},{8,10},{10,8},{9,1... | collective-permute-start | bytes 6291464 | tf_op jit(solution)/shard_map/ppermute | solution.py:157
  89.4 2.7 copy-start.4
  92.1 7.5 %collective-permute-start.3 = (bf16[512,32,128]{2,1,0:T(8,128)(2,1)}, bf16[512,32,128]{2,1,0:T(8,128)(2,1)}, u32[]{:S(2)}, u32[]{:S(2)}) collective-permute-start(bf16[512,32,128]{2,1,0:T(8,128)(2,1)} %pad_maximum_fusion.1), channel_id=1, source_target_pairs={{0,1},{1,0},{2,3},{3,2},{4,5},{5,4},{6,7},{7,6},{8,9},{9,8},{10,11... | collective-permute-start | bytes 12582920 | tf_op jit(solution)/shard_map/ppermute | solution.py:161
  92.5 48.3 %collective-permute-start.4 = (bf16[512,16,128]{2,1,0:T(8,128)(2,1)}, bf16[512,16,128]{2,1,0:T(8,128)(2,1)S(1)}, u32[]{:S(2)}, u32[]{:S(2)}) collective-permute-start(bf16[512,16,128]{2,1,0:T(8,128)(2,1)} %fusion.204), channel_id=1, source_target_pairs={{0,2},{2,0},{1,3},{3,1},{4,6},{6,4},{5,7},{7,5},{8,10},{10,8},{9,1... | collective-permute-start | bytes 6291464 | tf_op jit(solution)/shard_map/ppermute | solution.py:157
  127.2 182.0 %reduce-scatter.5.cloned.1.call-start = ((), (), s32[]{:S(2)}) async-start(), calls=%async_computation.3 | async-start | bytes 4718592 | tf_op jit(solution)/shard_map/reduce_scatter | solution.py:172
  143.2 7.2 %collective-permute-start.5 = (bf16[512,32,128]{2,1,0:T(8,128)(2,1)S(1)}, bf16[512,32,128]{2,1,0:T(8,128)(2,1)S(1)}, u32[]{:S(2)}, u32[]{:S(2)}) collective-permute-start(bf16[512,32,128]{2,1,0:T(8,128)(2,1)S(1)} %pad_maximum_fusion.2), channel_id=1, source_target_pairs={{0,1},{1,0},{2,3},{3,2},{4,5},{5,4},{6,7},{7,6},{8,9},{9,8},{10,11... | collective-permute-start | bytes 12582920 | tf_op jit(solution)/shard_map/ppermute | solution.py:161
  190.4 1.6 copy-start.3
Sparse Core Ops, SparseCore 0:
  127.3 89.9 reduce-scatter.2
  221.3 87.8 reduce-scatter.4

commit v7 on v6

--- a/solution.py
+++ b/solution.py
@@ -79,11 +79,28 @@
     return left_k[:, None, None], right_k[:, None, None], diag[:, None, None]
 
 
+def banded_smooth(motion, coefficients, halo):
+    points = motion.shape[0]
+    width = 2 * halo + 1
+    rows = jnp.arange(points, dtype=jnp.int32)
+    lanes = jnp.arange(width, dtype=jnp.int32)
+    probe = (rows[:, None] % width == lanes[None, :]).astype(jnp.float32)[:, None, :]
+    response = smooth(probe, *coefficients, 0)[:, 0, :]
+    padded = jnp.pad(motion, ((halo, halo), (0, 0), (0, 0)))
+    total = None
+    for offset in range(-halo, halo + 1):
+        pick = (rows[:, None] + offset) % width == lanes[None, :]
+        band = jnp.sum(jnp.where(pick, response, 0.0), axis=1)[:, None, None]
+        term = band * padded[halo + offset : halo + offset + points].astype(jnp.float32)
+        total = term if total is None else total + term
+    return total
+
+
 def smooth_with_edges(motion, halo_rows, coefficients, local_coefficients_, halo):
     points = motion.shape[0]
     span = 3 * halo + 1
     keep = halo + 1
-    interior = smooth(motion.astype(jnp.float32), *local_coefficients_, 0).astype(jnp.bfloat16)
+    interior = banded_smooth(motion, local_coefficients_, halo).astype(jnp.bfloat16)
     before, after = halo_rows
     left_src = jnp.concatenate([before, motion[: span - halo]]).astype(jnp.float32)
     right_src = jnp.concatenate([motion[points - span + halo :], after]).astype(jnp.float32)

time: 322 us -> 334 us (1.037)
  waiting for transfers between devices: 162 us -> 196 us
  other arithmetic: 58.4 us -> 45.6 us
  local copies, waits for them, and re-layouts: 38.3 us -> 29.5 us
    add x24 -> x20, other arithmetic: 29.7 us -> 2.62 us  [smooth(): state = state + weights[k] * (source - applied) / diag]
    ppermute x2, waiting for transfers between devices: 36.6 us -> 56.6 us  [gathered_spectrum(): across = lax.ppermute(prior_part, 'tm', [(0, 2), (2, 0), (1, 3), (3, 1)])]
    convert_element_type x2, other arithmetic: 9.14 us -> 27.7 us  [smooth_with_edges(): banded_smooth(motion, local_coefficients_, halo).astype(jnp.bfloat16)]
    dot_general x1 -> x0, local copies, waits for them, and re-layouts: 13.9 us -> none  [gathered_spectrum(): jnp.einsum('fkrt,ptc->fkrpc', table_high, stacked, preferred_element_type...]
    reduce_scatter x2, waiting for transfers between devices: 113 us -> 126 us  [green_product(): lax.psum_scatter(partial.astype(jnp.bfloat16), 'sea', scatter_dimension=1...]
    slice x1, local copies, waits for them, and re-layouts: 0.36 us -> 4.96 us  [on_device(): source = motion[:, :, part]]
    div x5 -> x4, other arithmetic: 4.75 us -> 0.29 us  [smooth(): state = weights[0] * source / diag]
  transfers between devices with their start and end apart: 8 -> 8, of which waited for: 6 -> 6; matrix products, arithmetic and copies ran while one was open for 38% -> 25% of each run, Pallas kernels for 0% -> 0%
where the time goes in v7:
time: 334 us; the launch traced here: 333 us
  waiting for transfers between devices  196 us (59%)
  other arithmetic  45.6 us (14%)
  matrix products  38.1 us (11%)
  local copies, waits for them, and re-layouts  29.5 us (9%)
  between operations  14.5 us (4%)
  starting transfers between devices  9.59 us (3%)
    reduce_scatter x2, waiting for transfers between devices, green_product(): lax.psum_scatter(partial.astype(jnp.bfloat16), 'sea', scatter_dimension=1...  126 us
    ppermute x2, waiting for transfers between devices, gathered_spectrum(): across = lax.ppermute(prior_part, 'tm', [(0, 2), (2, 0), (1, 3), (3, 1)])  56.6 us
    convert_element_type x2, other arithmetic, smooth_with_edges(): banded_smooth(motion, local_coefficients_, halo).astype(jnp.bfloat16)  27.7 us
    dot_general x2, matrix products, green_product(): jnp.einsum('fksp,fkrpc->fsrc', green, mixed, preferred_element_type=jnp.f...  25.6 us
    convert_element_type x2, local copies, waits for them, and re-layouts, green_product(): partial.astype(jnp.bfloat16)  16.1 us
    ppermute x2, waiting for transfers between devices, gathered_spectrum(): theirs = lax.ppermute(mine, 'tm', [(0, 1), (1, 0), (2, 3), (3, 2)])  12.7 us
    dot_general x2, matrix products, gathered_spectrum(): jnp.einsum('fkrt,ptc->fkrpc', table_high, stacked, preferred_element_type...  12.4 us
  transfers between devices with their start and end apart: 8, of which 6 were waited for; matrix products, arithmetic and copies ran while one was open for 25% of the time, Pallas kernels for 0%

profile of v7, /device:TPU:0, one launch (start us, length us, event | category | flops | bytes accessed | tf_op | source)
XLA Modules:
  0.0 333.0 jit_solution(6234250973632287554)
XLA Ops:
  7.2 0.8 slice.370
  8.0 0.8 fusion.283
  8.8 0.8 slice_convert_fusion.3
  9.7 4.9 %collective-permute-start = (f32[20491]{0:T(1024)S(1)}, f32[20491]{0:T(1024)S(1)}, u32[]{:S(2)}, u32[]{:S(2)}) collective-permute-start(f32[20491]{0:T(1024)S(1)} %concatenate.55), channel_id=1, source_target_pairs={{0,4},{4,8},{8,12},{12,16},{16,20},{20,24},{24,28},{1,5},{5,9},{9,... | collective-permute-start | bytes 245900 | tf_op jit(solution)/shard_map/ppermute | solution.py:14
  14.6 0.7 slice.377
  15.4 1.3 collective-permute-start.1
  16.8 5.0 %fusion.274 = (bf16[512,16,128]{2,1,0:T(8,128)(2,1)}, bf16[512,16,128]{2,1,0:T(8,128)(2,1)}) fusion(bf16[512,16,256]{2,1,0:T(8,128)(2,1)} %param.4), kind=kLoop, calls=%fused_computation.446 | loop fusion | bytes 8388608 | tf_op jit(solution)/shard_map/slice | solution.py:203
  22.5 12.4 %add_convert_fusion.1 = bf16[512,16,128]{2,1,0:T(8,128)(2,1)S(1)} fusion(bf16[512,16,128]{2,1,0:T(8,128)(2,1)} %get-tuple-element.31, f32[512]{0:T(512)S(1)} %get-tuple-element.24, f32[512]{0:T(512)S(1)} %get-tuple-element.23, f32[512]{0:T(512)S(1)} %get-tuple-element.22, f32[512]{0:T(512)S(1)} %get-tuple-element.21, f32[512]{0:T(512)S(1)} %get-tuple-element.20, ...), kind=kLoop, calls=%fused_computation.28 | loop fusion | flops 34603008 | bytes 4216832 | tf_op jit(solution)/shard_map/convert_element_type | solution.py:103
  34.9 0.8 fusion.273
  38.2 15.3 %add_convert_fusion = bf16[512,16,128]{2,1,0:T(8,128)(2,1)} fusion(bf16[512,16,128]{2,1,0:T(8,128)(2,1)S(1)} %copy-done, f32[512]{0:T(512)S(1)} %get-tuple-element.24, f32[512]{0:T(512)S(1)} %get-tuple-element.23, f32[512]{0:T(512)S(1)} %get-tuple-element.22, f32[512]{0:T(512)S(1)} %get-tuple-element.21, f32[512]{0:T(512)S(1)} %get-tuple-element.20, ...), kind=kLoop, calls=%fused_computation.27 | loop fusion | flops 34603008 | bytes 4216832 | tf_op jit(solution)/shard_map/convert_element_type | solution.py:103
  53.6 1.6 collective-permute-start.2
  56.0 0.7 fusion.216
  57.4 0.7 fusion.217
  58.1 42.6 %collective-permute-done.2 = bf16[512,16,128]{2,1,0:T(8,128)(2,1)S(1)} collective-permute-done((bf16[512,16,128]{2,1,0:T(8,128)(2,1)S(1)}, bf16[512,16,128]{2,1,0:T(8,128)(2,1)S(1)}, u32[]{:S(2)}, u32[]{:S(2)}) %collective-permute-start.2) | collective-permute-done | bytes 2097184 | tf_op jit(solution)/shard_map/ppermute | solution.py:174
  100.8 1.3 copy-done.1
  102.1 2.7 pad_maximum_fusion.1
  105.3 1.6 collective-permute-start.4
  106.8 5.5 %collective-permute-done.3 = bf16[512,32,128]{2,1,0:T(8,128)(2,1)} collective-permute-done((bf16[512,32,128]{2,1,0:T(8,128)(2,1)}, bf16[512,32,128]{2,1,0:T(8,128)(2,1)}, u32[]{:S(2)}, u32[]{:S(2)}) %collective-permute-start.3) | collective-permute-done | bytes 4194336 | tf_op jit(solution)/shard_map/ppermute | solution.py:178
  112.4 6.3 %fusion.17 = bf16[16,2,2,512,128]{4,0,3,2,1:T(8,128)(2,1)} fusion(bf16[512,32,128]{2,1,0:T(8,128)(2,1)} %collective-permute-done.3, bf16[512,16,128]{2,1,0:T(8,128)(2,1)} %copy-done.1, bf16[512,16,128]{2,1,0:T(8,128)(2,1)S(1)} %fusion.215, bf16[16,2,2,64]{3,0,2,1:T(8,128)(2,1)S(1)} %pad_maximum_fusion.7), kind=kOutput, calls=%fused_computation.21 | convolution fusion | flops 566231040 | bytes 16785408 | tf_op jit(solution)/shard_map/fkrt,ptc->fkrpc/dot_general | solution.py:183
  118.7 12.7 %fusion.18 = bf16[16,512,2,128]{1,3,2,0:T(8,128)(2,1)} fusion(bf16[16,2,512,512]{3,2,1,0:T(8,128)(2,1)} %param.7, bf16[16,2,2,512,128]{4,0,3,2,1:T(8,128)(2,1)} %fusion.17), kind=kOutput, calls=%fused_computation.22 | convolution fusion | flops 4297064448 | bytes 29360128 | tf_op jit(solution)/shard_map/fksp,fkrpc->fsrc/dot_general | solution.py:188
  131.4 8.1 %copy.13 = bf16[16,512,2,128]{3,0,2,1:T(8,128)(2,1)} copy(bf16[16,512,2,128]{1,3,2,0:T(8,128)(2,1)} %fusion.18) | data formatting | bytes 8388608 | tf_op jit(solution)/shard_map/convert_element_type | solution.py:189
  139.7 14.0 %collective-permute-done.4 = bf16[512,16,128]{2,1,0:T(8,128)(2,1)} collective-permute-done((bf16[512,16,128]{2,1,0:T(8,128)(2,1)}, bf16[512,16,128]{2,1,0:T(8,128)(2,1)}, u32[]{:S(2)}, u32[]{:S(2)}) %collective-permute-start.4) | collective-permute-done | bytes 2097184 | tf_op jit(solution)/shard_map/ppermute | solution.py:174
  153.7 3.0 pad_maximum_fusion.2
  156.7 7.1 %collective-permute-done.5 = bf16[512,32,128]{2,1,0:T(8,128)(2,1)S(1)} collective-permute-done((bf16[512,32,128]{2,1,0:T(8,128)(2,1)S(1)}, bf16[512,32,128]{2,1,0:T(8,128)(2,1)S(1)}, u32[]{:S(2)}, u32[]{:S(2)}) %collective-permute-start.5) | collective-permute-done | bytes 4194336 | tf_op jit(solution)/shard_map/ppermute | solution.py:178
  163.9 6.1 %fusion.16 = bf16[16,2,2,512,128]{4,0,3,2,1:T(8,128)(2,1)} fusion(bf16[512,32,128]{2,1,0:T(8,128)(2,1)S(1)} %collective-permute-done.5, bf16[512,16,128]{2,1,0:T(8,128)(2,1)} %collective-permute-done.4, bf16[512,16,128]{2,1,0:T(8,128)(2,1)} %fusion.217, bf16[16,2,2,64]{3,0,2,1:T(8,128)(2,1)S(1)} %pad_maximum_fusion.7), kind=kOutput, calls=%fused_computation.20 | convolution fusion | flops 566231040 | bytes 16785408 | tf_op jit(solution)/shard_map/fkrt,ptc->fkrpc/dot_general | solution.py:183
  170.0 12.9 %fusion.19 = bf16[16,512,2,128]{1,3,2,0:T(8,128)(2,1)} fusion(bf16[16,2,512,512]{3,2,1,0:T(8,128)(2,1)} %param.7, bf16[16,2,2,512,128]{4,0,3,2,1:T(8,128)(2,1)} %fusion.16), kind=kOutput, calls=%fused_computation.23 | convolution fusion | flops 4297064448 | bytes 29360128 | tf_op jit(solution)/shard_map/fksp,fkrpc->fsrc/dot_general | solution.py:188
  182.9 8.0 %copy.15 = bf16[16,512,2,128]{3,0,2,1:T(8,128)(2,1)} copy(bf16[16,512,2,128]{1,3,2,0:T(8,128)(2,1)} %fusion.19) | data formatting | bytes 8388608 | tf_op jit(solution)/shard_map/convert_element_type | solution.py:189
  190.9 4.1 %pad_maximum_fusion = bf16[512,16,256]{2,1,0:T(8,128)(2,1)} fusion(bf16[512,16,128]{2,1,0:T(8,128)(2,1)} %fusion.217, bf16[512,16,128]{2,1,0:T(8,128)(2,1)S(1)} %fusion.215), kind=kLoop, calls=%fused_computation.24 | loop fusion | flops 8388608 | bytes 8388608 | tf_op jit(solution)/shard_map/concatenate | solution.py:223
  195.1 34.6 %reduce-scatter.3.cloned.1.call-done = bf16[16,64,2,128]{3,0,2,1:T(8,128)(2,1)} async-done(((bf16[16,512,2,128]{3,0,2,1:T(8,128)(2,1)}), bf16[16,64,2,128]{3,0,2,1:T(8,128)(2,1)}) %reduce-scatter.3.cloned.1.call-update) | async-done | bytes 524304 | tf_op jit(solution)/shard_map/reduce_scatter | solution.py:189
  229.6 91.9 %reduce-scatter.5.cloned.1.call-done = bf16[16,64,2,128]{3,0,2,1:T(8,128)(2,1)} async-done(((bf16[16,512,2,128]{3,0,2,1:T(8,128)(2,1)}), bf16[16,64,2,128]{3,0,2,1:T(8,128)(2,1)}) %reduce-scatter.5.cloned.1.call-update) | async-done | bytes 524304 | tf_op jit(solution)/shard_map/reduce_scatter | solution.py:189
  321.6 1.4 maximum_convert_fusion
  322.9 3.2 copy.16
  (82 shorter events, 5.6 us)
Async XLA Ops:
  7.2 222.5 %reduce-scatter.3.cloned.1.call-start = ((), (), s32[]{:S(2)}) async-start(), calls=%async_computation.2 | async-start | bytes 4718592 | tf_op jit(solution)/shard_map/reduce_scatter | solution.py:189
  9.7 26.1 %collective-permute-start = (f32[20491]{0:T(1024)S(1)}, f32[20491]{0:T(1024)S(1)}, u32[]{:S(2)}, u32[]{:S(2)}) collective-permute-start(f32[20491]{0:T(1024)S(1)} %concatenate.55), channel_id=1, source_target_pairs={{0,4},{4,8},{8,12},{12,16},{16,20},{20,24},{24,28},{1,5},{5,9},{9,... | collective-permute-start | bytes 245900 | tf_op jit(solution)/shard_map/ppermute | solution.py:14
  15.4 20.3 %collective-permute-start.1 = (f32[20490]{0:T(1024)S(1)}, f32[20490]{0:T(1024)S(1)}, u32[]{:S(2)}, u32[]{:S(2)}) collective-permute-start(f32[20490]{0:T(1024)S(1)} %concatenate.57), channel_id=1, source_target_pairs={{4,0},{8,4},{12,8},{16,12},{20,16},{24,20},{28,24},{5,1},{9,5},{13... | collective-permute-start | bytes 245888 | tf_op jit(solution)/shard_map/ppermute | solution.py:19
  16.8 5.0 %copy-start.2 = (f32[512]{0:T(512)S(1)}, f32[512]{0:T(512)}, u32[]{:S(2)}) copy-start(f32[512]{0:T(512)} %param.5) | copy-start | bytes 6148
  16.8 5.0 %copy-start.3 = (f32[512]{0:T(512)S(1)}, f32[512]{0:T(512)}, u32[]{:S(2)}) copy-start(f32[512]{0:T(512)} %param.6) | copy-start | bytes 6148
  36.3 1.9 copy-start
  53.6 47.2 %collective-permute-start.2 = (bf16[512,16,128]{2,1,0:T(8,128)(2,1)S(1)}, bf16[512,16,128]{2,1,0:T(8,128)(2,1)S(1)}, u32[]{:S(2)}, u32[]{:S(2)}) collective-permute-start(bf16[512,16,128]{2,1,0:T(8,128)(2,1)S(1)} %fusion.215), channel_id=1, source_target_pairs={{0,2},{2,0},{1,3},{3,1},{4,6},{6,4},{5,7},{7,5},{8,10},{10,8},{9,1... | collective-permute-start | bytes 6291464 | tf_op jit(solution)/shard_map/ppermute | solution.py:174
  100.8 1.3 copy-start.1
  104.9 7.5 %collective-permute-start.3 = (bf16[512,32,128]{2,1,0:T(8,128)(2,1)}, bf16[512,32,128]{2,1,0:T(8,128)(2,1)}, u32[]{:S(2)}, u32[]{:S(2)}) collective-permute-start(bf16[512,32,128]{2,1,0:T(8,128)(2,1)} %pad_maximum_fusion.1), channel_id=1, source_target_pairs={{0,1},{1,0},{2,3},{3,2},{4,5},{5,4},{6,7},{7,6},{8,9},{9,8},{10,11... | collective-permute-start | bytes 12582920 | tf_op jit(solution)/shard_map/ppermute | solution.py:178
  105.3 48.4 %collective-permute-start.4 = (bf16[512,16,128]{2,1,0:T(8,128)(2,1)}, bf16[512,16,128]{2,1,0:T(8,128)(2,1)}, u32[]{:S(2)}, u32[]{:S(2)}) collective-permute-start(bf16[512,16,128]{2,1,0:T(8,128)(2,1)} %fusion.217), channel_id=1, source_target_pairs={{0,2},{2,0},{1,3},{3,1},{4,6},{6,4},{5,7},{7,5},{8,10},{10,8},{9,1... | collective-permute-start | bytes 6291464 | tf_op jit(solution)/shard_map/ppermute | solution.py:174
  139.5 182.0 %reduce-scatter.5.cloned.1.call-start = ((), (), s32[]{:S(2)}) async-start(), calls=%async_computation.3 | async-start | bytes 4718592 | tf_op jit(solution)/shard_map/reduce_scatter | solution.py:189
  156.7 7.2 %collective-permute-start.5 = (bf16[512,32,128]{2,1,0:T(8,128)(2,1)S(1)}, bf16[512,32,128]{2,1,0:T(8,128)(2,1)S(1)}, u32[]{:S(2)}, u32[]{:S(2)}) collective-permute-start(bf16[512,32,128]{2,1,0:T(8,128)(2,1)S(1)} %pad_maximum_fusion.2), channel_id=1, source_target_pairs={{0,1},{1,0},{2,3},{3,2},{4,5},{5,4},{6,7},{7,6},{8,9},{9,8},{10,11... | collective-permute-start | bytes 12582920 | tf_op jit(solution)/shard_map/ppermute | solution.py:178
Sparse Core Ops, SparseCore 0:
  139.6 89.9 reduce-scatter.2
  233.7 87.8 reduce-scatter.4

commit v8 on v6

--- a/solution.py
+++ b/solution.py
@@ -167,9 +167,34 @@
     return mixed.astype(jnp.bfloat16)
 
 
+def halving_reduce_scatter(x):
+    count = lax.axis_size("sea")
+    where_sea = lax.axis_index("sea")
+    bits = count.bit_length() - 1
+    freqs, rows, parts, cols = x.shape
+    current = x.reshape((freqs,) + (2,) * bits + (rows // count, parts, cols))
+    for bit in range(bits):
+        axis = bits - bit
+        mine = (where_sea >> bit) & 1
+        keep = lax.dynamic_index_in_dim(current, mine, axis, keepdims=False)
+        send = lax.dynamic_index_in_dim(current, 1 - mine, axis, keepdims=False)
+        got = lax.ppermute(send, "sea", [(i, i ^ (1 << bit)) for i in range(count)])
+        current = keep.astype(jnp.float32) + got.astype(jnp.float32)
+    return current.reshape(freqs, rows // count, parts, cols)
+
+
 def green_product(mixed, green):
     partial = jnp.einsum("fksp,fkrpc->fsrc", green, mixed, preferred_element_type=jnp.float32)
-    summed = lax.psum_scatter(partial.astype(jnp.bfloat16), "sea", scatter_dimension=1, tiled=True)
+    rounded = partial.astype(jnp.bfloat16)
+    count = lax.axis_size("sea")
+    if count & (count - 1) == 0:
+        half = rounded.shape[0] // 2
+        offloaded = lax.psum_scatter(rounded[:half], "sea", scatter_dimension=1, tiled=True)
+        summed = jnp.concatenate(
+            [offloaded.astype(jnp.float32), halving_reduce_scatter(rounded[half:])]
+        )
+    else:
+        summed = lax.psum_scatter(rounded, "sea", scatter_dimension=1, tiled=True)
     return jnp.transpose(summed, (1, 0, 2, 3)).astype(jnp.float32)
 
 

time: 322 us -> 346 us (1.075)
  starting transfers between devices: 9.41 us -> 18.2 us
  other arithmetic: 58.4 us -> 67.1 us
  waiting for transfers between devices: 162 us -> 168 us
    reduce_scatter x2, waiting for transfers between devices: 113 us -> 0.04 us  [green_product(): lax.psum_scatter(rounded[:half], 'sea', scatter_dimension=1, tiled=True)]
    ppermute x0 -> x6, waiting for transfers between devices: none -> 104 us  [halving_reduce_scatter(): got = lax.ppermute(send, 'sea', [(i, i ^ 1 << bit) for i in range(count)])]
    slice x0 -> x6, local copies, waits for them, and re-layouts: none -> 23.5 us  [the longest x4 16.3 us: green_product(): rounded[:half]]
    ppermute x2, waiting for transfers between devices: 36.6 us -> 58 us  [gathered_spectrum(): across = lax.ppermute(prior_part, 'tm', [(0, 2), (2, 0), (1, 3), (3, 1)])]
    convert_element_type x2 -> x0, local copies, waits for them, and re-layouts: 16.1 us -> none  [green_product(): partial.astype(jnp.bfloat16)]
    dot_general x1 -> x0, local copies, waits for them, and re-layouts: 13.9 us -> none  [gathered_spectrum(): jnp.einsum('fkrt,ptc->fkrpc', table_high, stacked, preferred_element_type...]
    ppermute x0 -> x6, starting transfers between devices: none -> 7.56 us  [halving_reduce_scatter(): got = lax.ppermute(send, 'sea', [(i, i ^ 1 << bit) for i in range(count)])]
    ppermute x2, waiting for transfers between devices: 12.7 us -> 5.38 us  [gathered_spectrum(): theirs = lax.ppermute(mine, 'tm', [(0, 1), (1, 0), (2, 3), (3, 2)])]
  transfers between devices with their start and end apart: 8 -> 14, of which waited for: 6 -> 6; matrix products, arithmetic and copies ran while one was open for 38% -> 36% of each run, Pallas kernels for 0% -> 0%
where the time goes in v8:
time: 346 us; the launch traced here: 345 us
  waiting for transfers between devices  168 us (49%)
  other arithmetic  67.1 us (19%)
  matrix products  39.2 us (11%)
  local copies, waits for them, and re-layouts  38 us (11%)
  starting transfers between devices  18.2 us (5%)
  between operations  14.6 us (4%)
    ppermute x6, waiting for transfers between devices, halving_reduce_scatter(): got = lax.ppermute(send, 'sea', [(i, i ^ 1 << bit) for i in range(count)])  104 us
    ppermute x2, waiting for transfers between devices, gathered_spectrum(): across = lax.ppermute(prior_part, 'tm', [(0, 2), (2, 0), (1, 3), (3, 1)])  58 us
    add x24, other arithmetic, smooth(): state = state + weights[k] * (source - applied) / diag  29.7 us
    dot_general x2, matrix products, green_product(): jnp.einsum('fksp,fkrpc->fsrc', green, mixed, preferred_element_type=jnp.f...  25.6 us
    slice x4, local copies, waits for them, and re-layouts, green_product(): rounded[:half]  16.3 us
    dot_general x2, matrix products, gathered_spectrum(): jnp.einsum('fkrt,ptc->fkrpc', table_high, stacked, preferred_element_type...  13.6 us
    convert_element_type x2, other arithmetic, smooth_with_edges(): smooth(motion.astype(jnp.float32), *local_coefficients_, 0)  9.14 us
    concatenate x2, other arithmetic, gathered_spectrum(): mine = jnp.concatenate([prior_part, across], axis=1)  7.81 us
  transfers between devices with their start and end apart: 14, of which 6 were waited for; matrix products, arithmetic and copies ran while one was open for 36% of the time, Pallas kernels for 0%

profile of v8, /device:TPU:0, one launch (start us, length us, event | category | flops | bytes accessed | tf_op | source)
XLA Modules:
  0.0 344.8 jit_solution(5509353817377317939)
XLA Ops:
  11.8 5.5 %collective-permute-start = (f32[20491]{0:T(1024)S(1)}, f32[20491]{0:T(1024)S(1)}, u32[]{:S(2)}, u32[]{:S(2)}) collective-permute-start(f32[20491]{0:T(1024)S(1)} %concatenate.58), channel_id=1, source_target_pairs={{0,4},{4,8},{8,12},{12,16},{16,20},{20,24},{24,28},{1,5},{5,9},{9,... | collective-permute-start | bytes 245900 | tf_op jit(solution)/shard_map/ppermute | solution.py:14
  18.3 3.0 fusion.20
  21.3 3.5 %fusion.23 = f32[512,16,128]{2,1,0:T(8,128)S(1)} fusion(f32[512,16,128]{2,1,0:T(8,128)S(1)} %fusion.20, f32[512]{0:T(512)S(1)} %get-tuple-element.19, f32[512]{0:T(512)S(1)} %get-tuple-element.63, f32[512]{0:T(512)S(1)} %get-tuple-element.18, bf16[512,16,256]{2,1,0:T(8,128)(2,1)S(1)} %copy-done), kind=kLoop, calls=%fused_computation.39 | loop fusion | flops 10485760 | bytes 10491904 | tf_op jit(solution)/shard_map/add | solution.py:68
  24.8 3.5 %fusion.26 = f32[512,16,128]{2,1,0:T(8,128)S(1)} fusion(f32[512,16,128]{2,1,0:T(8,128)S(1)} %fusion.23, f32[512]{0:T(512)S(1)} %get-tuple-element.19, f32[512]{0:T(512)S(1)} %get-tuple-element.63, f32[512]{0:T(512)S(1)} %get-tuple-element.18, bf16[512,16,256]{2,1,0:T(8,128)(2,1)S(1)} %copy-done), kind=kLoop, calls=%fused_computation.42 | loop fusion | flops 10485760 | bytes 10491904 | tf_op jit(solution)/shard_map/add | solution.py:68
  28.2 3.5 %fusion.29 = f32[512,16,128]{2,1,0:T(8,128)S(1)} fusion(f32[512,16,128]{2,1,0:T(8,128)S(1)} %fusion.26, f32[512]{0:T(512)S(1)} %get-tuple-element.19, f32[512]{0:T(512)S(1)} %get-tuple-element.63, f32[512]{0:T(512)S(1)} %get-tuple-element.18, bf16[512,16,256]{2,1,0:T(8,128)(2,1)S(1)} %copy-done), kind=kLoop, calls=%fused_computation.45 | loop fusion | flops 10485760 | bytes 10491904 | tf_op jit(solution)/shard_map/add | solution.py:68
  31.7 3.5 %fusion.32 = f32[512,16,128]{2,1,0:T(8,128)S(1)} fusion(f32[512,16,128]{2,1,0:T(8,128)S(1)} %fusion.29, f32[512]{0:T(512)S(1)} %get-tuple-element.19, f32[512]{0:T(512)S(1)} %get-tuple-element.63, f32[512]{0:T(512)S(1)} %get-tuple-element.18, bf16[512,16,256]{2,1,0:T(8,128)(2,1)S(1)} %copy-done), kind=kLoop, calls=%fused_computation.48 | loop fusion | flops 10485760 | bytes 10491904 | tf_op jit(solution)/shard_map/add | solution.py:68
  35.2 4.6 %fusion.53 = bf16[512,16,128]{2,1,0:T(8,128)(2,1)} fusion(f32[512,16,128]{2,1,0:T(8,128)S(1)} %fusion.32, f32[512]{0:T(512)S(1)} %get-tuple-element.19, f32[512]{0:T(512)S(1)} %get-tuple-element.63, f32[512]{0:T(512)S(1)} %get-tuple-element.18, bf16[512,16,256]{2,1,0:T(8,128)(2,1)S(1)} %copy-done), kind=kLoop, calls=%fused_computation.72 | loop fusion | flops 11534336 | bytes 8394752 | tf_op jit(solution)/shard_map/convert_element_type | solution.py:86
  46.9 3.4 fusion.39
  50.3 3.4 fusion.42
  53.7 3.4 fusion.45
  57.1 3.4 fusion.48
  60.6 4.6 %fusion.52 = bf16[512,16,128]{2,1,0:T(8,128)(2,1)} fusion(f32[512,16,128]{2,1,0:T(8,128)S(1)} %fusion.48, bf16[512,16,128]{2,1,0:T(8,128)(2,1)S(1)} %slice.375, f32[512]{0:T(512)S(1)} %get-tuple-element.19, f32[512]{0:T(512)S(1)} %get-tuple-element.63, f32[512]{0:T(512)S(1)} %get-tuple-element.18), kind=kLoop, calls=%fused_computation.71 | loop fusion | flops 11534336 | bytes 8394752 | tf_op jit(solution)/shard_map/convert_element_type | solution.py:86
  67.6 23.9 %collective-permute-done.2 = bf16[512,16,128]{2,1,0:T(8,128)(2,1)S(1)} collective-permute-done((bf16[512,16,128]{2,1,0:T(8,128)(2,1)S(1)}, bf16[512,16,128]{2,1,0:T(8,128)(2,1)S(1)}, u32[]{:S(2)}, u32[]{:S(2)}) %collective-permute-start.2) | collective-permute-done | bytes 2097184 | tf_op jit(solution)/shard_map/ppermute | solution.py:157
  91.6 2.7 pad_maximum_fusion.1
  96.4 5.4 %collective-permute-done.3 = bf16[512,32,128]{2,1,0:T(8,128)(2,1)} collective-permute-done((bf16[512,32,128]{2,1,0:T(8,128)(2,1)}, bf16[512,32,128]{2,1,0:T(8,128)(2,1)}, u32[]{:S(2)}, u32[]{:S(2)}) %collective-permute-start.3) | collective-permute-done | bytes 4194336 | tf_op jit(solution)/shard_map/ppermute | solution.py:161
  101.8 6.7 %fusion.17 = bf16[16,2,2,512,128]{4,0,3,2,1:T(8,128)(2,1)} fusion(bf16[512,32,128]{2,1,0:T(8,128)(2,1)} %collective-permute-done.3, bf16[512,16,128]{2,1,0:T(8,128)(2,1)} %copy-done.6, bf16[512,16,128]{2,1,0:T(8,128)(2,1)} %copy-done.2, bf16[16,2,2,64]{3,0,2,1:T(8,128)(2,1)S(1)} %pad_maximum_fusion.8), kind=kOutput, calls=%fused_computation.33 | convolution fusion | flops 566231040 | bytes 16785408 | tf_op jit(solution)/shard_map/fkrt,ptc->fkrpc/dot_general | solution.py:166
  108.5 34.0 %collective-permute-done.7 = bf16[512,16,128]{2,1,0:T(8,128)(2,1)S(1)} collective-permute-done((bf16[512,16,128]{2,1,0:T(8,128)(2,1)}, bf16[512,16,128]{2,1,0:T(8,128)(2,1)S(1)}, u32[]{:S(2)}, u32[]{:S(2)}) %collective-permute-start.7) | collective-permute-done | bytes 2097184 | tf_op jit(solution)/shard_map/ppermute | solution.py:157
  142.6 5.1 %pad_maximum_fusion.2 = bf16[512,32,128]{2,1,0:T(8,128)(2,1)} fusion(bf16[512,16,128]{2,1,0:T(8,128)(2,1)S(1)} %collective-permute-done.7, bf16[512,16,128]{2,1,0:T(8,128)(2,1)} %fusion.205), kind=kLoop, calls=%fused_computation.70 | loop fusion | flops 8388608 | bytes 8388608 | tf_op jit(solution)/shard_map/concatenate | solution.py:160
  147.6 12.7 %fusion.18 = bf16[16,512,2,128]{1,3,2,0:T(8,128)(2,1)} fusion(bf16[16,2,512,512]{3,2,1,0:T(8,128)(2,1)} %param.7, bf16[16,2,2,512,128]{4,0,3,2,1:T(8,128)(2,1)} %fusion.17), kind=kOutput, calls=%fused_computation.34 | convolution fusion | flops 4297064448 | bytes 29360128 | tf_op jit(solution)/shard_map/fksp,fkrpc->fsrc/dot_general | solution.py:187
  160.4 4.0 %fusion.228 = (bf16[8,512,2,128]{1,3,2,0:T(8,128)(2,1)S(1)}, bf16[8,512,2,128]{1,3,2,0:T(8,128)(2,1)}) fusion(bf16[16,512,2,128]{1,3,2,0:T(8,128)(2,1)} %fusion.18), kind=kLoop, calls=%fused_computation.361 | loop fusion | bytes 8388608 | tf_op jit(solution)/shard_map/slice | solution.py:192
  164.3 3.1 copy.57
  167.5 3.3 copy.59
  174.5 6.9 %fusion.16 = bf16[16,2,2,512,128]{4,0,3,2,1:T(8,128)(2,1)} fusion(bf16[512,32,128]{2,1,0:T(8,128)(2,1)} %collective-permute-done.8, bf16[512,16,128]{2,1,0:T(8,128)(2,1)} %copy-done.7, bf16[512,16,128]{2,1,0:T(8,128)(2,1)} %fusion.205, bf16[16,2,2,64]{3,0,2,1:T(8,128)(2,1)S(1)} %pad_maximum_fusion.8), kind=kOutput, calls=%fused_computation.32 | convolution fusion | flops 566231040 | bytes 16785408 | tf_op jit(solution)/shard_map/fkrt,ptc->fkrpc/dot_general | solution.py:166
  181.4 12.8 %fusion.19 = bf16[16,512,2,128]{1,3,2,0:T(8,128)(2,1)} fusion(bf16[16,2,512,512]{3,2,1,0:T(8,128)(2,1)} %param.7, bf16[16,2,2,512,128]{4,0,3,2,1:T(8,128)(2,1)} %fusion.16), kind=kOutput, calls=%fused_computation.35 | convolution fusion | flops 4297064448 | bytes 29360128 | tf_op jit(solution)/shard_map/fksp,fkrpc->fsrc/dot_general | solution.py:187
  194.2 4.7 %fusion.229 = (bf16[8,512,2,128]{1,3,2,0:T(8,128)(2,1)}, bf16[8,512,2,128]{1,3,2,0:T(8,128)(2,1)}) fusion(bf16[16,512,2,128]{1,3,2,0:T(8,128)(2,1)} %fusion.19), kind=kLoop, calls=%fused_computation.362 | loop fusion | bytes 8388608 | tf_op jit(solution)/shard_map/slice | solution.py:192
  198.9 4.5 %copy.65 = bf16[8,512,2,128]{3,0,2,1:T(8,128)(2,1)} copy(bf16[8,512,2,128]{1,3,2,0:T(8,128)(2,1)} %get-tuple-element.22) | data formatting | bytes 4194304 | tf_op jit(solution)/shard_map/slice | solution.py:192
  203.5 3.9 %copy.67 = bf16[8,512,2,128]{3,1,2,0:T(8,128)(2,1)} copy(bf16[8,512,2,128]{1,3,2,0:T(8,128)(2,1)} %get-tuple-element.23) | data formatting | bytes 4194304 | tf_op jit(solution)/shard_map/slice | solution.py:194
  213.1 27.5 %collective-permute-done.9 = bf16[8,2,2,64,2,128]{5,3,2,1,4,0:T(8,128)(2,1)} collective-permute-done((bf16[8,2,2,64,2,128]{5,3,2,1,4,0:T(8,128)(2,1)}, bf16[8,2,2,64,2,128]{5,3,2,1,4,0:T(8,128)(2,1)}, u32[]{:S(2)}, u32[]{:S(2)}) %collective-permute-start.9) | collective-permute-done | bytes 1048608 | tf_op jit(solution)/shard_map/ppermute | solution.py:181
  249.1 4.1 %pad_maximum_fusion = bf16[512,16,256]{2,1,0:T(8,128)(2,1)} fusion(bf16[512,16,128]{2,1,0:T(8,128)(2,1)} %fusion.205, bf16[512,16,128]{2,1,0:T(8,128)(2,1)S(1)} %copy-done.3), kind=kLoop, calls=%fused_computation.68 | loop fusion | flops 8388608 | bytes 8388608 | tf_op jit(solution)/shard_map/concatenate | solution.py:231
  253.2 44.6 %collective-permute-done.10 = f32[8,2,64,2,128]{4,2,3,1,0:T(8,128)} collective-permute-done((f32[8,2,64,2,128]{4,2,3,1,0:T(8,128)}, f32[8,2,64,2,128]{4,2,3,1,0:T(8,128)}, u32[]{:S(2)}, u32[]{:S(2)}) %collective-permute-start.10) | collective-permute-done | bytes 1048608 | tf_op jit(solution)/shard_map/ppermute | solution.py:181
  301.5 32.2 %collective-permute-done.11 = f32[8,64,2,128]{3,1,2,0:T(8,128)S(1)} collective-permute-done((f32[8,64,2,128]{3,1,2,0:T(8,128)}, f32[8,64,2,128]{3,1,2,0:T(8,128)S(1)}, u32[]{:S(2)}, u32[]{:S(2)}) %collective-permute-start.11) | collective-permute-done | bytes 524320 | tf_op jit(solution)/shard_map/ppermute | solution.py:181
  335.0 2.9 copy.72
  (126 shorter events, 40.0 us)
Async XLA Ops:
  7.2 293.2 %reduce-scatter.3.cloned.1.call-start = ((), (), s32[]{:S(2)}) async-start(), calls=%async_computation.2 | async-start | bytes 2359296 | tf_op jit(solution)/shard_map/reduce_scatter | solution.py:192
  9.7 30.5 %collective-permute-start.1 = (f32[20490]{0:T(1024)S(1)}, f32[20490]{0:T(1024)S(1)}, u32[]{:S(2)}, u32[]{:S(2)}) collective-permute-start(f32[20490]{0:T(1024)S(1)} %concatenate.60), channel_id=1, source_target_pairs={{4,0},{8,4},{12,8},{16,12},{20,16},{24,20},{28,24},{5,1},{9,5},{13... | collective-permute-start | bytes 245888 | tf_op jit(solution)/shard_map/ppermute | solution.py:19
  11.8 28.4 %collective-permute-start = (f32[20491]{0:T(1024)S(1)}, f32[20491]{0:T(1024)S(1)}, u32[]{:S(2)}, u32[]{:S(2)}) collective-permute-start(f32[20491]{0:T(1024)S(1)} %concatenate.58), channel_id=1, source_target_pairs={{0,4},{4,8},{8,12},{12,16},{16,20},{20,24},{24,28},{1,5},{5,9},{9,... | collective-permute-start | bytes 245900 | tf_op jit(solution)/shard_map/ppermute | solution.py:14
  17.3 3.9 %copy-start = (bf16[512,16,256]{2,1,0:T(8,128)(2,1)S(1)}, bf16[512,16,256]{2,1,0:T(8,128)(2,1)}, u32[]{:S(2)}) copy-start(bf16[512,16,256]{2,1,0:T(8,128)(2,1)} %param.4) | copy-start | bytes 12582916
  39.7 0.7 copy-start.8
  39.7 0.8 copy-start.9
  40.8 1.7 copy-start.1
  42.7 48.8 %copy-start.2 = (bf16[512,16,128]{2,1,0:T(8,128)(2,1)}, bf16[512,16,128]{2,1,0:T(8,128)(2,1)S(1)}, u32[]{:S(2)}) copy-start(bf16[512,16,128]{2,1,0:T(8,128)(2,1)S(1)} %fusion.203) | copy-start | bytes 6291460
  44.4 47.2 %collective-permute-start.2 = (bf16[512,16,128]{2,1,0:T(8,128)(2,1)S(1)}, bf16[512,16,128]{2,1,0:T(8,128)(2,1)S(1)}, u32[]{:S(2)}, u32[]{:S(2)}) collective-permute-start(bf16[512,16,128]{2,1,0:T(8,128)(2,1)S(1)} %fusion.203), channel_id=1, source_target_pairs={{0,2},{2,0},{1,3},{3,1},{4,6},{6,4},{5,7},{7,5},{8,10},{10,8},{9,1... | collective-permute-start | bytes 6291464 | tf_op jit(solution)/shard_map/ppermute | solution.py:157
  91.6 2.7 copy-start.6
  94.3 7.5 %collective-permute-start.3 = (bf16[512,32,128]{2,1,0:T(8,128)(2,1)}, bf16[512,32,128]{2,1,0:T(8,128)(2,1)}, u32[]{:S(2)}, u32[]{:S(2)}) collective-permute-start(bf16[512,32,128]{2,1,0:T(8,128)(2,1)} %pad_maximum_fusion.1), channel_id=1, source_target_pairs={{0,1},{1,0},{2,3},{3,2},{4,5},{5,4},{6,7},{7,6},{8,9},{9,8},{10,11... | collective-permute-start | bytes 12582920 | tf_op jit(solution)/shard_map/ppermute | solution.py:161
  94.3 48.3 %collective-permute-start.7 = (bf16[512,16,128]{2,1,0:T(8,128)(2,1)}, bf16[512,16,128]{2,1,0:T(8,128)(2,1)S(1)}, u32[]{:S(2)}, u32[]{:S(2)}) collective-permute-start(bf16[512,16,128]{2,1,0:T(8,128)(2,1)} %fusion.205), channel_id=1, source_target_pairs={{0,2},{2,0},{1,3},{3,1},{4,6},{6,4},{5,7},{7,5},{8,10},{10,8},{9,1... | collective-permute-start | bytes 6291464 | tf_op jit(solution)/shard_map/ppermute | solution.py:157
  142.6 5.1 %copy-start.7 = (bf16[512,16,128]{2,1,0:T(8,128)(2,1)}, bf16[512,16,128]{2,1,0:T(8,128)(2,1)S(1)}, u32[]{:S(2)}) copy-start(bf16[512,16,128]{2,1,0:T(8,128)(2,1)S(1)} %collective-permute-done.7) | copy-start | bytes 6291460
  147.6 26.9 %collective-permute-start.8 = (bf16[512,32,128]{2,1,0:T(8,128)(2,1)}, bf16[512,32,128]{2,1,0:T(8,128)(2,1)}, u32[]{:S(2)}, u32[]{:S(2)}) collective-permute-start(bf16[512,32,128]{2,1,0:T(8,128)(2,1)} %pad_maximum_fusion.2), channel_id=1, source_target_pairs={{0,1},{1,0},{2,3},{3,2},{4,5},{5,4},{6,7},{7,6},{8,9},{9,8},{10,11... | collective-permute-start | bytes 12582920 | tf_op jit(solution)/shard_map/ppermute | solution.py:161
  167.4 166.3 %reduce-scatter.5.cloned.1.call-start = ((), (), s32[]{:S(2)}) async-start(), calls=%async_computation.3 | async-start | bytes 2359296 | tf_op jit(solution)/shard_map/reduce_scatter | solution.py:192
  171.9 37.9 %collective-permute-start.4 = (bf16[8,2,2,64,2,128]{5,3,2,1,4,0:T(8,128)(2,1)}, bf16[8,2,2,64,2,128]{5,3,2,1,4,0:T(8,128)(2,1)S(1)}, u32[]{:S(2)}, u32[]{:S(2)}) collective-permute-start(bf16[8,2,2,64,2,128]{5,3,2,1,4,0:T(8,128)(2,1)} %dynamic-slice_bitcast_fusion.1), channel_id=1, source_target_pairs={{0,4},{4,0},{8,12},{12,8},{16,20},{20,16},{24,28},{28,24},{1,5},{5... | collective-permute-start | bytes 3145736 | tf_op jit(solution)/shard_map/ppermute | solution.py:181
  209.8 30.8 %collective-permute-start.9 = (bf16[8,2,2,64,2,128]{5,3,2,1,4,0:T(8,128)(2,1)}, bf16[8,2,2,64,2,128]{5,3,2,1,4,0:T(8,128)(2,1)}, u32[]{:S(2)}, u32[]{:S(2)}) collective-permute-start(bf16[8,2,2,64,2,128]{5,3,2,1,4,0:T(8,128)(2,1)} %dynamic-slice_bitcast_fusion), channel_id=1, source_target_pairs={{0,4},{4,0},{8,12},{12,8},{16,20},{20,16},{24,28},{28,24},{1,5},{5... | collective-permute-start | bytes 3145736 | tf_op jit(solution)/shard_map/ppermute | solution.py:181
  210.2 30.4 %copy-start.4 = (bf16[8,512,2,128]{3,1,2,0:T(8,128)(2,1)S(1)}, bf16[8,512,2,128]{3,1,2,0:T(8,128)(2,1)}, u32[]{:S(2)}) copy-start(bf16[8,512,2,128]{3,1,2,0:T(8,128)(2,1)} %copy.67) | copy-start | bytes 6291460
  211.5 34.4 %collective-permute-start.5 = (f32[8,2,64,2,128]{4,2,3,1,0:T(8,128)}, f32[8,2,64,2,128]{4,2,3,1,0:T(8,128)}, u32[]{:S(2)}, u32[]{:S(2)}) collective-permute-start(f32[8,2,64,2,128]{4,2,3,1,0:T(8,128)} %bitcast.91), channel_id=1, source_target_pairs={{0,8},{4,12},{8,0},{12,4},{16,24},{20,28},{24,16},{28,20},{1,9},{5... | collective-permute-start | bytes 3145736 | tf_op jit(solution)/shard_map/ppermute | solution.py:181
  243.4 5.7 %copy-start.3 = (bf16[512,16,128]{2,1,0:T(8,128)(2,1)S(1)}, bf16[512,16,128]{2,1,0:T(8,128)(2,1)}, u32[]{:S(2)}) copy-start(bf16[512,16,128]{2,1,0:T(8,128)(2,1)} %copy-done.2) | copy-start | bytes 6291460
  244.5 53.3 %collective-permute-start.10 = (f32[8,2,64,2,128]{4,2,3,1,0:T(8,128)}, f32[8,2,64,2,128]{4,2,3,1,0:T(8,128)}, u32[]{:S(2)}, u32[]{:S(2)}) collective-permute-start(f32[8,2,64,2,128]{4,2,3,1,0:T(8,128)} %bitcast.90), channel_id=1, source_target_pairs={{0,8},{4,12},{8,0},{12,4},{16,24},{20,28},{24,16},{28,20},{1,9},{5... | collective-permute-start | bytes 3145736 | tf_op jit(solution)/shard_map/ppermute | solution.py:181
  247.4 50.4 %copy-start.5 = (f32[8,2,1,64,2,128]{5,3,2,1,4,0:T(8,128)S(1)}, f32[8,2,1,64,2,128]{5,3,2,1,4,0:T(8,128)}, u32[]{:S(2)}) copy-start(f32[8,2,1,64,2,128]{5,3,2,1,4,0:T(8,128)} %get-tuple-element.30) | copy-start | bytes 3145732
  247.4 52.8 %collective-permute-start.6 = (f32[8,64,2,128]{3,1,2,0:T(8,128)S(1)}, f32[8,64,2,128]{3,1,2,0:T(8,128)S(1)}, u32[]{:S(2)}, u32[]{:S(2)}) collective-permute-start(f32[8,64,2,128]{3,1,2,0:T(8,128)S(1)} %dynamic-slice_bitcast_fusion.3), channel_id=1, source_target_pairs={{0,16},{4,20},{8,24},{12,28},{16,0},{20,4},{24,8},{28,12},{1,17},{... | collective-permute-start | bytes 1572872 | tf_op jit(solution)/shard_map/ppermute | solution.py:181
  300.0 33.6 %collective-permute-start.11 = (f32[8,64,2,128]{3,1,2,0:T(8,128)}, f32[8,64,2,128]{3,1,2,0:T(8,128)S(1)}, u32[]{:S(2)}, u32[]{:S(2)}) collective-permute-start(f32[8,64,2,128]{3,1,2,0:T(8,128)} %dynamic-slice_bitcast_fusion.2), channel_id=1, source_target_pairs={{0,16},{4,20},{8,24},{12,28},{16,0},{20,4},{24,8},{28,12},{1,17},{... | collective-permute-start | bytes 1572872 | tf_op jit(solution)/shard_map/ppermute | solution.py:181
Sparse Core Ops, SparseCore 0:
  167.5 78.9 reduce-scatter.2
  250.1 82.4 reduce-scatter.4

commit v9 on v6

--- a/solution.py
+++ b/solution.py
@@ -154,16 +154,25 @@
 
 def gathered_spectrum(prior_part, after=None):
     where_tm = lax.axis_index("tm").astype(jnp.int32)
-    across = lax.ppermute(prior_part, "tm", [(0, 2), (2, 0), (1, 3), (3, 1)])
+    cross_pairs = [(0, 2), (2, 0), (1, 3), (3, 1)]
+    chip_pairs = [(0, 1), (1, 0), (2, 3), (3, 2)]
+    partner = lax.ppermute(prior_part, "tm", chip_pairs)
+    across = lax.ppermute(prior_part, "tm", cross_pairs)
     if after is not None:
         across, _ = lax.optimization_barrier((across, after))
-    mine = jnp.concatenate([prior_part, across], axis=1)
-    theirs = lax.ppermute(mine, "tm", [(0, 1), (1, 0), (2, 3), (3, 2)])
-    stacked = jnp.concatenate([mine, theirs], axis=1)
-    blocks = [where_tm, where_tm ^ 2, where_tm ^ 1, where_tm ^ 3]
+    partner_across = lax.ppermute(across, "tm", chip_pairs)
+    early = jnp.concatenate([prior_part, partner], axis=1)
+    late = jnp.concatenate([across, partner_across], axis=1)
+    blocks = [where_tm, where_tm ^ 1, where_tm ^ 2, where_tm ^ 3]
     steps_all = prior_part.shape[1] * len(blocks)
     table_high, _ = gathered_tables(blocks, steps_all)
-    mixed = jnp.einsum("fkrt,ptc->fkrpc", table_high, stacked, preferred_element_type=jnp.float32)
+    half = steps_all // 2
+    mixed = jnp.einsum(
+        "fkrt,ptc->fkrpc", table_high[..., :half], early, preferred_element_type=jnp.float32
+    )
+    mixed = mixed + jnp.einsum(
+        "fkrt,ptc->fkrpc", table_high[..., half:], late, preferred_element_type=jnp.float32
+    )
     return mixed.astype(jnp.bfloat16)
 
 

time: 322 us -> 381 us (1.18)
  matrix products: 37.5 us -> 76.6 us
  local copies, waits for them, and re-layouts: 38.3 us -> 61.5 us
    dot_general x2 -> x4, matrix products: 12.7 us -> 41.8 us  [the longest x2 21.7 us: gathered_spectrum(): jnp.einsum('fkrt,ptc->fkrpc', table_high[..., :half], early, preferred_el...]
    reduce_scatter x2, waiting for transfers between devices: 113 us -> 85.6 us  [green_product(): lax.psum_scatter(partial.astype(jnp.bfloat16), 'sea', scatter_dimension=1...]
    ppermute x4 -> x6, waiting for transfers between devices: 49.2 us -> 76.2 us  [the longest x2 69.6 us: gathered_spectrum(): across = lax.ppermute(prior_part, 'tm', cross_pairs)]
    dot_general x1 -> x2, local copies, waits for them, and re-layouts: 13.9 us -> 38.6 us  [the longest x1 19.3 us: gathered_spectrum(): jnp.einsum('fkrt,ptc->fkrpc', table_high[..., :half], early, preferred_el...]
    dot_general x2, matrix products: 24.8 us -> 34.8 us  [green_product(): jnp.einsum('fksp,fkrpc->fsrc', green, mixed, preferred_element_type=jnp.f...]
    concatenate x2 -> x0, other arithmetic: 5.05 us -> none  [gathered_spectrum(): mine = jnp.concatenate([prior_part, across], axis=1)]
  transfers between devices with their start and end apart: 8 -> 10, of which waited for: 6 -> 4; matrix products, arithmetic and copies ran while one was open for 38% -> 39% of each run, Pallas kernels for 0% -> 0%
where the time goes in v9:
time: 381 us; the launch traced here: 379 us
  waiting for transfers between devices  162 us (43%)
  matrix products  76.6 us (20%)
  local copies, waits for them, and re-layouts  61.5 us (16%)
  other arithmetic  55.2 us (14%)
  between operations  14.5 us (4%)
  starting transfers between devices  9.85 us (3%)
    reduce_scatter x2, waiting for transfers between devices, green_product(): lax.psum_scatter(partial.astype(jnp.bfloat16), 'sea', scatter_dimension=1...  85.6 us
    ppermute x2, waiting for transfers between devices, gathered_spectrum(): across = lax.ppermute(prior_part, 'tm', cross_pairs)  69.6 us
    dot_general x2, matrix products, green_product(): jnp.einsum('fksp,fkrpc->fsrc', green, mixed, preferred_element_type=jnp.f...  34.8 us
    add x24, other arithmetic, smooth(): state = state + weights[k] * (source - applied) / diag  29.7 us
    dot_general x2, matrix products, gathered_spectrum(): jnp.einsum('fkrt,ptc->fkrpc', table_high[..., :half], early, preferred_el...  21.7 us
    dot_general x2, matrix products, gathered_spectrum(): jnp.einsum('fkrt,ptc->fkrpc', table_high[..., half:], late, preferred_ele...  20.1 us
    dot_general x1, local copies, waits for them, and re-layouts, gathered_spectrum(): jnp.einsum('fkrt,ptc->fkrpc', table_high[..., :half], early, preferred_el...  19.3 us
    dot_general x1, local copies, waits for them, and re-layouts, gathered_spectrum(): jnp.einsum('fkrt,ptc->fkrpc', table_high[..., half:], late, preferred_ele...  19.3 us
  transfers between devices with their start and end apart: 10, of which 4 were waited for; matrix products, arithmetic and copies ran while one was open for 39% of the time, Pallas kernels for 0%

profile of v9, /device:TPU:0, one launch (start us, length us, event | category | flops | bytes accessed | tf_op | source)
XLA Modules:
  0.0 379.4 jit_solution(6252882384992228854)
XLA Ops:
  9.7 4.9 %collective-permute-start = (f32[20491]{0:T(1024)S(1)}, f32[20491]{0:T(1024)S(1)}, u32[]{:S(2)}, u32[]{:S(2)}) collective-permute-start(f32[20491]{0:T(1024)S(1)} %concatenate.53), channel_id=1, source_target_pairs={{0,4},{4,8},{8,12},{12,16},{16,20},{20,24},{24,28},{1,5},{5,9},{9,... | collective-permute-start | bytes 245900 | tf_op jit(solution)/shard_map/ppermute | solution.py:14
  17.7 3.0 fusion.7
  20.7 3.5 fusion.10
  24.1 3.5 fusion.13
  27.6 3.5 fusion.16
  31.1 3.5 fusion.19
  34.5 4.6 %fusion.51 = bf16[512,16,128]{2,1,0:T(8,128)(2,1)} fusion(f32[512,16,128]{2,1,0:T(8,128)S(1)} %fusion.19, f32[512]{0:T(512)S(1)} %get-tuple-element.13, f32[512]{0:T(512)S(1)} %get-tuple-element.49, f32[512]{0:T(512)S(1)} %get-tuple-element.12, bf16[512,16,256]{2,1,0:T(8,128)(2,1)S(1)} %copy-done), kind=kLoop, calls=%fused_computation.72 | loop fusion | flops 11534336 | bytes 8394752 | tf_op jit(solution)/shard_map/convert_element_type | solution.py:86
  43.4 1.6 collective-permute-start.3
  45.0 1.5 fusion.23
  47.0 3.4 fusion.26
  50.4 3.4 fusion.29
  53.8 3.4 fusion.32
  57.2 3.4 fusion.35
  60.7 4.6 %fusion.50 = bf16[512,16,128]{2,1,0:T(8,128)(2,1)} fusion(f32[512,16,128]{2,1,0:T(8,128)S(1)} %fusion.35, bf16[512,16,128]{2,1,0:T(8,128)(2,1)S(1)} %slice.371, f32[512]{0:T(512)S(1)} %get-tuple-element.13, f32[512]{0:T(512)S(1)} %get-tuple-element.49, f32[512]{0:T(512)S(1)} %get-tuple-element.12), kind=kLoop, calls=%fused_computation.71 | loop fusion | flops 11534336 | bytes 8394752 | tf_op jit(solution)/shard_map/convert_element_type | solution.py:86
  67.6 23.2 %collective-permute-done.3 = bf16[512,16,128]{2,1,0:T(8,128)(2,1)} collective-permute-done((bf16[512,16,128]{2,1,0:T(8,128)(2,1)}, bf16[512,16,128]{2,1,0:T(8,128)(2,1)}, u32[]{:S(2)}, u32[]{:S(2)}) %collective-permute-start.3) | collective-permute-done | bytes 2097184 | tf_op jit(solution)/shard_map/ppermute | solution.py:160
  91.8 6.5 %collective-permute-done.4 = bf16[512,16,128]{2,1,0:T(8,128)(2,1)} collective-permute-done((bf16[512,16,128]{2,1,0:T(8,128)(2,1)}, bf16[512,16,128]{2,1,0:T(8,128)(2,1)}, u32[]{:S(2)}, u32[]{:S(2)}) %collective-permute-start.4) | collective-permute-done | bytes 2097184 | tf_op jit(solution)/shard_map/ppermute | solution.py:163
  98.3 10.3 %fusion.41 = f32[16,2,2,512,128]{4,0,3,2,1:T(8,128)} fusion(bf16[512,16,128]{2,1,0:T(8,128)(2,1)} %collective-permute-done.4, bf16[512,16,128]{2,1,0:T(8,128)(2,1)} %collective-permute-done.3, bf16[16,2,2,64]{3,0,2,1:T(8,128)(2,1)S(1)} %pad_maximum_fusion.5), kind=kOutput, calls=%fused_computation.60 | convolution fusion | flops 276824064 | bytes 20979712 | tf_op jit(solution)/shard_map/fkrt,ptc->fkrpc/dot_general | solution.py:173
  108.7 12.0 %add_convert_fusion.1 = bf16[16,2,2,512,128]{4,0,3,2,1:T(8,128)(2,1)} fusion(f32[16,2,2,512,128]{4,0,3,2,1:T(8,128)} %fusion.41, bf16[512,16,128]{2,1,0:T(8,128)(2,1)S(1)} %collective-permute-done.2, bf16[512,16,128]{2,1,0:T(8,128)(2,1)} %fusion.199, bf16[16,2,2,64]{3,0,2,1:T(8,128)(2,1)S(1)} %pad_maximum_fusion.5), kind=kOutput, calls=%fused_computation.5 | convolution fusion | flops 285212672 | bytes 29368320 | tf_op jit(solution)/shard_map/fkrt,ptc->fkrpc/dot_general | solution.py:170
  120.7 12.7 %fusion.5 = bf16[16,512,2,128]{1,3,2,0:T(8,128)(2,1)} fusion(bf16[16,2,512,512]{3,2,1,0:T(8,128)(2,1)} %param.7, bf16[16,2,2,512,128]{4,0,3,2,1:T(8,128)(2,1)} %add_convert_fusion.1), kind=kOutput, calls=%fused_computation.21 | convolution fusion | flops 4297064448 | bytes 29360128 | tf_op jit(solution)/shard_map/fksp,fkrpc->fsrc/dot_general | solution.py:180
  133.4 8.1 %copy.9 = bf16[16,512,2,128]{3,0,2,1:T(8,128)(2,1)} copy(bf16[16,512,2,128]{1,3,2,0:T(8,128)(2,1)} %fusion.5) | data formatting | bytes 8388608 | tf_op jit(solution)/shard_map/convert_element_type | solution.py:181
  141.6 1.6 collective-permute-start.6
  143.1 46.4 %collective-permute-done.6 = bf16[512,16,128]{2,1,0:T(8,128)(2,1)S(1)} collective-permute-done((bf16[512,16,128]{2,1,0:T(8,128)(2,1)}, bf16[512,16,128]{2,1,0:T(8,128)(2,1)S(1)}, u32[]{:S(2)}, u32[]{:S(2)}) %collective-permute-start.6) | collective-permute-done | bytes 2097184 | tf_op jit(solution)/shard_map/ppermute | solution.py:160
  189.5 9.7 %fusion.44 = f32[16,2,2,512,128]{4,0,3,2,1:T(8,128)} fusion(bf16[512,16,128]{2,1,0:T(8,128)(2,1)S(1)} %collective-permute-done.5, bf16[512,16,128]{2,1,0:T(8,128)(2,1)} %fusion.201, bf16[16,2,2,64]{3,0,2,1:T(8,128)(2,1)S(1)} %pad_maximum_fusion.5), kind=kOutput, calls=%fused_computation.64 | convolution fusion | flops 276824064 | bytes 20979712 | tf_op jit(solution)/shard_map/fkrt,ptc->fkrpc/dot_general | solution.py:170
  199.2 19.3 %copy.19 = f32[16,2,2,512,128]{3,4,1,2,0:T(8,128)} copy(f32[16,2,2,512,128]{4,0,3,2,1:T(8,128)} %fusion.44) | data formatting | bytes 33554432 | tf_op jit(solution)/shard_map/fkrt,ptc->fkrpc/dot_general | solution.py:170
  218.6 9.7 %fusion.47 = f32[16,2,2,512,128]{4,0,3,2,1:T(8,128)} fusion(bf16[512,16,128]{2,1,0:T(8,128)(2,1)} %collective-permute-done.7, bf16[512,16,128]{2,1,0:T(8,128)(2,1)S(1)} %collective-permute-done.6, bf16[16,2,2,64]{3,0,2,1:T(8,128)(2,1)S(1)} %pad_maximum_fusion.5), kind=kOutput, calls=%fused_computation.68 | convolution fusion | flops 276824064 | bytes 20979712 | tf_op jit(solution)/shard_map/fkrt,ptc->fkrpc/dot_general | solution.py:173
  228.3 19.3 %copy.21 = f32[16,2,2,512,128]{3,4,1,2,0:T(8,128)} copy(f32[16,2,2,512,128]{4,0,3,2,1:T(8,128)} %fusion.47) | data formatting | bytes 33554432 | tf_op jit(solution)/shard_map/fkrt,ptc->fkrpc/dot_general | solution.py:173
  247.6 22.1 %fusion.6 = bf16[16,512,2,128]{1,3,2,0:T(8,128)(2,1)} fusion(bf16[16,2,512,512]{3,2,1,0:T(8,128)(2,1)} %param.7, f32[16,2,2,512,128]{3,4,1,2,0:T(8,128)} %copy.19, f32[16,2,2,512,128]{3,4,1,2,0:T(8,128)} %copy.21), kind=kOutput, calls=%fused_computation.22 | convolution fusion | flops 4305453056 | bytes 54525952 | tf_op jit(solution)/shard_map/fksp,fkrpc->fsrc/dot_general | solution.py:180
  269.6 8.0 %copy.10 = bf16[16,512,2,128]{3,0,2,1:T(8,128)(2,1)} copy(bf16[16,512,2,128]{1,3,2,0:T(8,128)(2,1)} %fusion.6) | data formatting | bytes 8388608 | tf_op jit(solution)/shard_map/convert_element_type | solution.py:181
  277.7 4.7 %pad_maximum_fusion = bf16[512,16,256]{2,1,0:T(8,128)(2,1)} fusion(bf16[512,16,128]{2,1,0:T(8,128)(2,1)} %fusion.201, bf16[512,16,128]{2,1,0:T(8,128)(2,1)} %fusion.199), kind=kLoop, calls=%fused_computation.55 | loop fusion | flops 8388608 | bytes 8388608 | tf_op jit(solution)/shard_map/concatenate | solution.py:215
  282.4 85.6 %reduce-scatter.5.cloned.1.call-done = bf16[16,64,2,128]{3,0,2,1:T(8,128)(2,1)} async-done(((bf16[16,512,2,128]{3,0,2,1:T(8,128)(2,1)}), bf16[16,64,2,128]{3,0,2,1:T(8,128)(2,1)}) %reduce-scatter.5.cloned.1.call-update) | async-done | bytes 524304 | tf_op jit(solution)/shard_map/reduce_scatter | solution.py:181
  368.0 1.4 maximum_convert_fusion
  369.4 3.2 copy.11
  (84 shorter events, 13.5 us)
Async XLA Ops:
  7.2 275.2 %reduce-scatter.3.cloned.1.call-start = ((), (), s32[]{:S(2)}) async-start(), calls=%async_computation.2 | async-start | bytes 4718592 | tf_op jit(solution)/shard_map/reduce_scatter | solution.py:181
  9.7 30.0 %collective-permute-start = (f32[20491]{0:T(1024)S(1)}, f32[20491]{0:T(1024)S(1)}, u32[]{:S(2)}, u32[]{:S(2)}) collective-permute-start(f32[20491]{0:T(1024)S(1)} %concatenate.53), channel_id=1, source_target_pairs={{0,4},{4,8},{8,12},{12,16},{16,20},{20,24},{24,28},{1,5},{5,9},{9,... | collective-permute-start | bytes 245900 | tf_op jit(solution)/shard_map/ppermute | solution.py:14
  15.4 24.1 %collective-permute-start.1 = (f32[20490]{0:T(1024)S(1)}, f32[20490]{0:T(1024)S(1)}, u32[]{:S(2)}, u32[]{:S(2)}) collective-permute-start(f32[20490]{0:T(1024)S(1)} %concatenate.55), channel_id=1, source_target_pairs={{4,0},{8,4},{12,8},{16,12},{20,16},{24,20},{28,24},{5,1},{9,5},{13... | collective-permute-start | bytes 245888 | tf_op jit(solution)/shard_map/ppermute | solution.py:19
  16.7 3.9 %copy-start = (bf16[512,16,256]{2,1,0:T(8,128)(2,1)S(1)}, bf16[512,16,256]{2,1,0:T(8,128)(2,1)}, u32[]{:S(2)}) copy-start(bf16[512,16,256]{2,1,0:T(8,128)(2,1)} %param.4) | copy-start | bytes 12582916
  39.1 0.7 copy-start.1
  39.2 0.8 copy-start.2
  43.4 47.5 %collective-permute-start.3 = (bf16[512,16,128]{2,1,0:T(8,128)(2,1)}, bf16[512,16,128]{2,1,0:T(8,128)(2,1)}, u32[]{:S(2)}, u32[]{:S(2)}) collective-permute-start(bf16[512,16,128]{2,1,0:T(8,128)(2,1)} %fusion.199), channel_id=1, source_target_pairs={{0,2},{2,0},{1,3},{3,1},{4,6},{6,4},{5,7},{7,5},{8,10},{10,8},{9,1... | collective-permute-start | bytes 6291464 | tf_op jit(solution)/shard_map/ppermute | solution.py:160
  90.9 7.5 %collective-permute-start.4 = (bf16[512,16,128]{2,1,0:T(8,128)(2,1)}, bf16[512,16,128]{2,1,0:T(8,128)(2,1)}, u32[]{:S(2)}, u32[]{:S(2)}) collective-permute-start(bf16[512,16,128]{2,1,0:T(8,128)(2,1)} %collective-permute-done.3), channel_id=1, source_target_pairs={{0,1},{1,0},{2,3},{3,2},{4,5},{5,4},{6,7},{7,6},{8,9},{9,8},{10,11... | collective-permute-start | bytes 6291464 | tf_op jit(solution)/shard_map/ppermute | solution.py:163
  90.9 17.8 %collective-permute-start.2 = (bf16[512,16,128]{2,1,0:T(8,128)(2,1)}, bf16[512,16,128]{2,1,0:T(8,128)(2,1)S(1)}, u32[]{:S(2)}, u32[]{:S(2)}) collective-permute-start(bf16[512,16,128]{2,1,0:T(8,128)(2,1)} %fusion.199), channel_id=1, source_target_pairs={{0,1},{1,0},{2,3},{3,2},{4,5},{5,4},{6,7},{7,6},{8,9},{9,8},{10,11... | collective-permute-start | bytes 6291464 | tf_op jit(solution)/shard_map/ppermute | solution.py:159
  141.5 226.5 %reduce-scatter.5.cloned.1.call-start = ((), (), s32[]{:S(2)}) async-start(), calls=%async_computation.3 | async-start | bytes 4718592 | tf_op jit(solution)/shard_map/reduce_scatter | solution.py:181
  141.6 47.9 %collective-permute-start.6 = (bf16[512,16,128]{2,1,0:T(8,128)(2,1)}, bf16[512,16,128]{2,1,0:T(8,128)(2,1)S(1)}, u32[]{:S(2)}, u32[]{:S(2)}) collective-permute-start(bf16[512,16,128]{2,1,0:T(8,128)(2,1)} %fusion.201), channel_id=1, source_target_pairs={{0,2},{2,0},{1,3},{3,1},{4,6},{6,4},{5,7},{7,5},{8,10},{10,8},{9,1... | collective-permute-start | bytes 6291464 | tf_op jit(solution)/shard_map/ppermute | solution.py:160
  143.1 46.4 %collective-permute-start.5 = (bf16[512,16,128]{2,1,0:T(8,128)(2,1)}, bf16[512,16,128]{2,1,0:T(8,128)(2,1)S(1)}, u32[]{:S(2)}, u32[]{:S(2)}) collective-permute-start(bf16[512,16,128]{2,1,0:T(8,128)(2,1)} %fusion.201), channel_id=1, source_target_pairs={{0,1},{1,0},{2,3},{3,2},{4,5},{5,4},{6,7},{7,6},{8,9},{9,8},{10,11... | collective-permute-start | bytes 6291464 | tf_op jit(solution)/shard_map/ppermute | solution.py:159
  189.5 29.1 %collective-permute-start.7 = (bf16[512,16,128]{2,1,0:T(8,128)(2,1)S(1)}, bf16[512,16,128]{2,1,0:T(8,128)(2,1)}, u32[]{:S(2)}, u32[]{:S(2)}) collective-permute-start(bf16[512,16,128]{2,1,0:T(8,128)(2,1)S(1)} %collective-permute-done.6), channel_id=1, source_target_pairs={{0,1},{1,0},{2,3},{3,2},{4,5},{5,4},{6,7},{7,6},{8,9},{9,8},{10,11... | collective-permute-start | bytes 6291464 | tf_op jit(solution)/shard_map/ppermute | solution.py:163
Sparse Core Ops, SparseCore 0:
  141.6 90.1 reduce-scatter.2
  277.8 90.1 reduce-scatter.4

commit v10 on v6

--- a/solution.py
+++ b/solution.py
@@ -154,12 +154,13 @@
 
 def gathered_spectrum(prior_part, after=None):
     where_tm = lax.axis_index("tm").astype(jnp.int32)
+    chip_pairs = [(0, 1), (1, 0), (2, 3), (3, 2)]
     across = lax.ppermute(prior_part, "tm", [(0, 2), (2, 0), (1, 3), (3, 1)])
+    partner = lax.ppermute(prior_part, "tm", chip_pairs)
     if after is not None:
         across, _ = lax.optimization_barrier((across, after))
-    mine = jnp.concatenate([prior_part, across], axis=1)
-    theirs = lax.ppermute(mine, "tm", [(0, 1), (1, 0), (2, 3), (3, 2)])
-    stacked = jnp.concatenate([mine, theirs], axis=1)
+    partner_across = lax.ppermute(across, "tm", chip_pairs)
+    stacked = jnp.concatenate([prior_part, across, partner, partner_across], axis=1)
     blocks = [where_tm, where_tm ^ 2, where_tm ^ 1, where_tm ^ 3]
     steps_all = prior_part.shape[1] * len(blocks)
     table_high, _ = gathered_tables(blocks, steps_all)

time: 322 us -> 319 us (level)
    ppermute x2, waiting for transfers between devices: 36.6 us -> 70.4 us  [gathered_spectrum(): across = lax.ppermute(prior_part, 'tm', [(0, 2), (2, 0), (1, 3), (3, 1)])]
    reduce_scatter x2, waiting for transfers between devices: 113 us -> 84.9 us  [green_product(): lax.psum_scatter(partial.astype(jnp.bfloat16), 'sea', scatter_dimension=1...]
    concatenate x2 -> x0, other arithmetic: 5.05 us -> none  [gathered_spectrum(): mine = jnp.concatenate([prior_part, across], axis=1)]
    ppermute x2 -> x4, waiting for transfers between devices: 12.7 us -> 8.1 us  [the longest x2 8.1 us: gathered_spectrum(): partner_across = lax.ppermute(across, 'tm', chip_pairs)]
  transfers between devices with their start and end apart: 8 -> 10, of which waited for: 6 -> 5; matrix products, arithmetic and copies ran while one was open for 38% -> 28% of each run, Pallas kernels for 0% -> 0%
where the time goes in v10:
time: 319 us; the launch traced here: 318 us
  waiting for transfers between devices  163 us (51%)
  other arithmetic  55.2 us (17%)
  matrix products  36.9 us (12%)
  local copies, waits for them, and re-layouts  36.7 us (12%)
  between operations  14.5 us (5%)
  starting transfers between devices  10.7 us (3%)
    reduce_scatter x2, waiting for transfers between devices, green_product(): lax.psum_scatter(partial.astype(jnp.bfloat16), 'sea', scatter_dimension=1...  84.9 us
    ppermute x2, waiting for transfers between devices, gathered_spectrum(): across = lax.ppermute(prior_part, 'tm', [(0, 2), (2, 0), (1, 3), (3, 1)])  70.4 us
    add x24, other arithmetic, smooth(): state = state + weights[k] * (source - applied) / diag  29.7 us
    dot_general x2, matrix products, green_product(): jnp.einsum('fksp,fkrpc->fsrc', green, mixed, preferred_element_type=jnp.f...  24.7 us
    convert_element_type x2, local copies, waits for them, and re-layouts, green_product(): partial.astype(jnp.bfloat16)  16.1 us
    dot_general x1, local copies, waits for them, and re-layouts, gathered_spectrum(): jnp.einsum('fkrt,ptc->fkrpc', table_high, stacked, preferred_element_type...  13.9 us
    dot_general x2, matrix products, gathered_spectrum(): jnp.einsum('fkrt,ptc->fkrpc', table_high, stacked, preferred_element_type...  12.3 us
    convert_element_type x2, other arithmetic, smooth_with_edges(): smooth(motion.astype(jnp.float32), *local_coefficients_, 0)  9.16 us
  transfers between devices with their start and end apart: 10, of which 5 were waited for; matrix products, arithmetic and copies ran while one was open for 28% of the time, Pallas kernels for 0%

profile of v10, /device:TPU:0, one launch (start us, length us, event | category | flops | bytes accessed | tf_op | source)
XLA Modules:
  0.0 317.5 jit_solution(18363942875290675835)
XLA Ops:
  9.7 1.3 collective-permute-start.1
  11.8 5.5 %collective-permute-start = (f32[20491]{0:T(1024)S(1)}, f32[20491]{0:T(1024)S(1)}, u32[]{:S(2)}, u32[]{:S(2)}) collective-permute-start(f32[20491]{0:T(1024)S(1)} %concatenate.47), channel_id=1, source_target_pairs={{0,4},{4,8},{8,12},{12,16},{16,20},{20,24},{24,28},{1,5},{5,9},{9,... | collective-permute-start | bytes 245900 | tf_op jit(solution)/shard_map/ppermute | solution.py:14
  17.4 0.9 add_add_fusion
  18.3 3.0 fusion.23
  21.3 3.5 %fusion.26 = f32[512,16,128]{2,1,0:T(8,128)S(1)} fusion(f32[512,16,128]{2,1,0:T(8,128)S(1)} %fusion.23, f32[512]{0:T(512)S(1)} %get-tuple-element.13, f32[512]{0:T(512)S(1)} %get-tuple-element.49, f32[512]{0:T(512)S(1)} %get-tuple-element.12, bf16[512,16,256]{2,1,0:T(8,128)(2,1)S(1)} %copy-done), kind=kLoop, calls=%fused_computation.42 | loop fusion | flops 10485760 | bytes 10491904 | tf_op jit(solution)/shard_map/add | solution.py:68
  24.8 3.5 %fusion.29 = f32[512,16,128]{2,1,0:T(8,128)S(1)} fusion(f32[512,16,128]{2,1,0:T(8,128)S(1)} %fusion.26, f32[512]{0:T(512)S(1)} %get-tuple-element.13, f32[512]{0:T(512)S(1)} %get-tuple-element.49, f32[512]{0:T(512)S(1)} %get-tuple-element.12, bf16[512,16,256]{2,1,0:T(8,128)(2,1)S(1)} %copy-done), kind=kLoop, calls=%fused_computation.45 | loop fusion | flops 10485760 | bytes 10491904 | tf_op jit(solution)/shard_map/add | solution.py:68
  28.2 3.5 %fusion.32 = f32[512,16,128]{2,1,0:T(8,128)S(1)} fusion(f32[512,16,128]{2,1,0:T(8,128)S(1)} %fusion.29, f32[512]{0:T(512)S(1)} %get-tuple-element.13, f32[512]{0:T(512)S(1)} %get-tuple-element.49, f32[512]{0:T(512)S(1)} %get-tuple-element.12, bf16[512,16,256]{2,1,0:T(8,128)(2,1)S(1)} %copy-done), kind=kLoop, calls=%fused_computation.48 | loop fusion | flops 10485760 | bytes 10491904 | tf_op jit(solution)/shard_map/add | solution.py:68
  31.7 3.5 %fusion.35 = f32[512,16,128]{2,1,0:T(8,128)S(1)} fusion(f32[512,16,128]{2,1,0:T(8,128)S(1)} %fusion.32, f32[512]{0:T(512)S(1)} %get-tuple-element.13, f32[512]{0:T(512)S(1)} %get-tuple-element.49, f32[512]{0:T(512)S(1)} %get-tuple-element.12, bf16[512,16,256]{2,1,0:T(8,128)(2,1)S(1)} %copy-done), kind=kLoop, calls=%fused_computation.51 | loop fusion | flops 10485760 | bytes 10491904 | tf_op jit(solution)/shard_map/add | solution.py:68
  35.2 4.6 %fusion.56 = bf16[512,16,128]{2,1,0:T(8,128)(2,1)} fusion(f32[512,16,128]{2,1,0:T(8,128)S(1)} %fusion.35, f32[512]{0:T(512)S(1)} %get-tuple-element.13, f32[512]{0:T(512)S(1)} %get-tuple-element.49, f32[512]{0:T(512)S(1)} %get-tuple-element.12, bf16[512,16,256]{2,1,0:T(8,128)(2,1)S(1)} %copy-done), kind=kLoop, calls=%fused_computation.73 | loop fusion | flops 11534336 | bytes 8394752 | tf_op jit(solution)/shard_map/convert_element_type | solution.py:86
  43.9 1.5 fusion.39
  45.5 2.1 collective-permute-start.2
  48.1 3.4 %fusion.42 = f32[512,16,128]{2,1,0:T(8,128)S(1)} fusion(f32[512,16,128]{2,1,0:T(8,128)S(1)} %fusion.39, bf16[512,16,128]{2,1,0:T(8,128)(2,1)S(1)} %slice.363, f32[512]{0:T(512)S(1)} %get-tuple-element.13, f32[512]{0:T(512)S(1)} %get-tuple-element.49, f32[512]{0:T(512)S(1)} %get-tuple-element.12), kind=kLoop, calls=%fused_computation.58 | loop fusion | flops 10485760 | bytes 10491904 | tf_op jit(solution)/shard_map/add | solution.py:68
  51.5 3.4 %fusion.45 = f32[512,16,128]{2,1,0:T(8,128)S(1)} fusion(f32[512,16,128]{2,1,0:T(8,128)S(1)} %fusion.42, bf16[512,16,128]{2,1,0:T(8,128)(2,1)S(1)} %slice.363, f32[512]{0:T(512)S(1)} %get-tuple-element.13, f32[512]{0:T(512)S(1)} %get-tuple-element.49, f32[512]{0:T(512)S(1)} %get-tuple-element.12), kind=kLoop, calls=%fused_computation.61 | loop fusion | flops 10485760 | bytes 10491904 | tf_op jit(solution)/shard_map/add | solution.py:68
  54.9 3.4 %fusion.48 = f32[512,16,128]{2,1,0:T(8,128)S(1)} fusion(f32[512,16,128]{2,1,0:T(8,128)S(1)} %fusion.45, bf16[512,16,128]{2,1,0:T(8,128)(2,1)S(1)} %slice.363, f32[512]{0:T(512)S(1)} %get-tuple-element.13, f32[512]{0:T(512)S(1)} %get-tuple-element.49, f32[512]{0:T(512)S(1)} %get-tuple-element.12), kind=kLoop, calls=%fused_computation.64 | loop fusion | flops 10485760 | bytes 10491904 | tf_op jit(solution)/shard_map/add | solution.py:68
  58.3 3.4 %fusion.51 = f32[512,16,128]{2,1,0:T(8,128)S(1)} fusion(f32[512,16,128]{2,1,0:T(8,128)S(1)} %fusion.48, bf16[512,16,128]{2,1,0:T(8,128)(2,1)S(1)} %slice.363, f32[512]{0:T(512)S(1)} %get-tuple-element.13, f32[512]{0:T(512)S(1)} %get-tuple-element.49, f32[512]{0:T(512)S(1)} %get-tuple-element.12), kind=kLoop, calls=%fused_computation.67 | loop fusion | flops 10485760 | bytes 10491904 | tf_op jit(solution)/shard_map/add | solution.py:68
  61.8 4.6 %fusion.55 = bf16[512,16,128]{2,1,0:T(8,128)(2,1)} fusion(f32[512,16,128]{2,1,0:T(8,128)S(1)} %fusion.51, bf16[512,16,128]{2,1,0:T(8,128)(2,1)S(1)} %slice.363, f32[512]{0:T(512)S(1)} %get-tuple-element.13, f32[512]{0:T(512)S(1)} %get-tuple-element.49, f32[512]{0:T(512)S(1)} %get-tuple-element.12), kind=kLoop, calls=%fused_computation.72 | loop fusion | flops 11534336 | bytes 8394752 | tf_op jit(solution)/shard_map/convert_element_type | solution.py:86
  68.8 24.3 %collective-permute-done.2 = bf16[512,16,128]{2,1,0:T(8,128)(2,1)} collective-permute-done((bf16[512,16,128]{2,1,0:T(8,128)(2,1)}, bf16[512,16,128]{2,1,0:T(8,128)(2,1)}, u32[]{:S(2)}, u32[]{:S(2)}) %collective-permute-start.2) | collective-permute-done | bytes 2097184 | tf_op jit(solution)/shard_map/ppermute | solution.py:158
  93.4 3.9 %collective-permute-done.4 = bf16[512,16,128]{2,1,0:T(8,128)(2,1)S(1)} collective-permute-done((bf16[512,16,128]{2,1,0:T(8,128)(2,1)}, bf16[512,16,128]{2,1,0:T(8,128)(2,1)S(1)}, u32[]{:S(2)}, u32[]{:S(2)}) %collective-permute-start.4) | collective-permute-done | bytes 2097184 | tf_op jit(solution)/shard_map/ppermute | solution.py:162
  97.4 6.4 %fusion.20 = bf16[16,2,2,512,128]{4,0,3,2,1:T(8,128)(2,1)} fusion(bf16[512,16,128]{2,1,0:T(8,128)(2,1)S(1)} %collective-permute-done.4, bf16[512,16,128]{2,1,0:T(8,128)(2,1)} %collective-permute-done.3, bf16[512,16,128]{2,1,0:T(8,128)(2,1)} %collective-permute-done.2, bf16[512,16,128]{2,1,0:T(8,128)(2,1)} %fusion.206, ...), kind=kOutput, calls=%fused_computation.36 | convolution fusion | flops 574619648 | bytes 16785408 | tf_op jit(solution)/shard_map/fkrt,ptc->fkrpc/dot_general | solution.py:167
  103.8 12.7 %fusion.21 = bf16[16,512,2,128]{1,3,2,0:T(8,128)(2,1)} fusion(bf16[16,2,512,512]{3,2,1,0:T(8,128)(2,1)} %param.7, bf16[16,2,2,512,128]{4,0,3,2,1:T(8,128)(2,1)} %fusion.20), kind=kOutput, calls=%fused_computation.37 | convolution fusion | flops 4297064448 | bytes 29360128 | tf_op jit(solution)/shard_map/fksp,fkrpc->fsrc/dot_general | solution.py:172
  116.5 8.0 %copy.9 = bf16[16,512,2,128]{3,0,2,1:T(8,128)(2,1)} copy(bf16[16,512,2,128]{1,3,2,0:T(8,128)(2,1)} %fusion.21) | data formatting | bytes 8388608 | tf_op jit(solution)/shard_map/convert_element_type | solution.py:173
  124.6 1.8 collective-permute-start.5
  126.4 46.2 %collective-permute-done.5 = bf16[512,16,128]{2,1,0:T(8,128)(2,1)S(1)} collective-permute-done((bf16[512,16,128]{2,1,0:T(8,128)(2,1)}, bf16[512,16,128]{2,1,0:T(8,128)(2,1)S(1)}, u32[]{:S(2)}, u32[]{:S(2)}) %collective-permute-start.5) | collective-permute-done | bytes 2097184 | tf_op jit(solution)/shard_map/ppermute | solution.py:158
  172.6 4.2 %collective-permute-done.7 = bf16[512,16,128]{2,1,0:T(8,128)(2,1)S(1)} collective-permute-done((bf16[512,16,128]{2,1,0:T(8,128)(2,1)S(1)}, bf16[512,16,128]{2,1,0:T(8,128)(2,1)S(1)}, u32[]{:S(2)}, u32[]{:S(2)}) %collective-permute-start.7) | collective-permute-done | bytes 2097184 | tf_op jit(solution)/shard_map/ppermute | solution.py:162
  176.7 5.8 %fusion.11 = bf16[16,2,2,512,128]{4,0,3,2,1:T(8,128)(2,1)} fusion(bf16[512,16,128]{2,1,0:T(8,128)(2,1)S(1)} %collective-permute-done.7, bf16[512,16,128]{2,1,0:T(8,128)(2,1)S(1)} %collective-permute-done.6, bf16[512,16,128]{2,1,0:T(8,128)(2,1)S(1)} %collective-permute-done.5, bf16[512,16,128]{2,1,0:T(8,128)(2,1)} %fusion.208, ...), kind=kOutput, calls=%fused_computation.25 | convolution fusion | flops 570425344 | bytes 16785408 | tf_op jit(solution)/shard_map/fkrt,ptc->fkrpc/dot_general | solution.py:167
  182.6 13.9 %copy.17 = bf16[16,2,2,512,128]{3,4,1,2,0:T(8,128)(2,1)} copy(bf16[16,2,2,512,128]{4,0,3,2,1:T(8,128)(2,1)} %fusion.11) | data formatting | bytes 16777216 | tf_op jit(solution)/shard_map/fkrt,ptc->fkrpc/dot_general | solution.py:167
  196.5 11.9 %fusion.22 = bf16[16,512,2,128]{1,3,2,0:T(8,128)(2,1)} fusion(bf16[16,2,512,512]{3,2,1,0:T(8,128)(2,1)} %param.7, bf16[16,2,2,512,128]{3,4,1,2,0:T(8,128)(2,1)} %copy.17), kind=kOutput, calls=%fused_computation.38 | convolution fusion | flops 4297064448 | bytes 29360128 | tf_op jit(solution)/shard_map/fksp,fkrpc->fsrc/dot_general | solution.py:172
  208.4 8.0 %copy.10 = bf16[16,512,2,128]{3,0,2,1:T(8,128)(2,1)} copy(bf16[16,512,2,128]{1,3,2,0:T(8,128)(2,1)} %fusion.22) | data formatting | bytes 8388608 | tf_op jit(solution)/shard_map/convert_element_type | solution.py:173
  216.5 4.7 %pad_maximum_fusion = bf16[512,16,256]{2,1,0:T(8,128)(2,1)} fusion(bf16[512,16,128]{2,1,0:T(8,128)(2,1)} %fusion.208, bf16[512,16,128]{2,1,0:T(8,128)(2,1)} %fusion.206), kind=kLoop, calls=%fused_computation.71 | loop fusion | flops 8388608 | bytes 8388608 | tf_op jit(solution)/shard_map/concatenate | solution.py:207
  221.2 84.9 %reduce-scatter.5.cloned.1.call-done = bf16[16,64,2,128]{3,0,2,1:T(8,128)(2,1)} async-done(((bf16[16,512,2,128]{3,0,2,1:T(8,128)(2,1)}), bf16[16,64,2,128]{3,0,2,1:T(8,128)(2,1)}) %reduce-scatter.5.cloned.1.call-update) | async-done | bytes 524304 | tf_op jit(solution)/shard_map/reduce_scatter | solution.py:173
  306.1 1.4 maximum_convert_fusion
  307.4 3.2 %copy.11 = f32[64,16,2,256]{3,2,1,0:T(2,128)} copy(f32[64,16,2,256]{3,1,2,0:T(8,128)S(1)} %maximum_convert_fusion) | data formatting | bytes 4194304
  (81 shorter events, 10.8 us)
Async XLA Ops:
  7.2 214.0 %reduce-scatter.3.cloned.1.call-start = ((), (), s32[]{:S(2)}) async-start(), calls=%async_computation.2 | async-start | bytes 4718592 | tf_op jit(solution)/shard_map/reduce_scatter | solution.py:173
  9.7 30.5 %collective-permute-start.1 = (f32[20490]{0:T(1024)S(1)}, f32[20490]{0:T(1024)S(1)}, u32[]{:S(2)}, u32[]{:S(2)}) collective-permute-start(f32[20490]{0:T(1024)S(1)} %concatenate.49), channel_id=1, source_target_pairs={{4,0},{8,4},{12,8},{16,12},{20,16},{24,20},{28,24},{5,1},{9,5},{13... | collective-permute-start | bytes 245888 | tf_op jit(solution)/shard_map/ppermute | solution.py:19
  11.8 28.5 %collective-permute-start = (f32[20491]{0:T(1024)S(1)}, f32[20491]{0:T(1024)S(1)}, u32[]{:S(2)}, u32[]{:S(2)}) collective-permute-start(f32[20491]{0:T(1024)S(1)} %concatenate.47), channel_id=1, source_target_pairs={{0,4},{4,8},{8,12},{12,16},{16,20},{20,24},{24,28},{1,5},{5,9},{9,... | collective-permute-start | bytes 245900 | tf_op jit(solution)/shard_map/ppermute | solution.py:14
  17.3 3.9 %copy-start = (bf16[512,16,256]{2,1,0:T(8,128)(2,1)S(1)}, bf16[512,16,256]{2,1,0:T(8,128)(2,1)}, u32[]{:S(2)}) copy-start(bf16[512,16,256]{2,1,0:T(8,128)(2,1)} %param.4) | copy-start | bytes 12582916
  39.8 0.7 copy-start.1
  39.8 0.8 copy-start.2
  45.5 47.5 %collective-permute-start.2 = (bf16[512,16,128]{2,1,0:T(8,128)(2,1)}, bf16[512,16,128]{2,1,0:T(8,128)(2,1)}, u32[]{:S(2)}, u32[]{:S(2)}) collective-permute-start(bf16[512,16,128]{2,1,0:T(8,128)(2,1)} %fusion.206), channel_id=1, source_target_pairs={{0,2},{2,0},{1,3},{3,1},{4,6},{6,4},{5,7},{7,5},{8,10},{10,8},{9,1... | collective-permute-start | bytes 6291464 | tf_op jit(solution)/shard_map/ppermute | solution.py:158
  47.6 45.8 %collective-permute-start.3 = (bf16[512,16,128]{2,1,0:T(8,128)(2,1)}, bf16[512,16,128]{2,1,0:T(8,128)(2,1)}, u32[]{:S(2)}, u32[]{:S(2)}) collective-permute-start(bf16[512,16,128]{2,1,0:T(8,128)(2,1)} %fusion.206), channel_id=1, source_target_pairs={{0,1},{1,0},{2,3},{3,2},{4,5},{5,4},{6,7},{7,6},{8,9},{9,8},{10,11... | collective-permute-start | bytes 6291464 | tf_op jit(solution)/shard_map/ppermute | solution.py:159
  93.0 4.4 %collective-permute-start.4 = (bf16[512,16,128]{2,1,0:T(8,128)(2,1)}, bf16[512,16,128]{2,1,0:T(8,128)(2,1)S(1)}, u32[]{:S(2)}, u32[]{:S(2)}) collective-permute-start(bf16[512,16,128]{2,1,0:T(8,128)(2,1)} %collective-permute-done.2), channel_id=1, source_target_pairs={{0,1},{1,0},{2,3},{3,2},{4,5},{5,4},{6,7},{7,6},{8,9},{9,8},{10,11... | collective-permute-start | bytes 6291464 | tf_op jit(solution)/shard_map/ppermute | solution.py:162
  124.6 181.5 %reduce-scatter.5.cloned.1.call-start = ((), (), s32[]{:S(2)}) async-start(), calls=%async_computation.3 | async-start | bytes 4718592 | tf_op jit(solution)/shard_map/reduce_scatter | solution.py:173
  124.6 47.9 %collective-permute-start.5 = (bf16[512,16,128]{2,1,0:T(8,128)(2,1)}, bf16[512,16,128]{2,1,0:T(8,128)(2,1)S(1)}, u32[]{:S(2)}, u32[]{:S(2)}) collective-permute-start(bf16[512,16,128]{2,1,0:T(8,128)(2,1)} %fusion.208), channel_id=1, source_target_pairs={{0,2},{2,0},{1,3},{3,1},{4,6},{6,4},{5,7},{7,5},{8,10},{10,8},{9,1... | collective-permute-start | bytes 6291464 | tf_op jit(solution)/shard_map/ppermute | solution.py:158
  126.4 46.2 %collective-permute-start.6 = (bf16[512,16,128]{2,1,0:T(8,128)(2,1)}, bf16[512,16,128]{2,1,0:T(8,128)(2,1)S(1)}, u32[]{:S(2)}, u32[]{:S(2)}) collective-permute-start(bf16[512,16,128]{2,1,0:T(8,128)(2,1)} %fusion.208), channel_id=1, source_target_pairs={{0,1},{1,0},{2,3},{3,2},{4,5},{5,4},{6,7},{7,6},{8,9},{9,8},{10,11... | collective-permute-start | bytes 6291464 | tf_op jit(solution)/shard_map/ppermute | solution.py:159
  172.6 4.2 %collective-permute-start.7 = (bf16[512,16,128]{2,1,0:T(8,128)(2,1)S(1)}, bf16[512,16,128]{2,1,0:T(8,128)(2,1)S(1)}, u32[]{:S(2)}, u32[]{:S(2)}) collective-permute-start(bf16[512,16,128]{2,1,0:T(8,128)(2,1)S(1)} %collective-permute-done.5), channel_id=1, source_target_pairs={{0,1},{1,0},{2,3},{3,2},{4,5},{5,4},{6,7},{7,6},{8,9},{9,8},{10,11... | collective-permute-start | bytes 6291464 | tf_op jit(solution)/shard_map/ppermute | solution.py:162
Sparse Core Ops, SparseCore 0:
  124.7 89.3 reduce-scatter.2
  218.2 87.8 reduce-scatter.4

commit v11 on v7

--- a/solution.py
+++ b/solution.py
@@ -96,11 +96,14 @@
     return total
 
 
-def smooth_with_edges(motion, halo_rows, coefficients, local_coefficients_, halo):
+def smooth_with_edges(motion, halo_rows, coefficients, local_coefficients_, halo, banded=False):
     points = motion.shape[0]
     span = 3 * halo + 1
     keep = halo + 1
-    interior = banded_smooth(motion, local_coefficients_, halo).astype(jnp.bfloat16)
+    if banded:
+        interior = banded_smooth(motion, local_coefficients_, halo).astype(jnp.bfloat16)
+    else:
+        interior = smooth(motion.astype(jnp.float32), *local_coefficients_, 0).astype(jnp.bfloat16)
     before, after = halo_rows
     left_src = jnp.concatenate([before, motion[: span - halo]]).astype(jnp.float32)
     right_src = jnp.concatenate([motion[points - span + halo :], after]).astype(jnp.float32)
@@ -171,12 +174,13 @@
 
 def gathered_spectrum(prior_part, after=None):
     where_tm = lax.axis_index("tm").astype(jnp.int32)
+    chip_pairs = [(0, 1), (1, 0), (2, 3), (3, 2)]
     across = lax.ppermute(prior_part, "tm", [(0, 2), (2, 0), (1, 3), (3, 1)])
+    partner = lax.ppermute(prior_part, "tm", chip_pairs)
     if after is not None:
         across, _ = lax.optimization_barrier((across, after))
-    mine = jnp.concatenate([prior_part, across], axis=1)
-    theirs = lax.ppermute(mine, "tm", [(0, 1), (1, 0), (2, 3), (3, 2)])
-    stacked = jnp.concatenate([mine, theirs], axis=1)
+    partner_across = lax.ppermute(across, "tm", chip_pairs)
+    stacked = jnp.concatenate([prior_part, across, partner, partner_across], axis=1)
     blocks = [where_tm, where_tm ^ 2, where_tm ^ 1, where_tm ^ 3]
     steps_all = prior_part.shape[1] * len(blocks)
     table_high, _ = gathered_tables(blocks, steps_all)
@@ -204,7 +208,7 @@
         if priors:
             source, _ = lax.optimization_barrier((source, priors[-1]))
         rows = (halo_rows[0][:, :, part], halo_rows[1][:, :, part])
-        priors.append(smooth_with_edges(source, rows, coefficients, inner, halo))
+        priors.append(smooth_with_edges(source, rows, coefficients, inner, halo, c == 0))
     sensors = []
     if lax.axis_size("tm") == 4:
         spectra = []

time: 334 us -> 314 us (0.940)
  waiting for transfers between devices: 196 us -> 177 us
    reduce_scatter x2, waiting for transfers between devices: 126 us -> 97.9 us  [green_product(): lax.psum_scatter(partial.astype(jnp.bfloat16), 'sea', scatter_dimension=1...]
    convert_element_type x2 -> x1, other arithmetic: 27.7 us -> 13.1 us  [smooth_with_edges(): banded_smooth(motion, local_coefficients_, halo).astype(jnp.bfloat16)]
    ppermute x2, waiting for transfers between devices: 56.6 us -> 70.4 us  [gathered_spectrum(): across = lax.ppermute(prior_part, 'tm', [(0, 2), (2, 0), (1, 3), (3, 1)])]
    add x20 -> x24, other arithmetic: 2.62 us -> 16.2 us  [smooth(): state = state + weights[k] * (source - applied) / diag]
    concatenate x2 -> x0, other arithmetic: 5.7 us -> none  [gathered_spectrum(): mine = jnp.concatenate([prior_part, across], axis=1)]
    ppermute x2 -> x4, waiting for transfers between devices: 12.7 us -> 8.1 us  [the longest x2 8.1 us: gathered_spectrum(): partner_across = lax.ppermute(across, 'tm', chip_pairs)]
    convert_element_type x0 -> x1, other arithmetic: none -> 4.57 us  [smooth_with_edges(): smooth(motion.astype(jnp.float32), *local_coefficients_, 0)]
  transfers between devices with their start and end apart: 8 -> 10, of which waited for: 6 -> 6; matrix products, arithmetic and copies ran while one was open for 25% -> 23% of each run, Pallas kernels for 0% -> 0%
where the time goes in v11:
time: 314 us
  waiting for transfers between devices  177 us (56%)
  other arithmetic  46.8 us (15%)
  matrix products  37.6 us (12%)
  local copies, waits for them, and re-layouts  27.5 us (9%)
  between operations  14.5 us (5%)
  starting transfers between devices  10.7 us (3%)
    reduce_scatter x2, waiting for transfers between devices, green_product(): lax.psum_scatter(partial.astype(jnp.bfloat16), 'sea', scatter_dimension=1...  97.9 us
    ppermute x2, waiting for transfers between devices, gathered_spectrum(): across = lax.ppermute(prior_part, 'tm', [(0, 2), (2, 0), (1, 3), (3, 1)])  70.4 us
    dot_general x2, matrix products, green_product(): jnp.einsum('fksp,fkrpc->fsrc', green, mixed, preferred_element_type=jnp.f...  25.6 us
    add x24, other arithmetic, smooth(): state = state + weights[k] * (source - applied) / diag  16.2 us
    convert_element_type x2, local copies, waits for them, and re-layouts, green_product(): partial.astype(jnp.bfloat16)  16.1 us
    convert_element_type x1, other arithmetic, smooth_with_edges(): banded_smooth(motion, local_coefficients_, halo).astype(jnp.bfloat16)  13.1 us
    dot_general x2, matrix products, gathered_spectrum(): jnp.einsum('fkrt,ptc->fkrpc', table_high, stacked, preferred_element_type...  12 us
    ppermute x2, waiting for transfers between devices, gathered_spectrum(): partner_across = lax.ppermute(across, 'tm', chip_pairs)  8.1 us
  transfers between devices with their start and end apart: 10, of which 6 were waited for; matrix products, arithmetic and copies ran while one was open for 23% of the time, Pallas kernels for 0%

profile of v11, /device:TPU:0, one launch (start us, length us, event | category | flops | bytes accessed | tf_op | source)
XLA Modules:
  0.0 313.5 jit_solution(8294764455317295214)
XLA Ops:
  7.2 0.8 slice_convert_fusion.3
  8.1 0.8 fusion.304
  9.7 1.3 collective-permute-start.1
  11.0 0.8 slice.359
  11.8 5.5 %collective-permute-start = (f32[20491]{0:T(1024)S(1)}, f32[20491]{0:T(1024)S(1)}, u32[]{:S(2)}, u32[]{:S(2)}) collective-permute-start(f32[20491]{0:T(1024)S(1)} %concatenate.47), channel_id=1, source_target_pairs={{0,4},{4,8},{8,12},{12,16},{16,20},{20,24},{24,28},{1,5},{5,9},{9,... | collective-permute-start | bytes 245900 | tf_op jit(solution)/shard_map/ppermute | solution.py:14
  17.5 4.3 %fusion.295 = (bf16[512,16,128]{2,1,0:T(8,128)(2,1)}, bf16[512,16,128]{2,1,0:T(8,128)(2,1)S(1)}) fusion(bf16[512,16,256]{2,1,0:T(8,128)(2,1)} %param.4), kind=kLoop, calls=%fused_computation.466 | loop fusion | bytes 8388608 | tf_op jit(solution)/shard_map/slice | solution.py:207
  22.4 13.1 %add_convert_fusion = bf16[512,16,128]{2,1,0:T(8,128)(2,1)} fusion(bf16[512,16,128]{2,1,0:T(8,128)(2,1)} %get-tuple-element.31, f32[512]{0:T(512)S(1)} %get-tuple-element.24, f32[512]{0:T(512)S(1)} %get-tuple-element.23, f32[512]{0:T(512)S(1)} %get-tuple-element.22, f32[512]{0:T(512)S(1)} %get-tuple-element.21, f32[512]{0:T(512)S(1)} %get-tuple-element.20, ...), kind=kLoop, calls=%fused_computation.51 | loop fusion | flops 34603008 | bytes 4216832 | tf_op jit(solution)/shard_map/convert_element_type | solution.py:104
  35.5 0.8 fusion.294
  38.6 0.7 fusion.235
  40.0 1.5 fusion.24
  41.6 2.1 collective-permute-start.2
  44.2 3.4 %fusion.27 = f32[512,16,128]{2,1,0:T(8,128)S(1)} fusion(f32[512,16,128]{2,1,0:T(8,128)S(1)} %fusion.24, bf16[512,16,128]{2,1,0:T(8,128)(2,1)S(1)} %get-tuple-element.5, f32[512]{0:T(512)S(1)} %get-tuple-element.26, f32[512]{0:T(512)S(1)} %get-tuple-element.64, f32[512]{0:T(512)S(1)} %get-tuple-element.25), kind=kLoop, calls=%fused_computation.37 | loop fusion | flops 10485760 | bytes 10491904 | tf_op jit(solution)/shard_map/add | solution.py:68
  47.6 3.4 %fusion.30 = f32[512,16,128]{2,1,0:T(8,128)S(1)} fusion(f32[512,16,128]{2,1,0:T(8,128)S(1)} %fusion.27, bf16[512,16,128]{2,1,0:T(8,128)(2,1)S(1)} %get-tuple-element.5, f32[512]{0:T(512)S(1)} %get-tuple-element.26, f32[512]{0:T(512)S(1)} %get-tuple-element.64, f32[512]{0:T(512)S(1)} %get-tuple-element.25), kind=kLoop, calls=%fused_computation.40 | loop fusion | flops 10485760 | bytes 10491904 | tf_op jit(solution)/shard_map/add | solution.py:68
  51.0 3.4 %fusion.33 = f32[512,16,128]{2,1,0:T(8,128)S(1)} fusion(f32[512,16,128]{2,1,0:T(8,128)S(1)} %fusion.30, bf16[512,16,128]{2,1,0:T(8,128)(2,1)S(1)} %get-tuple-element.5, f32[512]{0:T(512)S(1)} %get-tuple-element.26, f32[512]{0:T(512)S(1)} %get-tuple-element.64, f32[512]{0:T(512)S(1)} %get-tuple-element.25), kind=kLoop, calls=%fused_computation.43 | loop fusion | flops 10485760 | bytes 10491904 | tf_op jit(solution)/shard_map/add | solution.py:68
  54.4 3.4 %fusion.36 = f32[512,16,128]{2,1,0:T(8,128)S(1)} fusion(f32[512,16,128]{2,1,0:T(8,128)S(1)} %fusion.33, bf16[512,16,128]{2,1,0:T(8,128)(2,1)S(1)} %get-tuple-element.5, f32[512]{0:T(512)S(1)} %get-tuple-element.26, f32[512]{0:T(512)S(1)} %get-tuple-element.64, f32[512]{0:T(512)S(1)} %get-tuple-element.25), kind=kLoop, calls=%fused_computation.46 | loop fusion | flops 10485760 | bytes 10491904 | tf_op jit(solution)/shard_map/add | solution.py:68
  57.9 4.6 %fusion.40 = bf16[512,16,128]{2,1,0:T(8,128)(2,1)} fusion(f32[512,16,128]{2,1,0:T(8,128)S(1)} %fusion.36, bf16[512,16,128]{2,1,0:T(8,128)(2,1)S(1)} %get-tuple-element.5, f32[512]{0:T(512)S(1)} %get-tuple-element.26, f32[512]{0:T(512)S(1)} %get-tuple-element.64, f32[512]{0:T(512)S(1)} %get-tuple-element.25), kind=kLoop, calls=%fused_computation.52 | loop fusion | flops 11534336 | bytes 8394752 | tf_op jit(solution)/shard_map/convert_element_type | solution.py:106
  64.9 24.3 %collective-permute-done.2 = bf16[512,16,128]{2,1,0:T(8,128)(2,1)} collective-permute-done((bf16[512,16,128]{2,1,0:T(8,128)(2,1)}, bf16[512,16,128]{2,1,0:T(8,128)(2,1)}, u32[]{:S(2)}, u32[]{:S(2)}) %collective-permute-start.2) | collective-permute-done | bytes 2097184 | tf_op jit(solution)/shard_map/ppermute | solution.py:178
  89.5 3.9 %collective-permute-done.4 = bf16[512,16,128]{2,1,0:T(8,128)(2,1)S(1)} collective-permute-done((bf16[512,16,128]{2,1,0:T(8,128)(2,1)}, bf16[512,16,128]{2,1,0:T(8,128)(2,1)S(1)}, u32[]{:S(2)}, u32[]{:S(2)}) %collective-permute-start.4) | collective-permute-done | bytes 2097184 | tf_op jit(solution)/shard_map/ppermute | solution.py:182
  93.5 6.3 %fusion.21 = bf16[16,2,2,512,128]{4,0,3,2,1:T(8,128)(2,1)} fusion(bf16[512,16,128]{2,1,0:T(8,128)(2,1)S(1)} %collective-permute-done.4, bf16[512,16,128]{2,1,0:T(8,128)(2,1)} %collective-permute-done.3, bf16[512,16,128]{2,1,0:T(8,128)(2,1)} %collective-permute-done.2, bf16[512,16,128]{2,1,0:T(8,128)(2,1)} %fusion.236, ...), kind=kOutput, calls=%fused_computation.31 | convolution fusion | flops 574619648 | bytes 16785408 | tf_op jit(solution)/shard_map/fkrt,ptc->fkrpc/dot_general | solution.py:187
  99.8 12.7 %fusion.22 = bf16[16,512,2,128]{1,3,2,0:T(8,128)(2,1)} fusion(bf16[16,2,512,512]{3,2,1,0:T(8,128)(2,1)} %param.7, bf16[16,2,2,512,128]{4,0,3,2,1:T(8,128)(2,1)} %fusion.21), kind=kOutput, calls=%fused_computation.32 | convolution fusion | flops 4297064448 | bytes 29360128 | tf_op jit(solution)/shard_map/fksp,fkrpc->fsrc/dot_general | solution.py:192
  112.5 8.1 %copy.13 = bf16[16,512,2,128]{3,0,2,1:T(8,128)(2,1)} copy(bf16[16,512,2,128]{1,3,2,0:T(8,128)(2,1)} %fusion.22) | data formatting | bytes 8388608 | tf_op jit(solution)/shard_map/convert_element_type | solution.py:193
  120.7 1.8 collective-permute-start.5
  122.5 46.2 %collective-permute-done.5 = bf16[512,16,128]{2,1,0:T(8,128)(2,1)S(1)} collective-permute-done((bf16[512,16,128]{2,1,0:T(8,128)(2,1)}, bf16[512,16,128]{2,1,0:T(8,128)(2,1)S(1)}, u32[]{:S(2)}, u32[]{:S(2)}) %collective-permute-start.5) | collective-permute-done | bytes 2097184 | tf_op jit(solution)/shard_map/ppermute | solution.py:178
  168.6 4.2 %collective-permute-done.7 = bf16[512,16,128]{2,1,0:T(8,128)(2,1)S(1)} collective-permute-done((bf16[512,16,128]{2,1,0:T(8,128)(2,1)S(1)}, bf16[512,16,128]{2,1,0:T(8,128)(2,1)S(1)}, u32[]{:S(2)}, u32[]{:S(2)}) %collective-permute-start.7) | collective-permute-done | bytes 2097184 | tf_op jit(solution)/shard_map/ppermute | solution.py:182
  172.8 5.7 %fusion.20 = bf16[16,2,2,512,128]{4,0,3,2,1:T(8,128)(2,1)} fusion(bf16[512,16,128]{2,1,0:T(8,128)(2,1)S(1)} %collective-permute-done.7, bf16[512,16,128]{2,1,0:T(8,128)(2,1)S(1)} %collective-permute-done.6, bf16[512,16,128]{2,1,0:T(8,128)(2,1)S(1)} %collective-permute-done.5, bf16[512,16,128]{2,1,0:T(8,128)(2,1)} %fusion.238, ...), kind=kOutput, calls=%fused_computation.30 | convolution fusion | flops 574619648 | bytes 16785408 | tf_op jit(solution)/shard_map/fkrt,ptc->fkrpc/dot_general | solution.py:187
  178.5 12.8 %fusion.23 = bf16[16,512,2,128]{1,3,2,0:T(8,128)(2,1)} fusion(bf16[16,2,512,512]{3,2,1,0:T(8,128)(2,1)} %param.7, bf16[16,2,2,512,128]{4,0,3,2,1:T(8,128)(2,1)} %fusion.20), kind=kOutput, calls=%fused_computation.33 | convolution fusion | flops 4297064448 | bytes 29360128 | tf_op jit(solution)/shard_map/fksp,fkrpc->fsrc/dot_general | solution.py:192
  191.3 8.0 %copy.15 = bf16[16,512,2,128]{3,0,2,1:T(8,128)(2,1)} copy(bf16[16,512,2,128]{1,3,2,0:T(8,128)(2,1)} %fusion.23) | data formatting | bytes 8388608 | tf_op jit(solution)/shard_map/convert_element_type | solution.py:193
  199.4 4.8 %pad_maximum_fusion = bf16[512,16,256]{2,1,0:T(8,128)(2,1)} fusion(bf16[512,16,128]{2,1,0:T(8,128)(2,1)} %fusion.238, bf16[512,16,128]{2,1,0:T(8,128)(2,1)} %fusion.236), kind=kLoop, calls=%fused_computation.50 | loop fusion | flops 8388608 | bytes 8388608 | tf_op jit(solution)/shard_map/concatenate | solution.py:227
  204.1 6.1 %reduce-scatter.3.cloned.1.call-done = bf16[16,64,2,128]{3,0,2,1:T(8,128)(2,1)} async-done(((bf16[16,512,2,128]{3,0,2,1:T(8,128)(2,1)}), bf16[16,64,2,128]{3,0,2,1:T(8,128)(2,1)}) %reduce-scatter.3.cloned.1.call-update) | async-done | bytes 524304 | tf_op jit(solution)/shard_map/reduce_scatter | solution.py:193
  210.2 91.9 %reduce-scatter.5.cloned.1.call-done = bf16[16,64,2,128]{3,0,2,1:T(8,128)(2,1)} async-done(((bf16[16,512,2,128]{3,0,2,1:T(8,128)(2,1)}), bf16[16,64,2,128]{3,0,2,1:T(8,128)(2,1)}) %reduce-scatter.5.cloned.1.call-update) | async-done | bytes 524304 | tf_op jit(solution)/shard_map/reduce_scatter | solution.py:193
  302.1 1.4 maximum_convert_fusion
  303.5 3.2 %copy.16 = f32[64,16,2,256]{3,2,1,0:T(2,128)} copy(f32[64,16,2,256]{3,1,2,0:T(8,128)S(1)} %maximum_convert_fusion) | data formatting | bytes 4194304
  (85 shorter events, 7.9 us)
Async XLA Ops:
  7.2 203.0 %reduce-scatter.3.cloned.1.call-start = ((), (), s32[]{:S(2)}) async-start(), calls=%async_computation.2 | async-start | bytes 4718592 | tf_op jit(solution)/shard_map/reduce_scatter | solution.py:193
  9.7 26.7 %collective-permute-start.1 = (f32[20490]{0:T(1024)S(1)}, f32[20490]{0:T(1024)S(1)}, u32[]{:S(2)}, u32[]{:S(2)}) collective-permute-start(f32[20490]{0:T(1024)S(1)} %concatenate.49), channel_id=1, source_target_pairs={{4,0},{8,4},{12,8},{16,12},{20,16},{24,20},{28,24},{5,1},{9,5},{13... | collective-permute-start | bytes 245888 | tf_op jit(solution)/shard_map/ppermute | solution.py:19
  11.8 24.7 %collective-permute-start = (f32[20491]{0:T(1024)S(1)}, f32[20491]{0:T(1024)S(1)}, u32[]{:S(2)}, u32[]{:S(2)}) collective-permute-start(f32[20491]{0:T(1024)S(1)} %concatenate.47), channel_id=1, source_target_pairs={{0,4},{4,8},{8,12},{12,16},{16,20},{20,24},{24,28},{1,5},{5,9},{9,... | collective-permute-start | bytes 245900 | tf_op jit(solution)/shard_map/ppermute | solution.py:14
  17.4 4.3 %copy-start = (f32[512]{0:T(512)S(1)}, f32[512]{0:T(512)}, u32[]{:S(2)}) copy-start(f32[512]{0:T(512)} %param.5) | copy-start | bytes 6148
  17.5 4.3 %copy-start.1 = (f32[512]{0:T(512)S(1)}, f32[512]{0:T(512)}, u32[]{:S(2)}) copy-start(f32[512]{0:T(512)} %param.6) | copy-start | bytes 6148
  41.6 47.5 %collective-permute-start.2 = (bf16[512,16,128]{2,1,0:T(8,128)(2,1)}, bf16[512,16,128]{2,1,0:T(8,128)(2,1)}, u32[]{:S(2)}, u32[]{:S(2)}) collective-permute-start(bf16[512,16,128]{2,1,0:T(8,128)(2,1)} %fusion.236), channel_id=1, source_target_pairs={{0,2},{2,0},{1,3},{3,1},{4,6},{6,4},{5,7},{7,5},{8,10},{10,8},{9,1... | collective-permute-start | bytes 6291464 | tf_op jit(solution)/shard_map/ppermute | solution.py:178
  43.7 45.8 %collective-permute-start.3 = (bf16[512,16,128]{2,1,0:T(8,128)(2,1)}, bf16[512,16,128]{2,1,0:T(8,128)(2,1)}, u32[]{:S(2)}, u32[]{:S(2)}) collective-permute-start(bf16[512,16,128]{2,1,0:T(8,128)(2,1)} %fusion.236), channel_id=1, source_target_pairs={{0,1},{1,0},{2,3},{3,2},{4,5},{5,4},{6,7},{7,6},{8,9},{9,8},{10,11... | collective-permute-start | bytes 6291464 | tf_op jit(solution)/shard_map/ppermute | solution.py:179
  89.1 4.4 %collective-permute-start.4 = (bf16[512,16,128]{2,1,0:T(8,128)(2,1)}, bf16[512,16,128]{2,1,0:T(8,128)(2,1)S(1)}, u32[]{:S(2)}, u32[]{:S(2)}) collective-permute-start(bf16[512,16,128]{2,1,0:T(8,128)(2,1)} %collective-permute-done.2), channel_id=1, source_target_pairs={{0,1},{1,0},{2,3},{3,2},{4,5},{5,4},{6,7},{7,6},{8,9},{9,8},{10,11... | collective-permute-start | bytes 6291464 | tf_op jit(solution)/shard_map/ppermute | solution.py:182
  120.6 181.4 %reduce-scatter.5.cloned.1.call-start = ((), (), s32[]{:S(2)}) async-start(), calls=%async_computation.3 | async-start | bytes 4718592 | tf_op jit(solution)/shard_map/reduce_scatter | solution.py:193
  120.7 47.9 %collective-permute-start.5 = (bf16[512,16,128]{2,1,0:T(8,128)(2,1)}, bf16[512,16,128]{2,1,0:T(8,128)(2,1)S(1)}, u32[]{:S(2)}, u32[]{:S(2)}) collective-permute-start(bf16[512,16,128]{2,1,0:T(8,128)(2,1)} %fusion.238), channel_id=1, source_target_pairs={{0,2},{2,0},{1,3},{3,1},{4,6},{6,4},{5,7},{7,5},{8,10},{10,8},{9,1... | collective-permute-start | bytes 6291464 | tf_op jit(solution)/shard_map/ppermute | solution.py:178
  122.5 46.2 %collective-permute-start.6 = (bf16[512,16,128]{2,1,0:T(8,128)(2,1)}, bf16[512,16,128]{2,1,0:T(8,128)(2,1)S(1)}, u32[]{:S(2)}, u32[]{:S(2)}) collective-permute-start(bf16[512,16,128]{2,1,0:T(8,128)(2,1)} %fusion.238), channel_id=1, source_target_pairs={{0,1},{1,0},{2,3},{3,2},{4,5},{5,4},{6,7},{7,6},{8,9},{9,8},{10,11... | collective-permute-start | bytes 6291464 | tf_op jit(solution)/shard_map/ppermute | solution.py:179
  168.6 4.2 %collective-permute-start.7 = (bf16[512,16,128]{2,1,0:T(8,128)(2,1)S(1)}, bf16[512,16,128]{2,1,0:T(8,128)(2,1)S(1)}, u32[]{:S(2)}, u32[]{:S(2)}) collective-permute-start(bf16[512,16,128]{2,1,0:T(8,128)(2,1)S(1)} %collective-permute-done.5), channel_id=1, source_target_pairs={{0,1},{1,0},{2,3},{3,2},{4,5},{5,4},{6,7},{7,6},{8,9},{9,8},{10,11... | collective-permute-start | bytes 6291464 | tf_op jit(solution)/shard_map/ppermute | solution.py:182
Sparse Core Ops, SparseCore 0:
  120.8 89.3 reduce-scatter.2
  214.3 87.7 reduce-scatter.4

commit v12 on v11

--- a/solution.py
+++ b/solution.py
@@ -87,10 +87,11 @@
     probe = (rows[:, None] % width == lanes[None, :]).astype(jnp.float32)[:, None, :]
     response = smooth(probe, *coefficients, 0)[:, 0, :]
     padded = jnp.pad(motion, ((halo, halo), (0, 0), (0, 0)))
+    picks = (rows[None, :, None] + lanes[:, None, None] - halo) % width == lanes[None, None, :]
+    bands = lax.optimization_barrier(jnp.sum(jnp.where(picks, response[None], 0.0), axis=2))
     total = None
     for offset in range(-halo, halo + 1):
-        pick = (rows[:, None] + offset) % width == lanes[None, :]
-        band = jnp.sum(jnp.where(pick, response, 0.0), axis=1)[:, None, None]
+        band = bands[offset + halo][:, None, None]
         term = band * padded[halo + offset : halo + offset + points].astype(jnp.float32)
         total = term if total is None else total + term
     return total

time: 314 us -> 314 us (level)
  no operation moved by 1% of the time
where the time goes in v12:
time: 314 us
  waiting for transfers between devices  176 us (56%)
  other arithmetic  46.7 us (15%)
  matrix products  37.8 us (12%)
  local copies, waits for them, and re-layouts  27.5 us (9%)
  between operations  14.5 us (5%)
  starting transfers between devices  10.7 us (3%)
    reduce_scatter x2, waiting for transfers between devices, green_product(): lax.psum_scatter(partial.astype(jnp.bfloat16), 'sea', scatter_dimension=1...  97.8 us
    ppermute x2, waiting for transfers between devices, gathered_spectrum(): across = lax.ppermute(prior_part, 'tm', [(0, 2), (2, 0), (1, 3), (3, 1)])  70.4 us
    dot_general x2, matrix products, green_product(): jnp.einsum('fksp,fkrpc->fsrc', green, mixed, preferred_element_type=jnp.f...  25.6 us
    add x24, other arithmetic, smooth(): state = state + weights[k] * (source - applied) / diag  16.2 us
    convert_element_type x2, local copies, waits for them, and re-layouts, green_product(): partial.astype(jnp.bfloat16)  16.2 us
    convert_element_type x1, other arithmetic, smooth_with_edges(): banded_smooth(motion, local_coefficients_, halo).astype(jnp.bfloat16)  13.2 us
    dot_general x2, matrix products, gathered_spectrum(): jnp.einsum('fkrt,ptc->fkrpc', table_high, stacked, preferred_element_type...  12.2 us
    ppermute x2, waiting for transfers between devices, gathered_spectrum(): partner_across = lax.ppermute(across, 'tm', chip_pairs)  8.1 us
  transfers between devices with their start and end apart: 10, of which 6 were waited for; matrix products, arithmetic and copies ran while one was open for 23% of the time, Pallas kernels for 0%

profile of v12, /device:TPU:0, one launch (start us, length us, event | category | flops | bytes accessed | tf_op | source)
XLA Modules:
  0.0 313.7 jit_solution(6375338516091630836)
XLA Ops:
  7.2 0.8 slice_convert_fusion.3
  8.1 0.8 fusion.268
  9.7 1.3 collective-permute-start.1
  11.0 0.8 slice.403
  11.8 5.5 %collective-permute-start = (f32[20491]{0:T(1024)S(1)}, f32[20491]{0:T(1024)S(1)}, u32[]{:S(2)}, u32[]{:S(2)}) collective-permute-start(f32[20491]{0:T(1024)S(1)} %concatenate.47), channel_id=1, source_target_pairs={{0,4},{4,8},{8,12},{12,16},{16,20},{20,24},{24,28},{1,5},{5,9},{9,... | collective-permute-start | bytes 245900 | tf_op jit(solution)/shard_map/ppermute | solution.py:14
  17.4 4.3 %fusion.258 = (bf16[512,16,128]{2,1,0:T(8,128)(2,1)}, bf16[512,16,128]{2,1,0:T(8,128)(2,1)S(1)}) fusion(bf16[512,16,256]{2,1,0:T(8,128)(2,1)} %param.4), kind=kLoop, calls=%fused_computation.391 | loop fusion | bytes 8388608 | tf_op jit(solution)/shard_map/slice | solution.py:208
  22.4 13.2 %add_convert_fusion = bf16[512,16,128]{2,1,0:T(8,128)(2,1)} fusion(bf16[512,16,128]{2,1,0:T(8,128)(2,1)} %get-tuple-element.20, f32[512]{0:T(512)S(1)} %bitcast.82, f32[512]{0:T(512)S(1)} %bitcast.83, f32[512]{0:T(512)S(1)} %bitcast.84, f32[512]{0:T(512)S(1)} %bitcast.85, f32[512]{0:T(512)S(1)} %bitcast.86, f32[512]{0:T(512)S(1)} %bitcast.87, ...), kind=kLoop, calls=%fused_computation.51 | loop fusion | flops 34603008 | bytes 4216832 | tf_op jit(solution)/shard_map/convert_element_type | solution.py:105
  35.5 0.8 fusion.257
  40.0 1.5 fusion.24
  41.6 2.1 collective-permute-start.2
  44.2 3.4 %fusion.27 = f32[512,16,128]{2,1,0:T(8,128)S(1)} fusion(f32[512,16,128]{2,1,0:T(8,128)S(1)} %fusion.24, bf16[512,16,128]{2,1,0:T(8,128)(2,1)S(1)} %get-tuple-element.5, f32[512]{0:T(512)S(1)} %get-tuple-element.15, f32[512]{0:T(512)S(1)} %get-tuple-element.64, f32[512]{0:T(512)S(1)} %get-tuple-element.14), kind=kLoop, calls=%fused_computation.37 | loop fusion | flops 10485760 | bytes 10491904 | tf_op jit(solution)/shard_map/add | solution.py:68
  47.6 3.4 %fusion.30 = f32[512,16,128]{2,1,0:T(8,128)S(1)} fusion(f32[512,16,128]{2,1,0:T(8,128)S(1)} %fusion.27, bf16[512,16,128]{2,1,0:T(8,128)(2,1)S(1)} %get-tuple-element.5, f32[512]{0:T(512)S(1)} %get-tuple-element.15, f32[512]{0:T(512)S(1)} %get-tuple-element.64, f32[512]{0:T(512)S(1)} %get-tuple-element.14), kind=kLoop, calls=%fused_computation.40 | loop fusion | flops 10485760 | bytes 10491904 | tf_op jit(solution)/shard_map/add | solution.py:68
  51.0 3.4 %fusion.33 = f32[512,16,128]{2,1,0:T(8,128)S(1)} fusion(f32[512,16,128]{2,1,0:T(8,128)S(1)} %fusion.30, bf16[512,16,128]{2,1,0:T(8,128)(2,1)S(1)} %get-tuple-element.5, f32[512]{0:T(512)S(1)} %get-tuple-element.15, f32[512]{0:T(512)S(1)} %get-tuple-element.64, f32[512]{0:T(512)S(1)} %get-tuple-element.14), kind=kLoop, calls=%fused_computation.43 | loop fusion | flops 10485760 | bytes 10491904 | tf_op jit(solution)/shard_map/add | solution.py:68
  54.4 3.4 %fusion.36 = f32[512,16,128]{2,1,0:T(8,128)S(1)} fusion(f32[512,16,128]{2,1,0:T(8,128)S(1)} %fusion.33, bf16[512,16,128]{2,1,0:T(8,128)(2,1)S(1)} %get-tuple-element.5, f32[512]{0:T(512)S(1)} %get-tuple-element.15, f32[512]{0:T(512)S(1)} %get-tuple-element.64, f32[512]{0:T(512)S(1)} %get-tuple-element.14), kind=kLoop, calls=%fused_computation.46 | loop fusion | flops 10485760 | bytes 10491904 | tf_op jit(solution)/shard_map/add | solution.py:68
  57.9 4.6 %fusion.40 = bf16[512,16,128]{2,1,0:T(8,128)(2,1)} fusion(f32[512,16,128]{2,1,0:T(8,128)S(1)} %fusion.36, bf16[512,16,128]{2,1,0:T(8,128)(2,1)S(1)} %get-tuple-element.5, f32[512]{0:T(512)S(1)} %get-tuple-element.15, f32[512]{0:T(512)S(1)} %get-tuple-element.64, f32[512]{0:T(512)S(1)} %get-tuple-element.14), kind=kLoop, calls=%fused_computation.52 | loop fusion | flops 11534336 | bytes 8394752 | tf_op jit(solution)/shard_map/convert_element_type | solution.py:107
  62.7 0.7 fusion.230
  64.8 24.3 %collective-permute-done.2 = bf16[512,16,128]{2,1,0:T(8,128)(2,1)} collective-permute-done((bf16[512,16,128]{2,1,0:T(8,128)(2,1)}, bf16[512,16,128]{2,1,0:T(8,128)(2,1)}, u32[]{:S(2)}, u32[]{:S(2)}) %collective-permute-start.2) | collective-permute-done | bytes 2097184 | tf_op jit(solution)/shard_map/ppermute | solution.py:179
  89.5 3.9 %collective-permute-done.4 = bf16[512,16,128]{2,1,0:T(8,128)(2,1)S(1)} collective-permute-done((bf16[512,16,128]{2,1,0:T(8,128)(2,1)}, bf16[512,16,128]{2,1,0:T(8,128)(2,1)S(1)}, u32[]{:S(2)}, u32[]{:S(2)}) %collective-permute-start.4) | collective-permute-done | bytes 2097184 | tf_op jit(solution)/shard_map/ppermute | solution.py:183
  93.5 6.4 %fusion.21 = bf16[16,2,2,512,128]{4,0,3,2,1:T(8,128)(2,1)} fusion(bf16[512,16,128]{2,1,0:T(8,128)(2,1)S(1)} %collective-permute-done.4, bf16[512,16,128]{2,1,0:T(8,128)(2,1)} %collective-permute-done.3, bf16[512,16,128]{2,1,0:T(8,128)(2,1)} %collective-permute-done.2, bf16[512,16,128]{2,1,0:T(8,128)(2,1)} %fusion.229, ...), kind=kOutput, calls=%fused_computation.31 | convolution fusion | flops 574619648 | bytes 16785408 | tf_op jit(solution)/shard_map/fkrt,ptc->fkrpc/dot_general | solution.py:188
  99.9 12.7 %fusion.22 = bf16[16,512,2,128]{1,3,2,0:T(8,128)(2,1)} fusion(bf16[16,2,512,512]{3,2,1,0:T(8,128)(2,1)} %param.7, bf16[16,2,2,512,128]{4,0,3,2,1:T(8,128)(2,1)} %fusion.21), kind=kOutput, calls=%fused_computation.32 | convolution fusion | flops 4297064448 | bytes 29360128 | tf_op jit(solution)/shard_map/fksp,fkrpc->fsrc/dot_general | solution.py:193
  112.6 8.1 %copy.13 = bf16[16,512,2,128]{3,0,2,1:T(8,128)(2,1)} copy(bf16[16,512,2,128]{1,3,2,0:T(8,128)(2,1)} %fusion.22) | data formatting | bytes 8388608 | tf_op jit(solution)/shard_map/convert_element_type | solution.py:194
  120.8 1.8 collective-permute-start.5
  122.6 46.2 %collective-permute-done.5 = bf16[512,16,128]{2,1,0:T(8,128)(2,1)S(1)} collective-permute-done((bf16[512,16,128]{2,1,0:T(8,128)(2,1)}, bf16[512,16,128]{2,1,0:T(8,128)(2,1)S(1)}, u32[]{:S(2)}, u32[]{:S(2)}) %collective-permute-start.5) | collective-permute-done | bytes 2097184 | tf_op jit(solution)/shard_map/ppermute | solution.py:179
  168.8 4.2 %collective-permute-done.7 = bf16[512,16,128]{2,1,0:T(8,128)(2,1)S(1)} collective-permute-done((bf16[512,16,128]{2,1,0:T(8,128)(2,1)S(1)}, bf16[512,16,128]{2,1,0:T(8,128)(2,1)S(1)}, u32[]{:S(2)}, u32[]{:S(2)}) %collective-permute-start.7) | collective-permute-done | bytes 2097184 | tf_op jit(solution)/shard_map/ppermute | solution.py:183
  172.9 5.8 %fusion.20 = bf16[16,2,2,512,128]{4,0,3,2,1:T(8,128)(2,1)} fusion(bf16[512,16,128]{2,1,0:T(8,128)(2,1)S(1)} %collective-permute-done.7, bf16[512,16,128]{2,1,0:T(8,128)(2,1)S(1)} %collective-permute-done.6, bf16[512,16,128]{2,1,0:T(8,128)(2,1)S(1)} %collective-permute-done.5, bf16[512,16,128]{2,1,0:T(8,128)(2,1)} %fusion.231, ...), kind=kOutput, calls=%fused_computation.30 | convolution fusion | flops 574619648 | bytes 16785408 | tf_op jit(solution)/shard_map/fkrt,ptc->fkrpc/dot_general | solution.py:188
  178.7 12.8 %fusion.23 = bf16[16,512,2,128]{1,3,2,0:T(8,128)(2,1)} fusion(bf16[16,2,512,512]{3,2,1,0:T(8,128)(2,1)} %param.7, bf16[16,2,2,512,128]{4,0,3,2,1:T(8,128)(2,1)} %fusion.20), kind=kOutput, calls=%fused_computation.33 | convolution fusion | flops 4297064448 | bytes 29360128 | tf_op jit(solution)/shard_map/fksp,fkrpc->fsrc/dot_general | solution.py:193
  191.6 8.0 %copy.15 = bf16[16,512,2,128]{3,0,2,1:T(8,128)(2,1)} copy(bf16[16,512,2,128]{1,3,2,0:T(8,128)(2,1)} %fusion.23) | data formatting | bytes 8388608 | tf_op jit(solution)/shard_map/convert_element_type | solution.py:194
  199.6 4.8 %pad_maximum_fusion = bf16[512,16,256]{2,1,0:T(8,128)(2,1)} fusion(bf16[512,16,128]{2,1,0:T(8,128)(2,1)} %fusion.231, bf16[512,16,128]{2,1,0:T(8,128)(2,1)} %fusion.229), kind=kLoop, calls=%fused_computation.50 | loop fusion | flops 8388608 | bytes 8388608 | tf_op jit(solution)/shard_map/concatenate | solution.py:228
  204.4 5.9 %reduce-scatter.3.cloned.1.call-done = bf16[16,64,2,128]{3,0,2,1:T(8,128)(2,1)} async-done(((bf16[16,512,2,128]{3,0,2,1:T(8,128)(2,1)}), bf16[16,64,2,128]{3,0,2,1:T(8,128)(2,1)}) %reduce-scatter.3.cloned.1.call-update) | async-done | bytes 524304 | tf_op jit(solution)/shard_map/reduce_scatter | solution.py:194
  210.3 91.9 %reduce-scatter.5.cloned.1.call-done = bf16[16,64,2,128]{3,0,2,1:T(8,128)(2,1)} async-done(((bf16[16,512,2,128]{3,0,2,1:T(8,128)(2,1)}), bf16[16,64,2,128]{3,0,2,1:T(8,128)(2,1)}) %reduce-scatter.5.cloned.1.call-update) | async-done | bytes 524304 | tf_op jit(solution)/shard_map/reduce_scatter | solution.py:194
  302.2 1.4 maximum_convert_fusion
  303.6 3.2 %copy.16 = f32[64,16,2,256]{3,2,1,0:T(2,128)} copy(f32[64,16,2,256]{3,1,2,0:T(8,128)S(1)} %maximum_convert_fusion) | data formatting | bytes 4194304
  (83 shorter events, 7.9 us)
Async XLA Ops:
  7.2 203.2 %reduce-scatter.3.cloned.1.call-start = ((), (), s32[]{:S(2)}) async-start(), calls=%async_computation.2 | async-start | bytes 4718592 | tf_op jit(solution)/shard_map/reduce_scatter | solution.py:194
  9.7 26.7 %collective-permute-start.1 = (f32[20490]{0:T(1024)S(1)}, f32[20490]{0:T(1024)S(1)}, u32[]{:S(2)}, u32[]{:S(2)}) collective-permute-start(f32[20490]{0:T(1024)S(1)} %concatenate.49), channel_id=1, source_target_pairs={{4,0},{8,4},{12,8},{16,12},{20,16},{24,20},{28,24},{5,1},{9,5},{13... | collective-permute-start | bytes 245888 | tf_op jit(solution)/shard_map/ppermute | solution.py:19
  11.8 24.7 %collective-permute-start = (f32[20491]{0:T(1024)S(1)}, f32[20491]{0:T(1024)S(1)}, u32[]{:S(2)}, u32[]{:S(2)}) collective-permute-start(f32[20491]{0:T(1024)S(1)} %concatenate.47), channel_id=1, source_target_pairs={{0,4},{4,8},{8,12},{12,16},{16,20},{20,24},{24,28},{1,5},{5,9},{9,... | collective-permute-start | bytes 245900 | tf_op jit(solution)/shard_map/ppermute | solution.py:14
  17.4 4.3 %copy-start = (f32[512]{0:T(512)S(1)}, f32[512]{0:T(512)}, u32[]{:S(2)}) copy-start(f32[512]{0:T(512)} %param.5) | copy-start | bytes 6148
  17.4 4.3 %copy-start.1 = (f32[512]{0:T(512)S(1)}, f32[512]{0:T(512)}, u32[]{:S(2)}) copy-start(f32[512]{0:T(512)} %param.6) | copy-start | bytes 6148
  41.6 47.5 %collective-permute-start.2 = (bf16[512,16,128]{2,1,0:T(8,128)(2,1)}, bf16[512,16,128]{2,1,0:T(8,128)(2,1)}, u32[]{:S(2)}, u32[]{:S(2)}) collective-permute-start(bf16[512,16,128]{2,1,0:T(8,128)(2,1)} %fusion.229), channel_id=1, source_target_pairs={{0,2},{2,0},{1,3},{3,1},{4,6},{6,4},{5,7},{7,5},{8,10},{10,8},{9,1... | collective-permute-start | bytes 6291464 | tf_op jit(solution)/shard_map/ppermute | solution.py:179
  43.7 45.8 %collective-permute-start.3 = (bf16[512,16,128]{2,1,0:T(8,128)(2,1)}, bf16[512,16,128]{2,1,0:T(8,128)(2,1)}, u32[]{:S(2)}, u32[]{:S(2)}) collective-permute-start(bf16[512,16,128]{2,1,0:T(8,128)(2,1)} %fusion.229), channel_id=1, source_target_pairs={{0,1},{1,0},{2,3},{3,2},{4,5},{5,4},{6,7},{7,6},{8,9},{9,8},{10,11... | collective-permute-start | bytes 6291464 | tf_op jit(solution)/shard_map/ppermute | solution.py:180
  89.1 4.4 %collective-permute-start.4 = (bf16[512,16,128]{2,1,0:T(8,128)(2,1)}, bf16[512,16,128]{2,1,0:T(8,128)(2,1)S(1)}, u32[]{:S(2)}, u32[]{:S(2)}) collective-permute-start(bf16[512,16,128]{2,1,0:T(8,128)(2,1)} %collective-permute-done.2), channel_id=1, source_target_pairs={{0,1},{1,0},{2,3},{3,2},{4,5},{5,4},{6,7},{7,6},{8,9},{9,8},{10,11... | collective-permute-start | bytes 6291464 | tf_op jit(solution)/shard_map/ppermute | solution.py:183
  120.8 181.5 %reduce-scatter.5.cloned.1.call-start = ((), (), s32[]{:S(2)}) async-start(), calls=%async_computation.3 | async-start | bytes 4718592 | tf_op jit(solution)/shard_map/reduce_scatter | solution.py:194
  120.8 48.0 %collective-permute-start.5 = (bf16[512,16,128]{2,1,0:T(8,128)(2,1)}, bf16[512,16,128]{2,1,0:T(8,128)(2,1)S(1)}, u32[]{:S(2)}, u32[]{:S(2)}) collective-permute-start(bf16[512,16,128]{2,1,0:T(8,128)(2,1)} %fusion.231), channel_id=1, source_target_pairs={{0,2},{2,0},{1,3},{3,1},{4,6},{6,4},{5,7},{7,5},{8,10},{10,8},{9,1... | collective-permute-start | bytes 6291464 | tf_op jit(solution)/shard_map/ppermute | solution.py:179
  122.6 46.2 %collective-permute-start.6 = (bf16[512,16,128]{2,1,0:T(8,128)(2,1)}, bf16[512,16,128]{2,1,0:T(8,128)(2,1)S(1)}, u32[]{:S(2)}, u32[]{:S(2)}) collective-permute-start(bf16[512,16,128]{2,1,0:T(8,128)(2,1)} %fusion.231), channel_id=1, source_target_pairs={{0,1},{1,0},{2,3},{3,2},{4,5},{5,4},{6,7},{7,6},{8,9},{9,8},{10,11... | collective-permute-start | bytes 6291464 | tf_op jit(solution)/shard_map/ppermute | solution.py:180
  168.8 4.2 %collective-permute-start.7 = (bf16[512,16,128]{2,1,0:T(8,128)(2,1)S(1)}, bf16[512,16,128]{2,1,0:T(8,128)(2,1)S(1)}, u32[]{:S(2)}, u32[]{:S(2)}) collective-permute-start(bf16[512,16,128]{2,1,0:T(8,128)(2,1)S(1)} %collective-permute-done.5), channel_id=1, source_target_pairs={{0,1},{1,0},{2,3},{3,2},{4,5},{5,4},{6,7},{7,6},{8,9},{9,8},{10,11... | collective-permute-start | bytes 6291464 | tf_op jit(solution)/shard_map/ppermute | solution.py:183
Sparse Core Ops, SparseCore 0:
  120.9 89.3 reduce-scatter.2
  214.4 87.8 reduce-scatter.4

commit v13 on v12

--- a/solution.py
+++ b/solution.py
@@ -86,15 +86,15 @@
     lanes = jnp.arange(width, dtype=jnp.int32)
     probe = (rows[:, None] % width == lanes[None, :]).astype(jnp.float32)[:, None, :]
     response = smooth(probe, *coefficients, 0)[:, 0, :]
-    padded = jnp.pad(motion, ((halo, halo), (0, 0), (0, 0)))
     picks = (rows[None, :, None] + lanes[:, None, None] - halo) % width == lanes[None, None, :]
     bands = lax.optimization_barrier(jnp.sum(jnp.where(picks, response[None], 0.0), axis=2))
+    inner = points - 2 * halo
     total = None
     for offset in range(-halo, halo + 1):
-        band = bands[offset + halo][:, None, None]
-        term = band * padded[halo + offset : halo + offset + points].astype(jnp.float32)
+        band = bands[offset + halo, halo : halo + inner][:, None, None]
+        term = band * motion[halo + offset : halo + offset + inner].astype(jnp.float32)
         total = term if total is None else total + term
-    return total
+    return jnp.pad(total, ((halo, halo), (0, 0), (0, 0)))
 
 
 def smooth_with_edges(motion, halo_rows, coefficients, local_coefficients_, halo, banded=False):

time: 314 us -> 313 us (level)
    convert_element_type x1 -> x0, other arithmetic: 13.2 us -> none  [smooth_with_edges(): banded_smooth(motion, local_coefficients_, halo).astype(jnp.bfloat16)]
    another operation x1 -> x2, other arithmetic: 0.13 us -> 12.9 us
    slice x1, local copies, waits for them, and re-layouts: 4.27 us -> 0.36 us  [on_device(): source = motion[:, :, part]]
    pad x0 -> x1, local copies, waits for them, and re-layouts: none -> 3.23 us  [banded_smooth(): return jnp.pad(total, ((halo, halo), (0, 0), (0, 0)))]
where the time goes in v13:
time: 313 us
  waiting for transfers between devices  176 us (56%)
  other arithmetic  47.2 us (15%)
  matrix products  37.8 us (12%)
  local copies, waits for them, and re-layouts  26.2 us (8%)
  between operations  14.5 us (5%)
  starting transfers between devices  10.7 us (3%)
    reduce_scatter x2, waiting for transfers between devices, green_product(): lax.psum_scatter(partial.astype(jnp.bfloat16), 'sea', scatter_dimension=1...  97.8 us
    ppermute x2, waiting for transfers between devices, gathered_spectrum(): across = lax.ppermute(prior_part, 'tm', [(0, 2), (2, 0), (1, 3), (3, 1)])  70.4 us
    dot_general x2, matrix products, green_product(): jnp.einsum('fksp,fkrpc->fsrc', green, mixed, preferred_element_type=jnp.f...  25.6 us
    add x24, other arithmetic, smooth(): state = state + weights[k] * (source - applied) / diag  16.2 us
    convert_element_type x2, local copies, waits for them, and re-layouts, green_product(): partial.astype(jnp.bfloat16)  16.2 us
    another operation x2, other arithmetic  12.9 us
    dot_general x2, matrix products, gathered_spectrum(): jnp.einsum('fkrt,ptc->fkrpc', table_high, stacked, preferred_element_type...  12.2 us
    ppermute x2, waiting for transfers between devices, gathered_spectrum(): partner_across = lax.ppermute(across, 'tm', chip_pairs)  8.1 us
  transfers between devices with their start and end apart: 10, of which 6 were waited for; matrix products, arithmetic and copies ran while one was open for 23% of the time, Pallas kernels for 0%

profile of v13, /device:TPU:0, one launch (start us, length us, event | category | flops | bytes accessed | tf_op | source)
XLA Modules:
  0.0 312.7 jit_solution(5914652516160133830)
XLA Ops:
  7.2 0.8 slice_convert_fusion.3
  8.1 0.8 fusion.267
  9.7 1.3 collective-permute-start.1
  11.0 0.8 slice.414
  11.8 5.5 %collective-permute-start = (f32[20491]{0:T(1024)S(1)}, f32[20491]{0:T(1024)S(1)}, u32[]{:S(2)}, u32[]{:S(2)}) collective-permute-start(f32[20491]{0:T(1024)S(1)} %concatenate.47), channel_id=1, source_target_pairs={{0,4},{4,8},{8,12},{12,16},{16,20},{20,24},{24,28},{1,5},{5,9},{9,... | collective-permute-start | bytes 245900 | tf_op jit(solution)/shard_map/ppermute | solution.py:14
  17.4 0.8 add_add_fusion
  19.0 12.8 %add_convert_fusion = bf16[502,16,128]{2,1,0:T(8,128)(2,1)} fusion(bf16[512,16,256]{2,1,0:T(8,128)(2,1)} %param.4, f32[502]{0:T(512)S(1)} %bitcast.82, f32[502]{0:T(512)S(1)} %bitcast.83, f32[502]{0:T(512)S(1)} %bitcast.84, f32[502]{0:T(512)S(1)} %bitcast.85, f32[502]{0:T(512)S(1)} %bitcast.86, f32[502]{0:T(512)S(1)} %bitcast.87, f32[502]{0:T(512)S(1)} %bitcast.88, ...), kind=kLoop, calls=%fused_computation.52 | loop fusion | flops 33927168 | bytes 24696392 | tf_op jit(solution)/shard_map/convert.19
  32.2 3.2 %pad.103 = bf16[512,16,128]{2,1,0:T(8,128)(2,1)} pad(bf16[502,16,128]{2,1,0:T(8,128)(2,1)} %add_convert_fusion, bf16[]{:T(256)} %constant.44.clone.1), padding=5_5x0_0x0_0 | pad | bytes 4153346 | tf_op jit(solution)/shard_map/jit(_pad)/pad | solution.py:97
  39.0 1.5 fusion.24
  40.7 2.1 collective-permute-start.2
  43.3 3.4 %fusion.27 = f32[512,16,128]{2,1,0:T(8,128)S(1)} fusion(f32[512,16,128]{2,1,0:T(8,128)S(1)} %fusion.24, bf16[512,16,128]{2,1,0:T(8,128)(2,1)S(1)} %slice.459, f32[512]{0:T(512)S(1)} %get-tuple-element.15, f32[512]{0:T(512)S(1)} %get-tuple-element.62, f32[512]{0:T(512)S(1)} %get-tuple-element.14), kind=kLoop, calls=%fused_computation.37 | loop fusion | flops 10485760 | bytes 10491904 | tf_op jit(solution)/shard_map/add | solution.py:68
  46.7 3.4 %fusion.30 = f32[512,16,128]{2,1,0:T(8,128)S(1)} fusion(f32[512,16,128]{2,1,0:T(8,128)S(1)} %fusion.27, bf16[512,16,128]{2,1,0:T(8,128)(2,1)S(1)} %slice.459, f32[512]{0:T(512)S(1)} %get-tuple-element.15, f32[512]{0:T(512)S(1)} %get-tuple-element.62, f32[512]{0:T(512)S(1)} %get-tuple-element.14), kind=kLoop, calls=%fused_computation.40 | loop fusion | flops 10485760 | bytes 10491904 | tf_op jit(solution)/shard_map/add | solution.py:68
  50.1 3.4 %fusion.33 = f32[512,16,128]{2,1,0:T(8,128)S(1)} fusion(f32[512,16,128]{2,1,0:T(8,128)S(1)} %fusion.30, bf16[512,16,128]{2,1,0:T(8,128)(2,1)S(1)} %slice.459, f32[512]{0:T(512)S(1)} %get-tuple-element.15, f32[512]{0:T(512)S(1)} %get-tuple-element.62, f32[512]{0:T(512)S(1)} %get-tuple-element.14), kind=kLoop, calls=%fused_computation.43 | loop fusion | flops 10485760 | bytes 10491904 | tf_op jit(solution)/shard_map/add | solution.py:68
  53.5 3.4 %fusion.36 = f32[512,16,128]{2,1,0:T(8,128)S(1)} fusion(f32[512,16,128]{2,1,0:T(8,128)S(1)} %fusion.33, bf16[512,16,128]{2,1,0:T(8,128)(2,1)S(1)} %slice.459, f32[512]{0:T(512)S(1)} %get-tuple-element.15, f32[512]{0:T(512)S(1)} %get-tuple-element.62, f32[512]{0:T(512)S(1)} %get-tuple-element.14), kind=kLoop, calls=%fused_computation.46 | loop fusion | flops 10485760 | bytes 10491904 | tf_op jit(solution)/shard_map/add | solution.py:68
  56.9 4.6 %fusion.40 = bf16[512,16,128]{2,1,0:T(8,128)(2,1)} fusion(f32[512,16,128]{2,1,0:T(8,128)S(1)} %fusion.36, bf16[512,16,128]{2,1,0:T(8,128)(2,1)S(1)} %slice.459, f32[512]{0:T(512)S(1)} %get-tuple-element.15, f32[512]{0:T(512)S(1)} %get-tuple-element.62, f32[512]{0:T(512)S(1)} %get-tuple-element.14), kind=kLoop, calls=%fused_computation.51 | loop fusion | flops 11534336 | bytes 8394752 | tf_op jit(solution)/shard_map/convert_element_type | solution.py:107
  61.8 0.7 fusion.230
  63.9 24.3 %collective-permute-done.2 = bf16[512,16,128]{2,1,0:T(8,128)(2,1)} collective-permute-done((bf16[512,16,128]{2,1,0:T(8,128)(2,1)}, bf16[512,16,128]{2,1,0:T(8,128)(2,1)}, u32[]{:S(2)}, u32[]{:S(2)}) %collective-permute-start.2) | collective-permute-done | bytes 2097184 | tf_op jit(solution)/shard_map/ppermute | solution.py:179
  88.6 3.9 %collective-permute-done.4 = bf16[512,16,128]{2,1,0:T(8,128)(2,1)S(1)} collective-permute-done((bf16[512,16,128]{2,1,0:T(8,128)(2,1)}, bf16[512,16,128]{2,1,0:T(8,128)(2,1)S(1)}, u32[]{:S(2)}, u32[]{:S(2)}) %collective-permute-start.4) | collective-permute-done | bytes 2097184 | tf_op jit(solution)/shard_map/ppermute | solution.py:183
  92.5 6.4 %fusion.21 = bf16[16,2,2,512,128]{4,0,3,2,1:T(8,128)(2,1)} fusion(bf16[512,16,128]{2,1,0:T(8,128)(2,1)S(1)} %collective-permute-done.4, bf16[512,16,128]{2,1,0:T(8,128)(2,1)} %collective-permute-done.3, bf16[512,16,128]{2,1,0:T(8,128)(2,1)} %collective-permute-done.2, bf16[512,16,128]{2,1,0:T(8,128)(2,1)} %fusion.229, ...), kind=kOutput, calls=%fused_computation.31 | convolution fusion | flops 574619648 | bytes 16785408 | tf_op jit(solution)/shard_map/fkrt,ptc->fkrpc/dot_general | solution.py:188
  99.0 12.7 %fusion.22 = bf16[16,512,2,128]{1,3,2,0:T(8,128)(2,1)} fusion(bf16[16,2,512,512]{3,2,1,0:T(8,128)(2,1)} %param.7, bf16[16,2,2,512,128]{4,0,3,2,1:T(8,128)(2,1)} %fusion.21), kind=kOutput, calls=%fused_computation.32 | convolution fusion | flops 4297064448 | bytes 29360128 | tf_op jit(solution)/shard_map/fksp,fkrpc->fsrc/dot_general | solution.py:193
  111.7 8.1 %copy.13 = bf16[16,512,2,128]{3,0,2,1:T(8,128)(2,1)} copy(bf16[16,512,2,128]{1,3,2,0:T(8,128)(2,1)} %fusion.22) | data formatting | bytes 8388608 | tf_op jit(solution)/shard_map/convert_element_type | solution.py:194
  119.9 1.8 collective-permute-start.5
  121.6 46.2 %collective-permute-done.5 = bf16[512,16,128]{2,1,0:T(8,128)(2,1)S(1)} collective-permute-done((bf16[512,16,128]{2,1,0:T(8,128)(2,1)}, bf16[512,16,128]{2,1,0:T(8,128)(2,1)S(1)}, u32[]{:S(2)}, u32[]{:S(2)}) %collective-permute-start.5) | collective-permute-done | bytes 2097184 | tf_op jit(solution)/shard_map/ppermute | solution.py:179
  167.8 4.2 %collective-permute-done.7 = bf16[512,16,128]{2,1,0:T(8,128)(2,1)S(1)} collective-permute-done((bf16[512,16,128]{2,1,0:T(8,128)(2,1)S(1)}, bf16[512,16,128]{2,1,0:T(8,128)(2,1)S(1)}, u32[]{:S(2)}, u32[]{:S(2)}) %collective-permute-start.7) | collective-permute-done | bytes 2097184 | tf_op jit(solution)/shard_map/ppermute | solution.py:183
  172.0 5.8 %fusion.20 = bf16[16,2,2,512,128]{4,0,3,2,1:T(8,128)(2,1)} fusion(bf16[512,16,128]{2,1,0:T(8,128)(2,1)S(1)} %collective-permute-done.7, bf16[512,16,128]{2,1,0:T(8,128)(2,1)S(1)} %collective-permute-done.6, bf16[512,16,128]{2,1,0:T(8,128)(2,1)S(1)} %collective-permute-done.5, bf16[512,16,128]{2,1,0:T(8,128)(2,1)} %fusion.231, ...), kind=kOutput, calls=%fused_computation.30 | convolution fusion | flops 574619648 | bytes 16785408 | tf_op jit(solution)/shard_map/fkrt,ptc->fkrpc/dot_general | solution.py:188
  177.8 12.8 %fusion.23 = bf16[16,512,2,128]{1,3,2,0:T(8,128)(2,1)} fusion(bf16[16,2,512,512]{3,2,1,0:T(8,128)(2,1)} %param.7, bf16[16,2,2,512,128]{4,0,3,2,1:T(8,128)(2,1)} %fusion.20), kind=kOutput, calls=%fused_computation.33 | convolution fusion | flops 4297064448 | bytes 29360128 | tf_op jit(solution)/shard_map/fksp,fkrpc->fsrc/dot_general | solution.py:193
  190.6 8.0 %copy.15 = bf16[16,512,2,128]{3,0,2,1:T(8,128)(2,1)} copy(bf16[16,512,2,128]{1,3,2,0:T(8,128)(2,1)} %fusion.23) | data formatting | bytes 8388608 | tf_op jit(solution)/shard_map/convert_element_type | solution.py:194
  198.7 4.8 %pad_maximum_fusion = bf16[512,16,256]{2,1,0:T(8,128)(2,1)} fusion(bf16[512,16,128]{2,1,0:T(8,128)(2,1)} %fusion.231, bf16[512,16,128]{2,1,0:T(8,128)(2,1)} %fusion.229), kind=kLoop, calls=%fused_computation.50 | loop fusion | flops 8388608 | bytes 8388608 | tf_op jit(solution)/shard_map/concatenate | solution.py:228
  203.4 5.9 %reduce-scatter.3.cloned.1.call-done = bf16[16,64,2,128]{3,0,2,1:T(8,128)(2,1)} async-done(((bf16[16,512,2,128]{3,0,2,1:T(8,128)(2,1)}), bf16[16,64,2,128]{3,0,2,1:T(8,128)(2,1)}) %reduce-scatter.3.cloned.1.call-update) | async-done | bytes 524304 | tf_op jit(solution)/shard_map/reduce_scatter | solution.py:194
  209.4 91.9 %reduce-scatter.5.cloned.1.call-done = bf16[16,64,2,128]{3,0,2,1:T(8,128)(2,1)} async-done(((bf16[16,512,2,128]{3,0,2,1:T(8,128)(2,1)}), bf16[16,64,2,128]{3,0,2,1:T(8,128)(2,1)}) %reduce-scatter.5.cloned.1.call-update) | async-done | bytes 524304 | tf_op jit(solution)/shard_map/reduce_scatter | solution.py:194
  301.3 1.4 maximum_convert_fusion
  302.7 3.2 %copy.16 = f32[64,16,2,256]{3,2,1,0:T(2,128)} copy(f32[64,16,2,256]{3,1,2,0:T(8,128)S(1)} %maximum_convert_fusion) | data formatting | bytes 4194304
  (86 shorter events, 8.3 us)
Async XLA Ops:
  7.2 202.2 %reduce-scatter.3.cloned.1.call-start = ((), (), s32[]{:S(2)}) async-start(), calls=%async_computation.2 | async-start | bytes 4718592 | tf_op jit(solution)/shard_map/reduce_scatter | solution.py:194
  9.7 25.8 %collective-permute-start.1 = (f32[20490]{0:T(1024)S(1)}, f32[20490]{0:T(1024)S(1)}, u32[]{:S(2)}, u32[]{:S(2)}) collective-permute-start(f32[20490]{0:T(1024)S(1)} %concatenate.49), channel_id=1, source_target_pairs={{4,0},{8,4},{12,8},{16,12},{20,16},{24,20},{28,24},{5,1},{9,5},{13... | collective-permute-start | bytes 245888 | tf_op jit(solution)/shard_map/ppermute | solution.py:19
  11.8 23.7 %collective-permute-start = (f32[20491]{0:T(1024)S(1)}, f32[20491]{0:T(1024)S(1)}, u32[]{:S(2)}, u32[]{:S(2)}) collective-permute-start(f32[20491]{0:T(1024)S(1)} %concatenate.47), channel_id=1, source_target_pairs={{0,4},{4,8},{8,12},{12,16},{16,20},{20,24},{24,28},{1,5},{5,9},{9,... | collective-permute-start | bytes 245900 | tf_op jit(solution)/shard_map/ppermute | solution.py:14
  18.9 12.8 %copy-start = (bf16[512,16,256]{2,1,0:T(8,128)(2,1)S(1)}, bf16[512,16,256]{2,1,0:T(8,128)(2,1)}, u32[]{:S(2)}) copy-start(bf16[512,16,256]{2,1,0:T(8,128)(2,1)} %param.4) | copy-start | bytes 12582916
  31.8 3.8 %copy-start.1 = (f32[512]{0:T(512)S(1)}, f32[512]{0:T(512)}, u32[]{:S(2)}) copy-start(f32[512]{0:T(512)} %param.5) | copy-start | bytes 6148
  31.8 3.9 %copy-start.2 = (f32[512]{0:T(512)S(1)}, f32[512]{0:T(512)}, u32[]{:S(2)}) copy-start(f32[512]{0:T(512)} %param.6) | copy-start | bytes 6148
  40.7 47.5 %collective-permute-start.2 = (bf16[512,16,128]{2,1,0:T(8,128)(2,1)}, bf16[512,16,128]{2,1,0:T(8,128)(2,1)}, u32[]{:S(2)}, u32[]{:S(2)}) collective-permute-start(bf16[512,16,128]{2,1,0:T(8,128)(2,1)} %fusion.229), channel_id=1, source_target_pairs={{0,2},{2,0},{1,3},{3,1},{4,6},{6,4},{5,7},{7,5},{8,10},{10,8},{9,1... | collective-permute-start | bytes 6291464 | tf_op jit(solution)/shard_map/ppermute | solution.py:179
  42.7 45.8 %collective-permute-start.3 = (bf16[512,16,128]{2,1,0:T(8,128)(2,1)}, bf16[512,16,128]{2,1,0:T(8,128)(2,1)}, u32[]{:S(2)}, u32[]{:S(2)}) collective-permute-start(bf16[512,16,128]{2,1,0:T(8,128)(2,1)} %fusion.229), channel_id=1, source_target_pairs={{0,1},{1,0},{2,3},{3,2},{4,5},{5,4},{6,7},{7,6},{8,9},{9,8},{10,11... | collective-permute-start | bytes 6291464 | tf_op jit(solution)/shard_map/ppermute | solution.py:180
  88.2 4.4 %collective-permute-start.4 = (bf16[512,16,128]{2,1,0:T(8,128)(2,1)}, bf16[512,16,128]{2,1,0:T(8,128)(2,1)S(1)}, u32[]{:S(2)}, u32[]{:S(2)}) collective-permute-start(bf16[512,16,128]{2,1,0:T(8,128)(2,1)} %collective-permute-done.2), channel_id=1, source_target_pairs={{0,1},{1,0},{2,3},{3,2},{4,5},{5,4},{6,7},{7,6},{8,9},{9,8},{10,11... | collective-permute-start | bytes 6291464 | tf_op jit(solution)/shard_map/ppermute | solution.py:183
  119.8 181.5 %reduce-scatter.5.cloned.1.call-start = ((), (), s32[]{:S(2)}) async-start(), calls=%async_computation.3 | async-start | bytes 4718592 | tf_op jit(solution)/shard_map/reduce_scatter | solution.py:194
  119.9 47.9 %collective-permute-start.5 = (bf16[512,16,128]{2,1,0:T(8,128)(2,1)}, bf16[512,16,128]{2,1,0:T(8,128)(2,1)S(1)}, u32[]{:S(2)}, u32[]{:S(2)}) collective-permute-start(bf16[512,16,128]{2,1,0:T(8,128)(2,1)} %fusion.231), channel_id=1, source_target_pairs={{0,2},{2,0},{1,3},{3,1},{4,6},{6,4},{5,7},{7,5},{8,10},{10,8},{9,1... | collective-permute-start | bytes 6291464 | tf_op jit(solution)/shard_map/ppermute | solution.py:179
  121.6 46.2 %collective-permute-start.6 = (bf16[512,16,128]{2,1,0:T(8,128)(2,1)}, bf16[512,16,128]{2,1,0:T(8,128)(2,1)S(1)}, u32[]{:S(2)}, u32[]{:S(2)}) collective-permute-start(bf16[512,16,128]{2,1,0:T(8,128)(2,1)} %fusion.231), channel_id=1, source_target_pairs={{0,1},{1,0},{2,3},{3,2},{4,5},{5,4},{6,7},{7,6},{8,9},{9,8},{10,11... | collective-permute-start | bytes 6291464 | tf_op jit(solution)/shard_map/ppermute | solution.py:180
  167.8 4.2 %collective-permute-start.7 = (bf16[512,16,128]{2,1,0:T(8,128)(2,1)S(1)}, bf16[512,16,128]{2,1,0:T(8,128)(2,1)S(1)}, u32[]{:S(2)}, u32[]{:S(2)}) collective-permute-start(bf16[512,16,128]{2,1,0:T(8,128)(2,1)S(1)} %collective-permute-done.5), channel_id=1, source_target_pairs={{0,1},{1,0},{2,3},{3,2},{4,5},{5,4},{6,7},{7,6},{8,9},{9,8},{10,11... | collective-permute-start | bytes 6291464 | tf_op jit(solution)/shard_map/ppermute | solution.py:183
Sparse Core Ops, SparseCore 0:
  119.9 89.3 reduce-scatter.2
  213.4 87.8 reduce-scatter.4

commit v14 on v13

--- a/solution.py
+++ b/solution.py
@@ -94,7 +94,7 @@
         band = bands[offset + halo, halo : halo + inner][:, None, None]
         term = band * motion[halo + offset : halo + offset + inner].astype(jnp.float32)
         total = term if total is None else total + term
-    return jnp.pad(total, ((halo, halo), (0, 0), (0, 0)))
+    return total
 
 
 def smooth_with_edges(motion, halo_rows, coefficients, local_coefficients_, halo, banded=False):
@@ -102,7 +102,7 @@
     span = 3 * halo + 1
     keep = halo + 1
     if banded:
-        interior = banded_smooth(motion, local_coefficients_, halo).astype(jnp.bfloat16)
+        inner = banded_smooth(motion, local_coefficients_, halo)[1 : points - 2 * halo - 1]
     else:
         interior = smooth(motion.astype(jnp.float32), *local_coefficients_, 0).astype(jnp.bfloat16)
     before, after = halo_rows
@@ -114,6 +114,8 @@
     right = smooth(
         right_src, left_k[extent - span :], right_k[extent - span :], diag[extent - span :], halo
     )
+    if banded:
+        return jnp.concatenate([left, inner, right]).astype(jnp.bfloat16)
     interior = lax.dynamic_update_slice_in_dim(interior, left.astype(jnp.bfloat16), 0, 0)
     return lax.dynamic_update_slice_in_dim(
         interior, right.astype(jnp.bfloat16), points - keep, 0

time: 313 us -> 320 us (1.022)
  other arithmetic: 47.2 us -> 52.1 us
    add x0 -> x1, other arithmetic: none -> 8.1 us  [banded_smooth(): total = term if total is None else total + term]
    another operation x2 -> x4, other arithmetic: 12.9 us -> 5.28 us
    slice x0 -> x1, other arithmetic: none -> 6.32 us  [banded_smooth(): motion[halo + offset:halo + offset + inner].astype(jnp.float32)]
    pad x1 -> x0, local copies, waits for them, and re-layouts: 3.23 us -> none  [banded_smooth(): return jnp.pad(total, ((halo, halo), (0, 0), (0, 0)))]
where the time goes in v14:
time: 320 us; the launch traced here: 319 us
  waiting for transfers between devices  176 us (55%)
  other arithmetic  52.1 us (16%)
  matrix products  40.6 us (13%)
  local copies, waits for them, and re-layouts  24.8 us (8%)
  between operations  14.6 us (5%)
  starting transfers between devices  10.7 us (3%)
    reduce_scatter x2, waiting for transfers between devices, green_product(): lax.psum_scatter(partial.astype(jnp.bfloat16), 'sea', scatter_dimension=1...  97.4 us
    ppermute x2, waiting for transfers between devices, gathered_spectrum(): across = lax.ppermute(prior_part, 'tm', [(0, 2), (2, 0), (1, 3), (3, 1)])  70.4 us
    dot_general x2, matrix products, green_product(): jnp.einsum('fksp,fkrpc->fsrc', green, mixed, preferred_element_type=jnp.f...  25.6 us
    add x24, other arithmetic, smooth(): state = state + weights[k] * (source - applied) / diag  16.2 us
    convert_element_type x2, local copies, waits for them, and re-layouts, green_product(): partial.astype(jnp.bfloat16)  16.1 us
    dot_general x2, matrix products, gathered_spectrum(): jnp.einsum('fkrt,ptc->fkrpc', table_high, stacked, preferred_element_type...  15.1 us
    ppermute x2, waiting for transfers between devices, gathered_spectrum(): partner_across = lax.ppermute(across, 'tm', chip_pairs)  8.23 us
    add x1, other arithmetic, banded_smooth(): total = term if total is None else total + term  8.1 us
  transfers between devices with their start and end apart: 10, of which 6 were waited for; matrix products, arithmetic and copies ran while one was open for 23% of the time, Pallas kernels for 0%

profile of v14, /device:TPU:0, one launch (start us, length us, event | category | flops | bytes accessed | tf_op | source)
XLA Modules:
  0.0 318.9 jit_solution(12673602285623634521)
XLA Ops:
  7.2 0.8 slice_convert_fusion.4
  8.1 0.8 fusion.275
  9.7 1.3 collective-permute-start.1
  11.8 5.5 %collective-permute-start = (f32[20491]{0:T(1024)S(1)}, f32[20491]{0:T(1024)S(1)}, u32[]{:S(2)}, u32[]{:S(2)}) collective-permute-start(f32[20491]{0:T(1024)S(1)} %concatenate.50), channel_id=1, source_target_pairs={{0,4},{4,8},{8,12},{12,16},{16,20},{20,24},{24,28},{1,5},{5,9},{9,... | collective-permute-start | bytes 245900 | tf_op jit(solution)/shard_map/ppermute | solution.py:14
  17.4 6.3 %fusion.265 = (bf16[502,16,128]{2,1,0:T(8,128)(2,1)S(1)}, bf16[502,16,128]{2,1,0:T(8,128)(2,1)}, bf16[502,16,128]{2,1,0:T(8,128)(2,1)}, f32[502,16,128]{2,1,0:T(8,128)}) fusion(bf16[512,16,256]{2,1,0:T(8,128)(2,1)} %param.4), kind=kLoop, calls=%fused_computation.399 | loop fusion | flops 1028096 | bytes 18505728 | tf_op jit(solution)/shard_map/slice | solution.py:95
  24.8 8.1 %multiply_add_fusion = (f32[502,16,128]{2,1,0:T(8,128)S(1)}, f32[502,16,128]{2,1,0:T(8,128)S(1)}) fusion(bf16[512,16,256]{2,1,0:T(8,128)(2,1)} %param.4, f32[502]{0:T(512)S(1)} %bitcast.82, f32[502]{0:T(512)S(1)} %bitcast.83, f32[502]{0:T(512)S(1)} %bitcast.84, f32[502]{0:T(512)S(1)} %bitcast.85, f32[502]{0:T(512)S(1)} %bitcast.86, f32[502]{0:T(512)S(1)} %bitcast.87, ...), kind=kLoop, calls=%fused_computation.57 | loop fusion | flops 19533824 | bytes 22632168 | tf_op jit(solution)/shard_map/add | solution.py:96
  33.0 5.0 %fusion.49 = bf16[500,16,128]{2,1,0:T(8,128)(2,1)} fusion(f32[502,16,128]{2,1,0:T(8,128)S(1)} %copy-done.3, f32[502,16,128]{2,1,0:T(8,128)S(1)} %get-tuple-element.23, f32[502,16,128]{2,1,0:T(8,128)S(1)} %get-tuple-element.22, f32[500]{0:T(512)S(1)} %slice.532, bf16[502,16,128]{2,1,0:T(8,128)(2,1)S(1)} %copy-done.4, f32[500]{0:T(512)S(1)} %slice.530, ...), kind=kLoop, calls=%fused_computation.63 | loop fusion | flops 13312000 | bytes 20488000 | tf_op jit(solution)/shard_map/convert.19
  40.8 1.6 pad_maximum_fusion.1
  42.4 1.5 fusion.28
  44.0 2.1 collective-permute-start.2
  46.6 3.4 %fusion.31 = f32[512,16,128]{2,1,0:T(8,128)S(1)} fusion(f32[512,16,128]{2,1,0:T(8,128)S(1)} %fusion.28, bf16[512,16,128]{2,1,0:T(8,128)(2,1)S(1)} %slice.464, f32[512]{0:T(512)S(1)} %get-tuple-element.15, f32[512]{0:T(512)S(1)} %get-tuple-element.66, f32[512]{0:T(512)S(1)} %get-tuple-element.14), kind=kLoop, calls=%fused_computation.41 | loop fusion | flops 10485760 | bytes 10491904 | tf_op jit(solution)/shard_map/add | solution.py:68
  50.0 3.4 %fusion.34 = f32[512,16,128]{2,1,0:T(8,128)S(1)} fusion(f32[512,16,128]{2,1,0:T(8,128)S(1)} %fusion.31, bf16[512,16,128]{2,1,0:T(8,128)(2,1)S(1)} %slice.464, f32[512]{0:T(512)S(1)} %get-tuple-element.15, f32[512]{0:T(512)S(1)} %get-tuple-element.66, f32[512]{0:T(512)S(1)} %get-tuple-element.14), kind=kLoop, calls=%fused_computation.44 | loop fusion | flops 10485760 | bytes 10491904 | tf_op jit(solution)/shard_map/add | solution.py:68
  53.4 3.4 %fusion.37 = f32[512,16,128]{2,1,0:T(8,128)S(1)} fusion(f32[512,16,128]{2,1,0:T(8,128)S(1)} %fusion.34, bf16[512,16,128]{2,1,0:T(8,128)(2,1)S(1)} %slice.464, f32[512]{0:T(512)S(1)} %get-tuple-element.15, f32[512]{0:T(512)S(1)} %get-tuple-element.66, f32[512]{0:T(512)S(1)} %get-tuple-element.14), kind=kLoop, calls=%fused_computation.47 | loop fusion | flops 10485760 | bytes 10491904 | tf_op jit(solution)/shard_map/add | solution.py:68
  56.8 3.4 %fusion.40 = f32[512,16,128]{2,1,0:T(8,128)S(1)} fusion(f32[512,16,128]{2,1,0:T(8,128)S(1)} %fusion.37, bf16[512,16,128]{2,1,0:T(8,128)(2,1)S(1)} %slice.464, f32[512]{0:T(512)S(1)} %get-tuple-element.15, f32[512]{0:T(512)S(1)} %get-tuple-element.66, f32[512]{0:T(512)S(1)} %get-tuple-element.14), kind=kLoop, calls=%fused_computation.50 | loop fusion | flops 10485760 | bytes 10491904 | tf_op jit(solution)/shard_map/add | solution.py:68
  60.3 4.6 %fusion.44 = bf16[512,16,128]{2,1,0:T(8,128)(2,1)} fusion(f32[512,16,128]{2,1,0:T(8,128)S(1)} %fusion.40, bf16[512,16,128]{2,1,0:T(8,128)(2,1)S(1)} %slice.464, f32[512]{0:T(512)S(1)} %get-tuple-element.15, f32[512]{0:T(512)S(1)} %get-tuple-element.66, f32[512]{0:T(512)S(1)} %get-tuple-element.14), kind=kLoop, calls=%fused_computation.55 | loop fusion | flops 11534336 | bytes 8394752 | tf_op jit(solution)/shard_map/convert_element_type | solution.py:107
  67.2 24.3 %collective-permute-done.2 = bf16[512,16,128]{2,1,0:T(8,128)(2,1)} collective-permute-done((bf16[512,16,128]{2,1,0:T(8,128)(2,1)}, bf16[512,16,128]{2,1,0:T(8,128)(2,1)}, u32[]{:S(2)}, u32[]{:S(2)}) %collective-permute-start.2) | collective-permute-done | bytes 2097184 | tf_op jit(solution)/shard_map/ppermute | solution.py:181
  91.9 4.1 %collective-permute-done.4 = bf16[512,16,128]{2,1,0:T(8,128)(2,1)} collective-permute-done((bf16[512,16,128]{2,1,0:T(8,128)(2,1)}, bf16[512,16,128]{2,1,0:T(8,128)(2,1)}, u32[]{:S(2)}, u32[]{:S(2)}) %collective-permute-start.4) | collective-permute-done | bytes 2097184 | tf_op jit(solution)/shard_map/ppermute | solution.py:185
  96.0 9.3 %fusion.25 = bf16[16,2,2,512,128]{4,0,3,2,1:T(8,128)(2,1)} fusion(bf16[512,16,128]{2,1,0:T(8,128)(2,1)} %collective-permute-done.4, bf16[512,16,128]{2,1,0:T(8,128)(2,1)} %collective-permute-done.3, bf16[512,16,128]{2,1,0:T(8,128)(2,1)} %collective-permute-done.2, bf16[6,16,128]{2,1,0:T(8,128)(2,1)S(1)} %fusion.192, bf16[500,16,128]{2,1,0:T(8,128)(2,1)} %fusion.49, ...), kind=kOutput, calls=%fused_computation.35 | convolution fusion | flops 591396864 | bytes 16785408 | tf_op jit(solution)/shard_map/fkrt,ptc->fkrpc/dot_general | solution.py:190
  105.3 12.7 %fusion.26 = bf16[16,512,2,128]{1,3,2,0:T(8,128)(2,1)} fusion(bf16[16,2,512,512]{3,2,1,0:T(8,128)(2,1)} %param.7, bf16[16,2,2,512,128]{4,0,3,2,1:T(8,128)(2,1)} %fusion.25), kind=kOutput, calls=%fused_computation.36 | convolution fusion | flops 4297064448 | bytes 29360128 | tf_op jit(solution)/shard_map/fksp,fkrpc->fsrc/dot_general | solution.py:195
  118.0 8.1 %copy.13 = bf16[16,512,2,128]{3,0,2,1:T(8,128)(2,1)} copy(bf16[16,512,2,128]{1,3,2,0:T(8,128)(2,1)} %fusion.26) | data formatting | bytes 8388608 | tf_op jit(solution)/shard_map/convert_element_type | solution.py:196
  126.2 1.8 collective-permute-start.5
  128.0 46.2 %collective-permute-done.5 = bf16[512,16,128]{2,1,0:T(8,128)(2,1)S(1)} collective-permute-done((bf16[512,16,128]{2,1,0:T(8,128)(2,1)}, bf16[512,16,128]{2,1,0:T(8,128)(2,1)S(1)}, u32[]{:S(2)}, u32[]{:S(2)}) %collective-permute-start.5) | collective-permute-done | bytes 2097184 | tf_op jit(solution)/shard_map/ppermute | solution.py:181
  174.1 4.2 %collective-permute-done.7 = bf16[512,16,128]{2,1,0:T(8,128)(2,1)S(1)} collective-permute-done((bf16[512,16,128]{2,1,0:T(8,128)(2,1)S(1)}, bf16[512,16,128]{2,1,0:T(8,128)(2,1)S(1)}, u32[]{:S(2)}, u32[]{:S(2)}) %collective-permute-start.7) | collective-permute-done | bytes 2097184 | tf_op jit(solution)/shard_map/ppermute | solution.py:185
  178.3 5.8 %fusion.24 = bf16[16,2,2,512,128]{4,0,3,2,1:T(8,128)(2,1)} fusion(bf16[512,16,128]{2,1,0:T(8,128)(2,1)S(1)} %collective-permute-done.7, bf16[512,16,128]{2,1,0:T(8,128)(2,1)S(1)} %collective-permute-done.6, bf16[512,16,128]{2,1,0:T(8,128)(2,1)S(1)} %collective-permute-done.5, bf16[512,16,128]{2,1,0:T(8,128)(2,1)} %fusion.238, ...), kind=kOutput, calls=%fused_computation.34 | convolution fusion | flops 574619648 | bytes 16785408 | tf_op jit(solution)/shard_map/fkrt,ptc->fkrpc/dot_general | solution.py:190
  184.1 12.8 %fusion.27 = bf16[16,512,2,128]{1,3,2,0:T(8,128)(2,1)} fusion(bf16[16,2,512,512]{3,2,1,0:T(8,128)(2,1)} %param.7, bf16[16,2,2,512,128]{4,0,3,2,1:T(8,128)(2,1)} %fusion.24), kind=kOutput, calls=%fused_computation.37 | convolution fusion | flops 4297064448 | bytes 29360128 | tf_op jit(solution)/shard_map/fksp,fkrpc->fsrc/dot_general | solution.py:195
  196.9 8.0 %copy.15 = bf16[16,512,2,128]{3,0,2,1:T(8,128)(2,1)} copy(bf16[16,512,2,128]{1,3,2,0:T(8,128)(2,1)} %fusion.27) | data formatting | bytes 8388608 | tf_op jit(solution)/shard_map/convert_element_type | solution.py:196
  205.0 1.6 copy-done.2
  206.5 3.5 %pad_maximum_fusion = bf16[512,16,256]{2,1,0:T(8,128)(2,1)} fusion(bf16[512,16,128]{2,1,0:T(8,128)(2,1)} %fusion.238, bf16[6,16,128]{2,1,0:T(8,128)(2,1)S(1)} %fusion.192, bf16[500,16,128]{2,1,0:T(8,128)(2,1)S(1)} %copy-done.2, bf16[6,16,128]{2,1,0:T(8,128)(2,1)S(1)} %fusion.195), kind=kLoop, calls=%fused_computation.54 | loop fusion | flops 16777216 | bytes 8388608 | tf_op jit(solution)/shard_map/concatenate | solution.py:230
  210.0 5.5 %reduce-scatter.3.cloned.1.call-done = bf16[16,64,2,128]{3,0,2,1:T(8,128)(2,1)} async-done(((bf16[16,512,2,128]{3,0,2,1:T(8,128)(2,1)}), bf16[16,64,2,128]{3,0,2,1:T(8,128)(2,1)}) %reduce-scatter.3.cloned.1.call-update) | async-done | bytes 524304 | tf_op jit(solution)/shard_map/reduce_scatter | solution.py:196
  215.5 91.9 %reduce-scatter.5.cloned.1.call-done = bf16[16,64,2,128]{3,0,2,1:T(8,128)(2,1)} async-done(((bf16[16,512,2,128]{3,0,2,1:T(8,128)(2,1)}), bf16[16,64,2,128]{3,0,2,1:T(8,128)(2,1)}) %reduce-scatter.5.cloned.1.call-update) | async-done | bytes 524304 | tf_op jit(solution)/shard_map/reduce_scatter | solution.py:196
  307.4 1.4 maximum_convert_fusion
  308.8 3.2 %copy.16 = f32[64,16,2,256]{3,2,1,0:T(2,128)} copy(f32[64,16,2,256]{3,1,2,0:T(8,128)S(1)} %maximum_convert_fusion) | data formatting | bytes 4194304
  (102 shorter events, 8.9 us)
Async XLA Ops:
  7.2 208.4 %reduce-scatter.3.cloned.1.call-start = ((), (), s32[]{:S(2)}) async-start(), calls=%async_computation.2 | async-start | bytes 4718592 | tf_op jit(solution)/shard_map/reduce_scatter | solution.py:196
  9.7 28.7 %collective-permute-start.1 = (f32[20490]{0:T(1024)S(1)}, f32[20490]{0:T(1024)S(1)}, u32[]{:S(2)}, u32[]{:S(2)}) collective-permute-start(f32[20490]{0:T(1024)S(1)} %concatenate.52), channel_id=1, source_target_pairs={{4,0},{8,4},{12,8},{16,12},{20,16},{24,20},{28,24},{5,1},{9,5},{13... | collective-permute-start | bytes 245888 | tf_op jit(solution)/shard_map/ppermute | solution.py:19
  11.8 26.7 %collective-permute-start = (f32[20491]{0:T(1024)S(1)}, f32[20491]{0:T(1024)S(1)}, u32[]{:S(2)}, u32[]{:S(2)}) collective-permute-start(f32[20491]{0:T(1024)S(1)} %concatenate.50), channel_id=1, source_target_pairs={{0,4},{4,8},{8,12},{12,16},{16,20},{20,24},{24,28},{1,5},{5,9},{9,... | collective-permute-start | bytes 245900 | tf_op jit(solution)/shard_map/ppermute | solution.py:14
  17.4 6.4 %copy-start.6 = (f32[512]{0:T(512)S(1)}, f32[512]{0:T(512)}, u32[]{:S(2)}) copy-start(f32[512]{0:T(512)} %param.5) | copy-start | bytes 6148
  17.4 6.3 %copy-start.7 = (f32[512]{0:T(512)S(1)}, f32[512]{0:T(512)}, u32[]{:S(2)}) copy-start(f32[512]{0:T(512)} %param.6) | copy-start | bytes 6148
  24.8 8.1 %copy-start.3 = (f32[502,16,128]{2,1,0:T(8,128)S(1)}, f32[502,16,128]{2,1,0:T(8,128)}, u32[]{:S(2)}) copy-start(f32[502,16,128]{2,1,0:T(8,128)} %get-tuple-element.21) | copy-start | bytes 12337156
  24.8 8.1 %copy-start.4 = (bf16[502,16,128]{2,1,0:T(8,128)(2,1)S(1)}, bf16[502,16,128]{2,1,0:T(8,128)(2,1)}, u32[]{:S(2)}) copy-start(bf16[502,16,128]{2,1,0:T(8,128)(2,1)} %get-tuple-element.19) | copy-start | bytes 6168580
  24.8 8.1 %copy-start.5 = (bf16[502,16,128]{2,1,0:T(8,128)(2,1)S(1)}, bf16[502,16,128]{2,1,0:T(8,128)(2,1)}, u32[]{:S(2)}) copy-start(bf16[502,16,128]{2,1,0:T(8,128)(2,1)} %get-tuple-element.20) | copy-start | bytes 6168580
  33.0 5.0 %copy-start = (bf16[512,16,256]{2,1,0:T(8,128)(2,1)S(1)}, bf16[512,16,256]{2,1,0:T(8,128)(2,1)}, u32[]{:S(2)}) copy-start(bf16[512,16,256]{2,1,0:T(8,128)(2,1)} %param.4) | copy-start | bytes 12582916
  38.9 1.9 copy-start.1
  44.0 47.5 %collective-permute-start.2 = (bf16[512,16,128]{2,1,0:T(8,128)(2,1)}, bf16[512,16,128]{2,1,0:T(8,128)(2,1)}, u32[]{:S(2)}, u32[]{:S(2)}) collective-permute-start(bf16[512,16,128]{2,1,0:T(8,128)(2,1)} %pad_maximum_fusion.1), channel_id=1, source_target_pairs={{0,2},{2,0},{1,3},{3,1},{4,6},{6,4},{5,7},{7,5},{8,10},{10,8},{9,1... | collective-permute-start | bytes 6291464 | tf_op jit(solution)/shard_map/ppermute | solution.py:181
  46.1 45.8 %collective-permute-start.3 = (bf16[512,16,128]{2,1,0:T(8,128)(2,1)}, bf16[512,16,128]{2,1,0:T(8,128)(2,1)}, u32[]{:S(2)}, u32[]{:S(2)}) collective-permute-start(bf16[512,16,128]{2,1,0:T(8,128)(2,1)} %pad_maximum_fusion.1), channel_id=1, source_target_pairs={{0,1},{1,0},{2,3},{3,2},{4,5},{5,4},{6,7},{7,6},{8,9},{9,8},{10,11... | collective-permute-start | bytes 6291464 | tf_op jit(solution)/shard_map/ppermute | solution.py:182
  91.5 4.5 %collective-permute-start.4 = (bf16[512,16,128]{2,1,0:T(8,128)(2,1)}, bf16[512,16,128]{2,1,0:T(8,128)(2,1)}, u32[]{:S(2)}, u32[]{:S(2)}) collective-permute-start(bf16[512,16,128]{2,1,0:T(8,128)(2,1)} %collective-permute-done.2), channel_id=1, source_target_pairs={{0,1},{1,0},{2,3},{3,2},{4,5},{5,4},{6,7},{7,6},{8,9},{9,8},{10,11... | collective-permute-start | bytes 6291464 | tf_op jit(solution)/shard_map/ppermute | solution.py:185
  126.1 181.3 %reduce-scatter.5.cloned.1.call-start = ((), (), s32[]{:S(2)}) async-start(), calls=%async_computation.3 | async-start | bytes 4718592 | tf_op jit(solution)/shard_map/reduce_scatter | solution.py:196
  126.2 47.9 %collective-permute-start.5 = (bf16[512,16,128]{2,1,0:T(8,128)(2,1)}, bf16[512,16,128]{2,1,0:T(8,128)(2,1)S(1)}, u32[]{:S(2)}, u32[]{:S(2)}) collective-permute-start(bf16[512,16,128]{2,1,0:T(8,128)(2,1)} %fusion.238), channel_id=1, source_target_pairs={{0,2},{2,0},{1,3},{3,1},{4,6},{6,4},{5,7},{7,5},{8,10},{10,8},{9,1... | collective-permute-start | bytes 6291464 | tf_op jit(solution)/shard_map/ppermute | solution.py:181
  128.0 46.2 %collective-permute-start.6 = (bf16[512,16,128]{2,1,0:T(8,128)(2,1)}, bf16[512,16,128]{2,1,0:T(8,128)(2,1)S(1)}, u32[]{:S(2)}, u32[]{:S(2)}) collective-permute-start(bf16[512,16,128]{2,1,0:T(8,128)(2,1)} %fusion.238), channel_id=1, source_target_pairs={{0,1},{1,0},{2,3},{3,2},{4,5},{5,4},{6,7},{7,6},{8,9},{9,8},{10,11... | collective-permute-start | bytes 6291464 | tf_op jit(solution)/shard_map/ppermute | solution.py:182
  174.1 4.2 %collective-permute-start.7 = (bf16[512,16,128]{2,1,0:T(8,128)(2,1)S(1)}, bf16[512,16,128]{2,1,0:T(8,128)(2,1)S(1)}, u32[]{:S(2)}, u32[]{:S(2)}) collective-permute-start(bf16[512,16,128]{2,1,0:T(8,128)(2,1)S(1)} %collective-permute-done.5), channel_id=1, source_target_pairs={{0,1},{1,0},{2,3},{3,2},{4,5},{5,4},{6,7},{7,6},{8,9},{9,8},{10,11... | collective-permute-start | bytes 6291464 | tf_op jit(solution)/shard_map/ppermute | solution.py:185
  204.9 1.6 copy-start.2
Sparse Core Ops, SparseCore 0:
  126.3 89.2 reduce-scatter.2
  219.6 87.7 reduce-scatter.4

commit v15 on v13

--- a/solution.py
+++ b/solution.py
@@ -97,14 +97,9 @@
     return jnp.pad(total, ((halo, halo), (0, 0), (0, 0)))
 
 
-def smooth_with_edges(motion, halo_rows, coefficients, local_coefficients_, halo, banded=False):
+def edge_rows(motion, halo_rows, coefficients, halo):
     points = motion.shape[0]
     span = 3 * halo + 1
-    keep = halo + 1
-    if banded:
-        interior = banded_smooth(motion, local_coefficients_, halo).astype(jnp.bfloat16)
-    else:
-        interior = smooth(motion.astype(jnp.float32), *local_coefficients_, 0).astype(jnp.bfloat16)
     before, after = halo_rows
     left_src = jnp.concatenate([before, motion[: span - halo]]).astype(jnp.float32)
     right_src = jnp.concatenate([motion[points - span + halo :], after]).astype(jnp.float32)
@@ -114,10 +109,19 @@
     right = smooth(
         right_src, left_k[extent - span :], right_k[extent - span :], diag[extent - span :], halo
     )
-    interior = lax.dynamic_update_slice_in_dim(interior, left.astype(jnp.bfloat16), 0, 0)
-    return lax.dynamic_update_slice_in_dim(
-        interior, right.astype(jnp.bfloat16), points - keep, 0
-    )
+    return left.astype(jnp.bfloat16), right.astype(jnp.bfloat16)
+
+
+def smooth_with_edges(motion, edges, local_coefficients_, halo, banded=False):
+    points = motion.shape[0]
+    keep = halo + 1
+    if banded:
+        interior = banded_smooth(motion, local_coefficients_, halo).astype(jnp.bfloat16)
+    else:
+        interior = smooth(motion.astype(jnp.float32), *local_coefficients_, 0).astype(jnp.bfloat16)
+    left, right = edges
+    interior = lax.dynamic_update_slice_in_dim(interior, left, 0, 0)
+    return lax.dynamic_update_slice_in_dim(interior, right, points - keep, 0)
 
 
 def dft_tables(steps_all):
@@ -202,14 +206,15 @@
     halo_rows, kappa_ext, react_ext = exchange_halo(motion, kappa, react, halo)
     coefficients = extended_coefficients(kappa_ext, react_ext, motion.shape[0], halo)
     inner = local_coefficients(kappa, react)
+    left_all, right_all = edge_rows(motion, halo_rows, coefficients, halo)
     priors = []
     for c in range(CHUNKS):
         part = slice(c * width, (c + 1) * width)
         source = motion[:, :, part]
         if priors:
             source, _ = lax.optimization_barrier((source, priors[-1]))
-        rows = (halo_rows[0][:, :, part], halo_rows[1][:, :, part])
-        priors.append(smooth_with_edges(source, rows, coefficients, inner, halo, c == 0))
+        edges = (left_all[:, :, part], right_all[:, :, part])
+        priors.append(smooth_with_edges(source, edges, inner, halo, c == 0))
     sensors = []
     if lax.axis_size("tm") == 4:
         spectra = []

time: 313 us -> 312 us (level)
  other arithmetic: 47.2 us -> 43.3 us
    add x24 -> x16, other arithmetic: 16.2 us -> 15.5 us  [smooth(): state = state + weights[k] * (source - applied) / diag]
    another operation x2 -> x4, other arithmetic: 12.9 us -> 13.3 us
where the time goes in v15:
time: 312 us; the launch traced here: 311 us
  waiting for transfers between devices  176 us (56%)
  other arithmetic  43.3 us (14%)
  matrix products  37.7 us (12%)
  local copies, waits for them, and re-layouts  28.5 us (9%)
  between operations  14.4 us (5%)
  starting transfers between devices  10.6 us (3%)
    reduce_scatter x2, waiting for transfers between devices, green_product(): lax.psum_scatter(partial.astype(jnp.bfloat16), 'sea', scatter_dimension=1...  97.5 us
    ppermute x2, waiting for transfers between devices, gathered_spectrum(): across = lax.ppermute(prior_part, 'tm', [(0, 2), (2, 0), (1, 3), (3, 1)])  70.7 us
    dot_general x2, matrix products, green_product(): jnp.einsum('fksp,fkrpc->fsrc', green, mixed, preferred_element_type=jnp.f...  25.6 us
    convert_element_type x2, local copies, waits for them, and re-layouts, green_product(): partial.astype(jnp.bfloat16)  16.1 us
    add x16, other arithmetic, smooth(): state = state + weights[k] * (source - applied) / diag  15.5 us
    another operation x4, other arithmetic  13.3 us
    dot_general x2, matrix products, gathered_spectrum(): jnp.einsum('fkrt,ptc->fkrpc', table_high, stacked, preferred_element_type...  12.1 us
    ppermute x2, waiting for transfers between devices, gathered_spectrum(): partner_across = lax.ppermute(across, 'tm', chip_pairs)  8.1 us
  transfers between devices with their start and end apart: 10, of which 6 were waited for; matrix products, arithmetic and copies ran while one was open for 23% of the time, Pallas kernels for 0%

profile of v15, /device:TPU:0, one launch (start us, length us, event | category | flops | bytes accessed | tf_op | source)
XLA Modules:
  0.0 310.9 jit_solution(6234199448281253451)
XLA Ops:
  7.2 0.8 slice_convert_fusion.3
  8.1 0.8 fusion.189
  8.9 0.7 slice.338
  9.7 1.3 collective-permute-start.1
  11.0 0.8 slice.332
  11.8 5.5 %collective-permute-start = (f32[20491]{0:T(1024)S(1)}, f32[20491]{0:T(1024)S(1)}, u32[]{:S(2)}, u32[]{:S(2)}) collective-permute-start(f32[20491]{0:T(1024)S(1)} %concatenate.41), channel_id=1, source_target_pairs={{0,4},{4,8},{8,12},{12,16},{16,20},{20,24},{24,28},{1,5},{5,9},{9,... | collective-permute-start | bytes 245900 | tf_op jit(solution)/shard_map/ppermute | solution.py:14
  17.4 0.8 add_add_fusion
  19.0 12.8 %add_convert_fusion = bf16[502,16,128]{2,1,0:T(8,128)(2,1)} fusion(bf16[512,16,256]{2,1,0:T(8,128)(2,1)} %param.4, f32[502]{0:T(512)S(1)} %bitcast.82, f32[502]{0:T(512)S(1)} %bitcast.83, f32[502]{0:T(512)S(1)} %bitcast.84, f32[502]{0:T(512)S(1)} %bitcast.85, f32[502]{0:T(512)S(1)} %bitcast.86, f32[502]{0:T(512)S(1)} %bitcast.87, f32[502]{0:T(512)S(1)} %bitcast.88, ...), kind=kLoop, calls=%fused_computation.52 | loop fusion | flops 33927168 | bytes 24696392 | tf_op jit(solution)/shard_map/convert.17
  32.2 3.3 %pad.73 = bf16[512,16,128]{2,1,0:T(8,128)(2,1)} pad(bf16[502,16,128]{2,1,0:T(8,128)(2,1)} %add_convert_fusion, bf16[]{:T(256)} %constant.44.clone.1), padding=5_5x0_0x0_0 | pad | bytes 4153346 | tf_op jit(solution)/shard_map/jit(_pad)/pad | solution.py:97
  39.3 2.0 collective-permute-start.2
  41.3 1.5 fusion.24
  42.9 3.4 %fusion.27 = f32[512,16,128]{2,1,0:T(8,128)S(1)} fusion(f32[512,16,128]{2,1,0:T(8,128)S(1)} %fusion.24, bf16[512,16,128]{2,1,0:T(8,128)(2,1)S(1)} %slice.375, f32[512]{0:T(512)S(1)} %get-tuple-element.15, f32[512]{0:T(512)S(1)} %get-tuple-element.46, f32[512]{0:T(512)S(1)} %get-tuple-element.14), kind=kLoop, calls=%fused_computation.37 | loop fusion | flops 10485760 | bytes 10491904 | tf_op jit(solution)/shard_map/add | solution.py:68
  46.2 3.4 %fusion.30 = f32[512,16,128]{2,1,0:T(8,128)S(1)} fusion(f32[512,16,128]{2,1,0:T(8,128)S(1)} %fusion.27, bf16[512,16,128]{2,1,0:T(8,128)(2,1)S(1)} %slice.375, f32[512]{0:T(512)S(1)} %get-tuple-element.15, f32[512]{0:T(512)S(1)} %get-tuple-element.46, f32[512]{0:T(512)S(1)} %get-tuple-element.14), kind=kLoop, calls=%fused_computation.40 | loop fusion | flops 10485760 | bytes 10491904 | tf_op jit(solution)/shard_map/add | solution.py:68
  49.6 3.4 %fusion.33 = f32[512,16,128]{2,1,0:T(8,128)S(1)} fusion(f32[512,16,128]{2,1,0:T(8,128)S(1)} %fusion.30, bf16[512,16,128]{2,1,0:T(8,128)(2,1)S(1)} %slice.375, f32[512]{0:T(512)S(1)} %get-tuple-element.15, f32[512]{0:T(512)S(1)} %get-tuple-element.46, f32[512]{0:T(512)S(1)} %get-tuple-element.14), kind=kLoop, calls=%fused_computation.43 | loop fusion | flops 10485760 | bytes 10491904 | tf_op jit(solution)/shard_map/add | solution.py:68
  53.0 3.4 %fusion.36 = f32[512,16,128]{2,1,0:T(8,128)S(1)} fusion(f32[512,16,128]{2,1,0:T(8,128)S(1)} %fusion.33, bf16[512,16,128]{2,1,0:T(8,128)(2,1)S(1)} %slice.375, f32[512]{0:T(512)S(1)} %get-tuple-element.15, f32[512]{0:T(512)S(1)} %get-tuple-element.46, f32[512]{0:T(512)S(1)} %get-tuple-element.14), kind=kLoop, calls=%fused_computation.46 | loop fusion | flops 10485760 | bytes 10491904 | tf_op jit(solution)/shard_map/add | solution.py:68
  56.5 4.6 %fusion.40 = bf16[512,16,128]{2,1,0:T(8,128)(2,1)} fusion(f32[512,16,128]{2,1,0:T(8,128)S(1)} %fusion.36, bf16[512,16,128]{2,1,0:T(8,128)(2,1)S(1)} %slice.375, f32[512]{0:T(512)S(1)} %get-tuple-element.15, f32[512]{0:T(512)S(1)} %get-tuple-element.46, f32[512]{0:T(512)S(1)} %get-tuple-element.14), kind=kLoop, calls=%fused_computation.51 | loop fusion | flops 11534336 | bytes 8394752 | tf_op jit(solution)/shard_map/convert_element_type | solution.py:121
  62.2 24.5 %collective-permute-done.2 = bf16[512,16,128]{2,1,0:T(8,128)(2,1)} collective-permute-done((bf16[512,16,128]{2,1,0:T(8,128)(2,1)}, bf16[512,16,128]{2,1,0:T(8,128)(2,1)}, u32[]{:S(2)}, u32[]{:S(2)}) %collective-permute-start.2) | collective-permute-done | bytes 2097184 | tf_op jit(solution)/shard_map/ppermute | solution.py:183
  87.2 3.9 %collective-permute-done.4 = bf16[512,16,128]{2,1,0:T(8,128)(2,1)S(1)} collective-permute-done((bf16[512,16,128]{2,1,0:T(8,128)(2,1)}, bf16[512,16,128]{2,1,0:T(8,128)(2,1)S(1)}, u32[]{:S(2)}, u32[]{:S(2)}) %collective-permute-start.4) | collective-permute-done | bytes 2097184 | tf_op jit(solution)/shard_map/ppermute | solution.py:187
  91.1 6.4 %fusion.21 = bf16[16,2,2,512,128]{4,0,3,2,1:T(8,128)(2,1)} fusion(bf16[512,16,128]{2,1,0:T(8,128)(2,1)S(1)} %collective-permute-done.4, bf16[512,16,128]{2,1,0:T(8,128)(2,1)} %collective-permute-done.3, bf16[512,16,128]{2,1,0:T(8,128)(2,1)} %collective-permute-done.2, bf16[512,16,128]{2,1,0:T(8,128)(2,1)} %slice_dynamic-update-slice_fusion.2, ...), kind=kOutput, calls=%fused_computation.31 | convolution fusion | flops 574619648 | bytes 16785408 | tf_op jit(solution)/shard_map/fkrt,ptc->fkrpc/dot_general | solution.py:192
  97.5 12.7 %fusion.22 = bf16[16,512,2,128]{1,3,2,0:T(8,128)(2,1)} fusion(bf16[16,2,512,512]{3,2,1,0:T(8,128)(2,1)} %param.7, bf16[16,2,2,512,128]{4,0,3,2,1:T(8,128)(2,1)} %fusion.21), kind=kOutput, calls=%fused_computation.32 | convolution fusion | flops 4297064448 | bytes 29360128 | tf_op jit(solution)/shard_map/fksp,fkrpc->fsrc/dot_general | solution.py:197
  110.2 8.1 %copy.13 = bf16[16,512,2,128]{3,0,2,1:T(8,128)(2,1)} copy(bf16[16,512,2,128]{1,3,2,0:T(8,128)(2,1)} %fusion.22) | data formatting | bytes 8388608 | tf_op jit(solution)/shard_map/convert_element_type | solution.py:198
  118.4 1.8 collective-permute-start.5
  120.2 46.2 %collective-permute-done.5 = bf16[512,16,128]{2,1,0:T(8,128)(2,1)S(1)} collective-permute-done((bf16[512,16,128]{2,1,0:T(8,128)(2,1)}, bf16[512,16,128]{2,1,0:T(8,128)(2,1)S(1)}, u32[]{:S(2)}, u32[]{:S(2)}) %collective-permute-start.5) | collective-permute-done | bytes 2097184 | tf_op jit(solution)/shard_map/ppermute | solution.py:183
  166.4 4.2 %collective-permute-done.7 = bf16[512,16,128]{2,1,0:T(8,128)(2,1)S(1)} collective-permute-done((bf16[512,16,128]{2,1,0:T(8,128)(2,1)S(1)}, bf16[512,16,128]{2,1,0:T(8,128)(2,1)S(1)}, u32[]{:S(2)}, u32[]{:S(2)}) %collective-permute-start.7) | collective-permute-done | bytes 2097184 | tf_op jit(solution)/shard_map/ppermute | solution.py:187
  170.5 5.8 %fusion.20 = bf16[16,2,2,512,128]{4,0,3,2,1:T(8,128)(2,1)} fusion(bf16[512,16,128]{2,1,0:T(8,128)(2,1)S(1)} %collective-permute-done.7, bf16[512,16,128]{2,1,0:T(8,128)(2,1)S(1)} %collective-permute-done.6, bf16[512,16,128]{2,1,0:T(8,128)(2,1)S(1)} %collective-permute-done.5, bf16[512,16,128]{2,1,0:T(8,128)(2,1)} %slice_dynamic-update-slice_fusion, ...), kind=kOutput, calls=%fused_computation.30 | convolution fusion | flops 574619648 | bytes 16785408 | tf_op jit(solution)/shard_map/fkrt,ptc->fkrpc/dot_general | solution.py:192
  176.3 12.8 %fusion.23 = bf16[16,512,2,128]{1,3,2,0:T(8,128)(2,1)} fusion(bf16[16,2,512,512]{3,2,1,0:T(8,128)(2,1)} %param.7, bf16[16,2,2,512,128]{4,0,3,2,1:T(8,128)(2,1)} %fusion.20), kind=kOutput, calls=%fused_computation.33 | convolution fusion | flops 4297064448 | bytes 29360128 | tf_op jit(solution)/shard_map/fksp,fkrpc->fsrc/dot_general | solution.py:197
  189.1 8.0 %copy.15 = bf16[16,512,2,128]{3,0,2,1:T(8,128)(2,1)} copy(bf16[16,512,2,128]{1,3,2,0:T(8,128)(2,1)} %fusion.23) | data formatting | bytes 8388608 | tf_op jit(solution)/shard_map/convert_element_type | solution.py:198
  197.2 4.8 %pad_maximum_fusion = bf16[512,16,256]{2,1,0:T(8,128)(2,1)} fusion(bf16[512,16,128]{2,1,0:T(8,128)(2,1)} %slice_dynamic-update-slice_fusion, bf16[512,16,128]{2,1,0:T(8,128)(2,1)} %slice_dynamic-update-slice_fusion.2), kind=kLoop, calls=%fused_computation.50 | loop fusion | flops 8388608 | bytes 8388608 | tf_op jit(solution)/shard_map/concatenate | solution.py:233
  201.9 5.8 %reduce-scatter.3.cloned.1.call-done = bf16[16,64,2,128]{3,0,2,1:T(8,128)(2,1)} async-done(((bf16[16,512,2,128]{3,0,2,1:T(8,128)(2,1)}), bf16[16,64,2,128]{3,0,2,1:T(8,128)(2,1)}) %reduce-scatter.3.cloned.1.call-update) | async-done | bytes 524304 | tf_op jit(solution)/shard_map/reduce_scatter | solution.py:198
  207.8 91.7 %reduce-scatter.5.cloned.1.call-done = bf16[16,64,2,128]{3,0,2,1:T(8,128)(2,1)} async-done(((bf16[16,512,2,128]{3,0,2,1:T(8,128)(2,1)}), bf16[16,64,2,128]{3,0,2,1:T(8,128)(2,1)}) %reduce-scatter.5.cloned.1.call-update) | async-done | bytes 524304 | tf_op jit(solution)/shard_map/reduce_scatter | solution.py:198
  299.5 1.4 maximum_convert_fusion
  300.9 3.2 %copy.16 = f32[64,16,2,256]{3,2,1,0:T(2,128)} copy(f32[64,16,2,256]{3,1,2,0:T(8,128)S(1)} %maximum_convert_fusion) | data formatting | bytes 4194304
  (67 shorter events, 6.8 us)
Async XLA Ops:
  7.2 200.6 %reduce-scatter.3.cloned.1.call-start = ((), (), s32[]{:S(2)}) async-start(), calls=%async_computation.2 | async-start | bytes 4718592 | tf_op jit(solution)/shard_map/reduce_scatter | solution.py:198
  9.7 25.8 %collective-permute-start.1 = (f32[20490]{0:T(1024)S(1)}, f32[20490]{0:T(1024)S(1)}, u32[]{:S(2)}, u32[]{:S(2)}) collective-permute-start(f32[20490]{0:T(1024)S(1)} %concatenate.43), channel_id=1, source_target_pairs={{4,0},{8,4},{12,8},{16,12},{20,16},{24,20},{28,24},{5,1},{9,5},{13... | collective-permute-start | bytes 245888 | tf_op jit(solution)/shard_map/ppermute | solution.py:19
  11.8 23.7 %collective-permute-start = (f32[20491]{0:T(1024)S(1)}, f32[20491]{0:T(1024)S(1)}, u32[]{:S(2)}, u32[]{:S(2)}) collective-permute-start(f32[20491]{0:T(1024)S(1)} %concatenate.41), channel_id=1, source_target_pairs={{0,4},{4,8},{8,12},{12,16},{16,20},{20,24},{24,28},{1,5},{5,9},{9,... | collective-permute-start | bytes 245900 | tf_op jit(solution)/shard_map/ppermute | solution.py:14
  18.9 12.8 %copy-start = (bf16[512,16,256]{2,1,0:T(8,128)(2,1)S(1)}, bf16[512,16,256]{2,1,0:T(8,128)(2,1)}, u32[]{:S(2)}) copy-start(bf16[512,16,256]{2,1,0:T(8,128)(2,1)} %param.4) | copy-start | bytes 12582916
  31.8 3.8 %copy-start.1 = (f32[512]{0:T(512)S(1)}, f32[512]{0:T(512)}, u32[]{:S(2)}) copy-start(f32[512]{0:T(512)} %param.5) | copy-start | bytes 6148
  31.8 4.0 %copy-start.2 = (f32[512]{0:T(512)S(1)}, f32[512]{0:T(512)}, u32[]{:S(2)}) copy-start(f32[512]{0:T(512)} %param.6) | copy-start | bytes 6148
  39.3 47.4 %collective-permute-start.2 = (bf16[512,16,128]{2,1,0:T(8,128)(2,1)}, bf16[512,16,128]{2,1,0:T(8,128)(2,1)}, u32[]{:S(2)}, u32[]{:S(2)}) collective-permute-start(bf16[512,16,128]{2,1,0:T(8,128)(2,1)} %slice_dynamic-update-slice_fusion.2), channel_id=1, source_target_pairs={{0,2},{2,0},{1,3},{3,1},{4,6},{6,4},{5,7},{7,5},{8,10},{10,8},{9,1... | collective-permute-start | bytes 6291464 | tf_op jit(solution)/shard_map/ppermute | solution.py:183
  41.3 45.8 %collective-permute-start.3 = (bf16[512,16,128]{2,1,0:T(8,128)(2,1)}, bf16[512,16,128]{2,1,0:T(8,128)(2,1)}, u32[]{:S(2)}, u32[]{:S(2)}) collective-permute-start(bf16[512,16,128]{2,1,0:T(8,128)(2,1)} %slice_dynamic-update-slice_fusion.2), channel_id=1, source_target_pairs={{0,1},{1,0},{2,3},{3,2},{4,5},{5,4},{6,7},{7,6},{8,9},{9,8},{10,11... | collective-permute-start | bytes 6291464 | tf_op jit(solution)/shard_map/ppermute | solution.py:184
  86.8 4.4 %collective-permute-start.4 = (bf16[512,16,128]{2,1,0:T(8,128)(2,1)}, bf16[512,16,128]{2,1,0:T(8,128)(2,1)S(1)}, u32[]{:S(2)}, u32[]{:S(2)}) collective-permute-start(bf16[512,16,128]{2,1,0:T(8,128)(2,1)} %collective-permute-done.2), channel_id=1, source_target_pairs={{0,1},{1,0},{2,3},{3,2},{4,5},{5,4},{6,7},{7,6},{8,9},{9,8},{10,11... | collective-permute-start | bytes 6291464 | tf_op jit(solution)/shard_map/ppermute | solution.py:187
  118.4 181.1 %reduce-scatter.5.cloned.1.call-start = ((), (), s32[]{:S(2)}) async-start(), calls=%async_computation.3 | async-start | bytes 4718592 | tf_op jit(solution)/shard_map/reduce_scatter | solution.py:198
  118.4 47.9 %collective-permute-start.5 = (bf16[512,16,128]{2,1,0:T(8,128)(2,1)}, bf16[512,16,128]{2,1,0:T(8,128)(2,1)S(1)}, u32[]{:S(2)}, u32[]{:S(2)}) collective-permute-start(bf16[512,16,128]{2,1,0:T(8,128)(2,1)} %slice_dynamic-update-slice_fusion), channel_id=1, source_target_pairs={{0,2},{2,0},{1,3},{3,1},{4,6},{6,4},{5,7},{7,5},{8,10},{10,8},{9,1... | collective-permute-start | bytes 6291464 | tf_op jit(solution)/shard_map/ppermute | solution.py:183
  120.2 46.2 %collective-permute-start.6 = (bf16[512,16,128]{2,1,0:T(8,128)(2,1)}, bf16[512,16,128]{2,1,0:T(8,128)(2,1)S(1)}, u32[]{:S(2)}, u32[]{:S(2)}) collective-permute-start(bf16[512,16,128]{2,1,0:T(8,128)(2,1)} %slice_dynamic-update-slice_fusion), channel_id=1, source_target_pairs={{0,1},{1,0},{2,3},{3,2},{4,5},{5,4},{6,7},{7,6},{8,9},{9,8},{10,11... | collective-permute-start | bytes 6291464 | tf_op jit(solution)/shard_map/ppermute | solution.py:184
  166.4 4.2 %collective-permute-start.7 = (bf16[512,16,128]{2,1,0:T(8,128)(2,1)S(1)}, bf16[512,16,128]{2,1,0:T(8,128)(2,1)S(1)}, u32[]{:S(2)}, u32[]{:S(2)}) collective-permute-start(bf16[512,16,128]{2,1,0:T(8,128)(2,1)S(1)} %collective-permute-done.5), channel_id=1, source_target_pairs={{0,1},{1,0},{2,3},{3,2},{4,5},{5,4},{6,7},{7,6},{8,9},{9,8},{10,11... | collective-permute-start | bytes 6291464 | tf_op jit(solution)/shard_map/ppermute | solution.py:187
Sparse Core Ops, SparseCore 0:
  118.5 89.2 reduce-scatter.2
  211.8 87.6 reduce-scatter.4

commit v16 on v15

--- a/solution.py
+++ b/solution.py
@@ -103,13 +103,21 @@
     before, after = halo_rows
     left_src = jnp.concatenate([before, motion[: span - halo]]).astype(jnp.float32)
     right_src = jnp.concatenate([motion[points - span + halo :], after]).astype(jnp.float32)
-    left_k, right_k, diag = coefficients
-    extent = left_k.shape[0]
-    left = smooth(left_src, left_k[:span], right_k[:span], diag[:span], halo)
-    right = smooth(
-        right_src, left_k[extent - span :], right_k[extent - span :], diag[extent - span :], halo
-    )
-    return left.astype(jnp.bfloat16), right.astype(jnp.bfloat16)
+    extent = coefficients[0].shape[0]
+    steps = motion.shape[1]
+    paired = [
+        jnp.concatenate(
+            [
+                jnp.broadcast_to(vector[:span], (span, steps, 1)),
+                jnp.broadcast_to(vector[extent - span :], (span, steps, 1)),
+            ],
+            axis=1,
+        )
+        for vector in coefficients
+    ]
+    both = smooth(jnp.concatenate([left_src, right_src], axis=1), *paired, halo)
+    both = both.astype(jnp.bfloat16)
+    return both[:, :steps], both[:, steps:]
 
 
 def smooth_with_edges(motion, edges, local_coefficients_, halo, banded=False):

time: 312 us -> 312 us (level)
    add x16 -> x12, other arithmetic: 15.5 us -> 15.1 us  [smooth(): state = state + weights[k] * (source - applied) / diag]
    another operation x4 -> x3, other arithmetic: 13.3 us -> 13.2 us
where the time goes in v16:
time: 312 us; the launch traced here: 311 us
  waiting for transfers between devices  176 us (56%)
  other arithmetic  43.2 us (14%)
  matrix products  37.8 us (12%)
  local copies, waits for them, and re-layouts  29 us (9%)
  between operations  14.4 us (5%)
  starting transfers between devices  10.6 us (3%)
    reduce_scatter x2, waiting for transfers between devices, green_product(): lax.psum_scatter(partial.astype(jnp.bfloat16), 'sea', scatter_dimension=1...  97.5 us
    ppermute x2, waiting for transfers between devices, gathered_spectrum(): across = lax.ppermute(prior_part, 'tm', [(0, 2), (2, 0), (1, 3), (3, 1)])  70.7 us
    dot_general x2, matrix products, green_product(): jnp.einsum('fksp,fkrpc->fsrc', green, mixed, preferred_element_type=jnp.f...  25.6 us
    convert_element_type x2, local copies, waits for them, and re-layouts, green_product(): partial.astype(jnp.bfloat16)  16.1 us
    add x12, other arithmetic, smooth(): state = state + weights[k] * (source - applied) / diag  15.1 us
    another operation x3, other arithmetic  13.2 us
    dot_general x2, matrix products, gathered_spectrum(): jnp.einsum('fkrt,ptc->fkrpc', table_high, stacked, preferred_element_type...  12.2 us
    ppermute x2, waiting for transfers between devices, gathered_spectrum(): partner_across = lax.ppermute(across, 'tm', chip_pairs)  8.1 us
  transfers between devices with their start and end apart: 10, of which 6 were waited for; matrix products, arithmetic and copies ran while one was open for 23% of the time, Pallas kernels for 0%

profile of v16, /device:TPU:0, one launch (start us, length us, event | category | flops | bytes accessed | tf_op | source)
XLA Modules:
  0.0 311.2 jit_solution(5881995381922343350)
XLA Ops:
  7.2 0.8 slice_convert_fusion.3
  8.1 0.8 fusion.152
  8.9 0.7 slice.312
  9.7 1.3 collective-permute-start.1
  11.0 0.8 slice.306
  11.8 5.5 %collective-permute-start = (f32[20491]{0:T(1024)S(1)}, f32[20491]{0:T(1024)S(1)}, u32[]{:S(2)}, u32[]{:S(2)}) collective-permute-start(f32[20491]{0:T(1024)S(1)} %concatenate.56), channel_id=1, source_target_pairs={{0,4},{4,8},{8,12},{12,16},{16,20},{20,24},{24,28},{1,5},{5,9},{9,... | collective-permute-start | bytes 245900 | tf_op jit(solution)/shard_map/ppermute | solution.py:14
  17.4 0.8 add_add_fusion
  19.0 12.8 %add_convert_fusion = bf16[502,16,128]{2,1,0:T(8,128)(2,1)} fusion(bf16[512,16,256]{2,1,0:T(8,128)(2,1)} %param.4, f32[502]{0:T(512)S(1)} %bitcast.88, f32[502]{0:T(512)S(1)} %bitcast.89, f32[502]{0:T(512)S(1)} %bitcast.90, f32[502]{0:T(512)S(1)} %bitcast.91, f32[502]{0:T(512)S(1)} %bitcast.92, f32[502]{0:T(512)S(1)} %bitcast.93, f32[502]{0:T(512)S(1)} %bitcast.94, ...), kind=kLoop, calls=%fused_computation.52 | loop fusion | flops 33927168 | bytes 24696392 | tf_op jit(solution)/shard_map/convert.17
  32.2 3.3 %pad.58 = bf16[512,16,128]{2,1,0:T(8,128)(2,1)} pad(bf16[502,16,128]{2,1,0:T(8,128)(2,1)} %add_convert_fusion, bf16[]{:T(256)} %constant.44.clone.1), padding=5_5x0_0x0_0 | pad | bytes 4153346 | tf_op jit(solution)/shard_map/jit(_pad)/pad | solution.py:97
  39.6 2.0 collective-permute-start.2
  41.6 1.5 fusion.24
  43.1 3.4 %fusion.27 = f32[512,16,128]{2,1,0:T(8,128)S(1)} fusion(f32[512,16,128]{2,1,0:T(8,128)S(1)} %fusion.24, bf16[512,16,128]{2,1,0:T(8,128)(2,1)S(1)} %slice.339, f32[512]{0:T(512)S(1)} %get-tuple-element.15, f32[512]{0:T(512)S(1)} %get-tuple-element.46, f32[512]{0:T(512)S(1)} %get-tuple-element.14), kind=kLoop, calls=%fused_computation.37 | loop fusion | flops 10485760 | bytes 10491904 | tf_op jit(solution)/shard_map/add | solution.py:68
  46.5 3.4 %fusion.30 = f32[512,16,128]{2,1,0:T(8,128)S(1)} fusion(f32[512,16,128]{2,1,0:T(8,128)S(1)} %fusion.27, bf16[512,16,128]{2,1,0:T(8,128)(2,1)S(1)} %slice.339, f32[512]{0:T(512)S(1)} %get-tuple-element.15, f32[512]{0:T(512)S(1)} %get-tuple-element.46, f32[512]{0:T(512)S(1)} %get-tuple-element.14), kind=kLoop, calls=%fused_computation.40 | loop fusion | flops 10485760 | bytes 10491904 | tf_op jit(solution)/shard_map/add | solution.py:68
  49.9 3.4 %fusion.33 = f32[512,16,128]{2,1,0:T(8,128)S(1)} fusion(f32[512,16,128]{2,1,0:T(8,128)S(1)} %fusion.30, bf16[512,16,128]{2,1,0:T(8,128)(2,1)S(1)} %slice.339, f32[512]{0:T(512)S(1)} %get-tuple-element.15, f32[512]{0:T(512)S(1)} %get-tuple-element.46, f32[512]{0:T(512)S(1)} %get-tuple-element.14), kind=kLoop, calls=%fused_computation.43 | loop fusion | flops 10485760 | bytes 10491904 | tf_op jit(solution)/shard_map/add | solution.py:68
  53.3 3.4 %fusion.36 = f32[512,16,128]{2,1,0:T(8,128)S(1)} fusion(f32[512,16,128]{2,1,0:T(8,128)S(1)} %fusion.33, bf16[512,16,128]{2,1,0:T(8,128)(2,1)S(1)} %slice.339, f32[512]{0:T(512)S(1)} %get-tuple-element.15, f32[512]{0:T(512)S(1)} %get-tuple-element.46, f32[512]{0:T(512)S(1)} %get-tuple-element.14), kind=kLoop, calls=%fused_computation.46 | loop fusion | flops 10485760 | bytes 10491904 | tf_op jit(solution)/shard_map/add | solution.py:68
  56.7 4.6 %fusion.40 = bf16[512,16,128]{2,1,0:T(8,128)(2,1)} fusion(f32[512,16,128]{2,1,0:T(8,128)S(1)} %fusion.36, bf16[512,16,128]{2,1,0:T(8,128)(2,1)S(1)} %slice.339, f32[512]{0:T(512)S(1)} %get-tuple-element.15, f32[512]{0:T(512)S(1)} %get-tuple-element.46, f32[512]{0:T(512)S(1)} %get-tuple-element.14), kind=kLoop, calls=%fused_computation.51 | loop fusion | flops 11534336 | bytes 8394752 | tf_op jit(solution)/shard_map/convert_element_type | solution.py:129
  62.5 24.5 %collective-permute-done.2 = bf16[512,16,128]{2,1,0:T(8,128)(2,1)} collective-permute-done((bf16[512,16,128]{2,1,0:T(8,128)(2,1)}, bf16[512,16,128]{2,1,0:T(8,128)(2,1)}, u32[]{:S(2)}, u32[]{:S(2)}) %collective-permute-start.2) | collective-permute-done | bytes 2097184 | tf_op jit(solution)/shard_map/ppermute | solution.py:191
  87.4 3.9 %collective-permute-done.4 = bf16[512,16,128]{2,1,0:T(8,128)(2,1)S(1)} collective-permute-done((bf16[512,16,128]{2,1,0:T(8,128)(2,1)}, bf16[512,16,128]{2,1,0:T(8,128)(2,1)S(1)}, u32[]{:S(2)}, u32[]{:S(2)}) %collective-permute-start.4) | collective-permute-done | bytes 2097184 | tf_op jit(solution)/shard_map/ppermute | solution.py:195
  91.4 6.4 %fusion.21 = bf16[16,2,2,512,128]{4,0,3,2,1:T(8,128)(2,1)} fusion(bf16[512,16,128]{2,1,0:T(8,128)(2,1)S(1)} %collective-permute-done.4, bf16[512,16,128]{2,1,0:T(8,128)(2,1)} %collective-permute-done.3, bf16[512,16,128]{2,1,0:T(8,128)(2,1)} %collective-permute-done.2, bf16[512,16,128]{2,1,0:T(8,128)(2,1)} %slice_dynamic-update-slice_fusion.2, ...), kind=kOutput, calls=%fused_computation.31 | convolution fusion | flops 574619648 | bytes 16785408 | tf_op jit(solution)/shard_map/fkrt,ptc->fkrpc/dot_general | solution.py:200
  97.8 12.7 %fusion.22 = bf16[16,512,2,128]{1,3,2,0:T(8,128)(2,1)} fusion(bf16[16,2,512,512]{3,2,1,0:T(8,128)(2,1)} %param.7, bf16[16,2,2,512,128]{4,0,3,2,1:T(8,128)(2,1)} %fusion.21), kind=kOutput, calls=%fused_computation.32 | convolution fusion | flops 4297064448 | bytes 29360128 | tf_op jit(solution)/shard_map/fksp,fkrpc->fsrc/dot_general | solution.py:205
  110.5 8.1 %copy.13 = bf16[16,512,2,128]{3,0,2,1:T(8,128)(2,1)} copy(bf16[16,512,2,128]{1,3,2,0:T(8,128)(2,1)} %fusion.22) | data formatting | bytes 8388608 | tf_op jit(solution)/shard_map/convert_element_type | solution.py:206
  118.7 1.8 collective-permute-start.5
  120.5 46.2 %collective-permute-done.5 = bf16[512,16,128]{2,1,0:T(8,128)(2,1)S(1)} collective-permute-done((bf16[512,16,128]{2,1,0:T(8,128)(2,1)}, bf16[512,16,128]{2,1,0:T(8,128)(2,1)S(1)}, u32[]{:S(2)}, u32[]{:S(2)}) %collective-permute-start.5) | collective-permute-done | bytes 2097184 | tf_op jit(solution)/shard_map/ppermute | solution.py:191
  166.7 4.2 %collective-permute-done.7 = bf16[512,16,128]{2,1,0:T(8,128)(2,1)S(1)} collective-permute-done((bf16[512,16,128]{2,1,0:T(8,128)(2,1)S(1)}, bf16[512,16,128]{2,1,0:T(8,128)(2,1)S(1)}, u32[]{:S(2)}, u32[]{:S(2)}) %collective-permute-start.7) | collective-permute-done | bytes 2097184 | tf_op jit(solution)/shard_map/ppermute | solution.py:195
  170.8 5.8 %fusion.20 = bf16[16,2,2,512,128]{4,0,3,2,1:T(8,128)(2,1)} fusion(bf16[512,16,128]{2,1,0:T(8,128)(2,1)S(1)} %collective-permute-done.7, bf16[512,16,128]{2,1,0:T(8,128)(2,1)S(1)} %collective-permute-done.6, bf16[512,16,128]{2,1,0:T(8,128)(2,1)S(1)} %collective-permute-done.5, bf16[512,16,128]{2,1,0:T(8,128)(2,1)} %slice_dynamic-update-slice_fusion, ...), kind=kOutput, calls=%fused_computation.30 | convolution fusion | flops 574619648 | bytes 16785408 | tf_op jit(solution)/shard_map/fkrt,ptc->fkrpc/dot_general | solution.py:200
  176.6 12.8 %fusion.23 = bf16[16,512,2,128]{1,3,2,0:T(8,128)(2,1)} fusion(bf16[16,2,512,512]{3,2,1,0:T(8,128)(2,1)} %param.7, bf16[16,2,2,512,128]{4,0,3,2,1:T(8,128)(2,1)} %fusion.20), kind=kOutput, calls=%fused_computation.33 | convolution fusion | flops 4297064448 | bytes 29360128 | tf_op jit(solution)/shard_map/fksp,fkrpc->fsrc/dot_general | solution.py:205
  189.5 8.0 %copy.15 = bf16[16,512,2,128]{3,0,2,1:T(8,128)(2,1)} copy(bf16[16,512,2,128]{1,3,2,0:T(8,128)(2,1)} %fusion.23) | data formatting | bytes 8388608 | tf_op jit(solution)/shard_map/convert_element_type | solution.py:206
  197.5 4.8 %pad_maximum_fusion = bf16[512,16,256]{2,1,0:T(8,128)(2,1)} fusion(bf16[512,16,128]{2,1,0:T(8,128)(2,1)} %slice_dynamic-update-slice_fusion, bf16[512,16,128]{2,1,0:T(8,128)(2,1)} %slice_dynamic-update-slice_fusion.2), kind=kLoop, calls=%fused_computation.50 | loop fusion | flops 8388608 | bytes 8388608 | tf_op jit(solution)/shard_map/concatenate | solution.py:241
  202.3 5.8 %reduce-scatter.3.cloned.1.call-done = bf16[16,64,2,128]{3,0,2,1:T(8,128)(2,1)} async-done(((bf16[16,512,2,128]{3,0,2,1:T(8,128)(2,1)}), bf16[16,64,2,128]{3,0,2,1:T(8,128)(2,1)}) %reduce-scatter.3.cloned.1.call-update) | async-done | bytes 524304 | tf_op jit(solution)/shard_map/reduce_scatter | solution.py:206
  208.1 91.7 %reduce-scatter.5.cloned.1.call-done = bf16[16,64,2,128]{3,0,2,1:T(8,128)(2,1)} async-done(((bf16[16,512,2,128]{3,0,2,1:T(8,128)(2,1)}), bf16[16,64,2,128]{3,0,2,1:T(8,128)(2,1)}) %reduce-scatter.5.cloned.1.call-update) | async-done | bytes 524304 | tf_op jit(solution)/shard_map/reduce_scatter | solution.py:206
  299.8 1.4 maximum_convert_fusion
  301.2 3.2 %copy.16 = f32[64,16,2,256]{3,2,1,0:T(2,128)} copy(f32[64,16,2,256]{3,1,2,0:T(8,128)S(1)} %maximum_convert_fusion) | data formatting | bytes 4194304
  (71 shorter events, 7.1 us)
Async XLA Ops:
  7.2 200.9 %reduce-scatter.3.cloned.1.call-start = ((), (), s32[]{:S(2)}) async-start(), calls=%async_computation.2 | async-start | bytes 4718592 | tf_op jit(solution)/shard_map/reduce_scatter | solution.py:206
  9.7 25.8 %collective-permute-start.1 = (f32[20490]{0:T(1024)S(1)}, f32[20490]{0:T(1024)S(1)}, u32[]{:S(2)}, u32[]{:S(2)}) collective-permute-start(f32[20490]{0:T(1024)S(1)} %concatenate.58), channel_id=1, source_target_pairs={{4,0},{8,4},{12,8},{16,12},{20,16},{24,20},{28,24},{5,1},{9,5},{13... | collective-permute-start | bytes 245888 | tf_op jit(solution)/shard_map/ppermute | solution.py:19
  11.8 23.8 %collective-permute-start = (f32[20491]{0:T(1024)S(1)}, f32[20491]{0:T(1024)S(1)}, u32[]{:S(2)}, u32[]{:S(2)}) collective-permute-start(f32[20491]{0:T(1024)S(1)} %concatenate.56), channel_id=1, source_target_pairs={{0,4},{4,8},{8,12},{12,16},{16,20},{20,24},{24,28},{1,5},{5,9},{9,... | collective-permute-start | bytes 245900 | tf_op jit(solution)/shard_map/ppermute | solution.py:14
  18.9 12.8 %copy-start = (bf16[512,16,256]{2,1,0:T(8,128)(2,1)S(1)}, bf16[512,16,256]{2,1,0:T(8,128)(2,1)}, u32[]{:S(2)}) copy-start(bf16[512,16,256]{2,1,0:T(8,128)(2,1)} %param.4) | copy-start | bytes 12582916
  31.8 3.8 %copy-start.1 = (f32[512]{0:T(512)S(1)}, f32[512]{0:T(512)}, u32[]{:S(2)}) copy-start(f32[512]{0:T(512)} %param.5) | copy-start | bytes 6148
  31.8 4.0 %copy-start.2 = (f32[512]{0:T(512)S(1)}, f32[512]{0:T(512)}, u32[]{:S(2)}) copy-start(f32[512]{0:T(512)} %param.6) | copy-start | bytes 6148
  39.6 47.4 %collective-permute-start.2 = (bf16[512,16,128]{2,1,0:T(8,128)(2,1)}, bf16[512,16,128]{2,1,0:T(8,128)(2,1)}, u32[]{:S(2)}, u32[]{:S(2)}) collective-permute-start(bf16[512,16,128]{2,1,0:T(8,128)(2,1)} %slice_dynamic-update-slice_fusion.2), channel_id=1, source_target_pairs={{0,2},{2,0},{1,3},{3,1},{4,6},{6,4},{5,7},{7,5},{8,10},{10,8},{9,1... | collective-permute-start | bytes 6291464 | tf_op jit(solution)/shard_map/ppermute | solution.py:191
  41.6 45.8 %collective-permute-start.3 = (bf16[512,16,128]{2,1,0:T(8,128)(2,1)}, bf16[512,16,128]{2,1,0:T(8,128)(2,1)}, u32[]{:S(2)}, u32[]{:S(2)}) collective-permute-start(bf16[512,16,128]{2,1,0:T(8,128)(2,1)} %slice_dynamic-update-slice_fusion.2), channel_id=1, source_target_pairs={{0,1},{1,0},{2,3},{3,2},{4,5},{5,4},{6,7},{7,6},{8,9},{9,8},{10,11... | collective-permute-start | bytes 6291464 | tf_op jit(solution)/shard_map/ppermute | solution.py:192
  87.0 4.4 %collective-permute-start.4 = (bf16[512,16,128]{2,1,0:T(8,128)(2,1)}, bf16[512,16,128]{2,1,0:T(8,128)(2,1)S(1)}, u32[]{:S(2)}, u32[]{:S(2)}) collective-permute-start(bf16[512,16,128]{2,1,0:T(8,128)(2,1)} %collective-permute-done.2), channel_id=1, source_target_pairs={{0,1},{1,0},{2,3},{3,2},{4,5},{5,4},{6,7},{7,6},{8,9},{9,8},{10,11... | collective-permute-start | bytes 6291464 | tf_op jit(solution)/shard_map/ppermute | solution.py:195
  118.7 181.1 %reduce-scatter.5.cloned.1.call-start = ((), (), s32[]{:S(2)}) async-start(), calls=%async_computation.3 | async-start | bytes 4718592 | tf_op jit(solution)/shard_map/reduce_scatter | solution.py:206
  118.7 47.9 %collective-permute-start.5 = (bf16[512,16,128]{2,1,0:T(8,128)(2,1)}, bf16[512,16,128]{2,1,0:T(8,128)(2,1)S(1)}, u32[]{:S(2)}, u32[]{:S(2)}) collective-permute-start(bf16[512,16,128]{2,1,0:T(8,128)(2,1)} %slice_dynamic-update-slice_fusion), channel_id=1, source_target_pairs={{0,2},{2,0},{1,3},{3,1},{4,6},{6,4},{5,7},{7,5},{8,10},{10,8},{9,1... | collective-permute-start | bytes 6291464 | tf_op jit(solution)/shard_map/ppermute | solution.py:191
  120.5 46.2 %collective-permute-start.6 = (bf16[512,16,128]{2,1,0:T(8,128)(2,1)}, bf16[512,16,128]{2,1,0:T(8,128)(2,1)S(1)}, u32[]{:S(2)}, u32[]{:S(2)}) collective-permute-start(bf16[512,16,128]{2,1,0:T(8,128)(2,1)} %slice_dynamic-update-slice_fusion), channel_id=1, source_target_pairs={{0,1},{1,0},{2,3},{3,2},{4,5},{5,4},{6,7},{7,6},{8,9},{9,8},{10,11... | collective-permute-start | bytes 6291464 | tf_op jit(solution)/shard_map/ppermute | solution.py:192
  166.7 4.2 %collective-permute-start.7 = (bf16[512,16,128]{2,1,0:T(8,128)(2,1)S(1)}, bf16[512,16,128]{2,1,0:T(8,128)(2,1)S(1)}, u32[]{:S(2)}, u32[]{:S(2)}) collective-permute-start(bf16[512,16,128]{2,1,0:T(8,128)(2,1)S(1)} %collective-permute-done.5), channel_id=1, source_target_pairs={{0,1},{1,0},{2,3},{3,2},{4,5},{5,4},{6,7},{7,6},{8,9},{9,8},{10,11... | collective-permute-start | bytes 6291464 | tf_op jit(solution)/shard_map/ppermute | solution.py:195
Sparse Core Ops, SparseCore 0:
  118.8 89.2 reduce-scatter.2
  212.1 87.6 reduce-scatter.4
